TPU v7x, 32 devices: a whole 2x2x4 slice. The times are simulated.
32 devices in a mesh: dp: 2 (over y), expert: 16 (over z, x, core).
Axes of the slice: x: 2, y: 2, z: 4, core: 2. Of those that a mesh axis runs over, the one named last changes fastest.
Arguments:
- attention: bfloat16 [16, 2, 16, 1024], P('expert', 'dp'), may hold values from -6 to 6
- residual: bfloat16 [16, 2, 16, 2048], P('expert', 'dp')
- out_proj: bfloat16 [1024, 2048], P(None, 'dp'), may hold values from -0.1875 to 0.1875
- gain_in: float32 [2048], replicated, may hold values from 0.5 to 1.5
- router: bfloat16 [2048, 16], P(None, 'dp')
- expert_ids: int32 [16, 2, 16, 6], P('expert'), may hold values from 0 to 15, all different within a row; in each aligned block of 16 rows (0 to 15, 16 to 31, ..., all dimensions but the last counted through in order) at most 12 rows name the same one
- live_rows: int32 [2, 16], P(None, 'expert'), may hold values from 1 to 16, 224 in all within a row
- expert_gate: bfloat16 [16, 1408, 2048], P('expert', 'dp'), may hold values from -0.25 to 0.25
- expert_up: bfloat16 [16, 1408, 2048], P('expert', 'dp'), may hold values from -0.25 to 0.25
- expert_down: bfloat16 [16, 1408, 2048], P('expert', None, 'dp'), may hold values from -0.15625 to 0.15625
- shared_gate: bfloat16 [1408, 2048], P('dp'), may hold values from -0.125 to 0.125
- shared_up: bfloat16 [1408, 2048], P('dp'), may hold values from -0.125 to 0.125
- shared_down: bfloat16 [1408, 2048], P(None, 'dp'), may hold values from -0.15625 to 0.15625
- gain_out: float32 [2048], replicated, may hold values from 0.5 to 1.5
Outputs:
- stream: bfloat16 [16, 2, 16, 2048], P('expert', 'dp')
- normed: bfloat16 [16, 2, 16, 2048], P('expert', 'dp')
Inputs may be any that keep to these rules, and one draw needn't show every extreme that they name: `expert_ids`: each row names 6 different experts; the 16 rows of one block [o, g] name one expert at most 12 times, a bound that some block reaches. The live rows of a device are its first live_rows[g, o]; the 16 counts of each g sum to 224, and one of them is 16.
All inputs are finite; a program needn't handle non-finite values.
Results may differ from a plain program's by a relative error of at most 0.0095.
Values may be sent and summed in bfloat16 or wider, within the bound.
No kernel may reach another device: no remote copies, remote signals or barrier semaphores. Data moves between devices by JAX's collectives and lax.ppermute only.
A program may use at most 128 MiB of HBM per device.

v0:
```python
import jax
import jax.numpy as jnp
from jax import lax
from jax.sharding import PartitionSpec as P


def rms_scale(features, scale_gain):
    return (
        features
        * lax.rsqrt(jnp.mean(features * features, axis=-1, keepdims=True) + 1e-06)
        * scale_gain
    )


def by_rows(left, weight_rows):
    return lax.dot_general(
        left, weight_rows, (((1,), (1,)), ((), ())), preferred_element_type=jnp.float32
    )


def fill_slots(features, targets, slot_total, top_count):
    entries = jnp.arange(targets.shape[0], dtype=jnp.int32)
    source = jnp.full((slot_total,), -1, jnp.int32).at[targets].set(entries, mode="drop")
    chosen = jnp.take(features, jnp.maximum(source, 0) // top_count, axis=0)
    return jnp.where((source >= 0)[:, None], chosen, jnp.zeros_like(chosen))


def shards(
    attention,
    residual,
    out_proj,
    gain_in,
    router,
    expert_ids,
    live_rows,
    expert_gate,
    expert_up,
    expert_down,
    shared_gate,
    shared_up,
    shared_down,
    gain_out,
):
    groups = lax.axis_size("dp")
    experts = lax.axis_size("expert")
    row_count = attention.shape[2]
    feature_width = residual.shape[3]
    top_count = expert_ids.shape[3]
    capacity = max(2, (2 * row_count * top_count + experts - 1) // experts)
    gate_local = expert_gate[0]
    up_local = expert_up[0]
    down_local = expert_down[0]
    column_width = down_local.shape[1]
    pieces = lax.all_gather(attention, "dp", axis=1, tiled=True)
    flattened = pieces.reshape(-1, pieces.shape[-1])
    product = jnp.dot(flattened, out_proj, preferred_element_type=jnp.float32).astype(jnp.bfloat16)
    columns = product.reshape(pieces.shape[:-1] + (out_proj.shape[1],))
    projected = lax.all_to_all(columns, "dp", split_axis=1, concat_axis=3, tiled=True)[0, 0]
    stream_in = residual[0, 0].astype(jnp.float32) + projected.astype(jnp.float32)
    normal_rows = rms_scale(stream_in, gain_in).astype(jnp.bfloat16)
    column = lax.all_gather(normal_rows[None], "dp", axis=0, tiled=True).reshape(
        groups * row_count, feature_width
    )
    logit_part = jnp.dot(column, router, preferred_element_type=jnp.float32)
    logits = lax.all_gather(logit_part, "dp", axis=1, tiled=True)
    flat_experts = expert_ids[0].reshape(groups * row_count, top_count)
    picked = jnp.take_along_axis(logits, flat_experts, axis=1)
    probabilities = jax.nn.softmax(picked, axis=1)
    row_live = (jnp.arange(row_count, dtype=jnp.int32)[None, :] < live_rows[:, 0][:, None]).reshape(
        groups * row_count
    )
    slot_live = jnp.broadcast_to(row_live[:, None], (groups * row_count, top_count))
    weights = probabilities.astype(jnp.bfloat16) * slot_live.astype(jnp.bfloat16)
    block_experts = flat_experts.reshape(groups, row_count * top_count)
    block_live = slot_live.reshape(groups, row_count * top_count)
    onehot = (
        (block_experts[:, :, None] == jnp.arange(experts, dtype=jnp.int32)) & block_live[:, :, None]
    ).astype(jnp.int32)
    before = jnp.cumsum(onehot, axis=1) - onehot
    position = jnp.sum(before * onehot, axis=2)
    slot_total = experts * groups * capacity
    offsets = jnp.arange(groups, dtype=jnp.int32)[:, None] * capacity
    target = jnp.where(
        block_live, block_experts * (groups * capacity) + offsets + position, slot_total
    ).reshape(-1)
    outgoing = fill_slots(column, target, slot_total, top_count).reshape(
        experts, groups * capacity, feature_width
    )
    slot_rows = lax.all_to_all(outgoing, "expert", split_axis=0, concat_axis=0, tiled=True)
    flattened = slot_rows.reshape(-1, slot_rows.shape[-1])
    gate_value = by_rows(flattened, gate_local)
    up_value = by_rows(flattened, up_local)
    hidden = (jax.nn.silu(gate_value) * up_value).astype(jnp.bfloat16)
    routed_hidden = hidden.reshape(slot_rows.shape[:-1] + (gate_local.shape[0],))
    shared_gate_value = by_rows(column, shared_gate)
    shared_up_value = by_rows(column, shared_up)
    shared_hidden = (jax.nn.silu(shared_gate_value) * shared_up_value).astype(jnp.bfloat16)[None]
    routed_piece = lax.all_gather(routed_hidden, "dp", axis=2, tiled=True)
    shared_piece = lax.all_gather(shared_hidden, "dp", axis=2, tiled=True)
    count = routed_piece.shape[2]
    routed_total = jnp.dot(
        routed_piece.reshape(-1, count), down_local, preferred_element_type=jnp.float32
    )
    shared_total = jnp.dot(
        shared_piece.reshape(-1, shared_piece.shape[2]),
        shared_down,
        preferred_element_type=jnp.float32,
    )
    routed_total, shared = (routed_total, shared_total)
    expert_out = routed_total.astype(jnp.bfloat16).reshape(experts, groups * capacity, column_width)
    returned = lax.all_to_all(
        expert_out, "expert", split_axis=0, concat_axis=0, tiled=True
    ).reshape(slot_total, column_width)
    gathered = jnp.take(returned, jnp.minimum(target, slot_total - 1), axis=0).reshape(
        groups * row_count, top_count, column_width
    )
    routed = jnp.einsum("nk,nkd->nd", weights, gathered, preferred_element_type=jnp.float32)
    combined = jnp.where(row_live[:, None], routed + shared, 0.0).reshape(
        groups, row_count, column_width
    )
    summed = lax.all_to_all(combined, "dp", split_axis=0, concat_axis=2, tiled=True)[0]
    stream_sum = stream_in + summed
    stream = stream_sum.astype(jnp.bfloat16)[None, None]
    normed = rms_scale(stream_sum, gain_out).astype(jnp.bfloat16)[None, None]
    return (stream, normed)


def solution(mesh):
    placed = (
        P("expert", "dp", None, None),
        P("expert", "dp", None, None),
        P(None, "dp"),
        P(),
        P(None, "dp"),
        P("expert", None, None, None),
        P(None, "expert"),
        P("expert", "dp", None),
        P("expert", "dp", None),
        P("expert", None, "dp"),
        P("dp", None),
        P("dp", None),
        P(None, "dp"),
        P(),
    )
    return jax.shard_map(
        shards,
        mesh=mesh,
        in_specs=placed,
        out_specs=(P("expert", "dp", None, None), P("expert", "dp", None, None)),
        check_vma=False,
    )
```

profile of v0, /device:TPU:0, one launch (start us, length us, event | category | flops | bytes accessed | tf_op | source)
XLA Modules:
  0.0 224.4 jit_solution(8419740053843985817)
XLA Ops:
  7.2 5.9 %all_gather.15 = bf16[1,2,16,1024]{3,2,0,1:T(8,128)(2,1)S(1)} all-gather(bf16[1,1,16,1024]{3,2,0,1:T(8,128)(2,1)} %bitcast.143), channel_id=1, replica_groups=mesh['dp'=2,'expert'=16] {'dp'}, dimensions={1}, use_global_device_ids=true | all-gather | bytes 98304 | tf_op jit(solution)/shard_map/all_gather | solution.py:54
  13.1 2.7 %convolution_convert_fusion = bf16[32,1024]{1,0:T(8,128)(2,1)} fusion(bf16[32,1024]{1,0:T(8,128)(2,1)S(1)} %bitcast.142, bf16[1024,1024]{1,0:T(8,128)(2,1)} %param.16), kind=kOutput, calls=%fused_computation.17 | convolution fusion | flops 67141632 | bytes 2228224 | tf_op jit(solution)/shard_map/dot_general | solution.py:56
  15.8 3.3 %all-to-all-start = ((bf16[1,2,16,1024]{3,2,0,1:T(8,128)(2,1)}), bf16[1,2,16,1024]{3,2,0,1:T(8,128)(2,1)S(1)}, u32[]{:S(2)}, u32[]{:S(2)}) async-start(bf16[1,2,16,1024]{3,2,0,1:T(8,128)(2,1)} %bitcast.3), calls=%async_computation | async-start | bytes 131072 | tf_op jit(solution)/shard_map/all_to_all | solution.py:58
  23.9 4.9 %all_gather.16 = bf16[2,16,2048]{2,1,0:T(8,128)(2,1)S(1)} all-gather(bf16[1,16,2048]{2,1,0:T(8,128)(2,1)S(1)} %fusion.28), channel_id=1, replica_groups=mesh['dp'=2,'expert'=16] {'dp'}, dimensions={0}, use_global_device_ids=true | all-gather | bytes 196608 | tf_op jit(solution)/shard_map/all_gather | solution.py:61
  28.9 3.1 %gather_fusion = bf16[384,2048]{1,0:T(8,128)(2,1)} fusion(bf16[32,2048]{1,0:T(8,128)(2,1)S(1)} %bitcast.127, s32[1024]{0:T(1024)S(1)} %pad_clamp_fusion.1), kind=kCustom, calls=%fused_computation | custom fusion | bytes 3147264 | tf_op jit(solution)/shard_map/jit(_take)/gather | solution.py:24
  32.0 1.7 select_select_fusion
  33.7 42.6 %all_to_all.34 = bf16[16,24,2048]{2,1,0:T(8,128)(2,1)S(1)} all-to-all(bf16[16,24,2048]{2,1,0:T(8,128)(2,1)S(1)} %select_select_fusion), channel_id=1, replica_groups=mesh['dp'=2,'expert'=16] {'expert'}, dimensions={0} | all-to-all | bytes 3145728 | tf_op jit(solution)/shard_map/all_to_all | solution.py:89
  76.3 1.7 fusion.4
  78.1 2.5 %fusion.12 = bf16[384,704]{0,1:T(8,128)(2,1)} fusion(bf16[384,2048]{1,0:T(8,128)(2,1)S(1)} %bitcast.137, bf16[1,704,2048]{2,1,0:T(8,128)(2,1)S(1)} %copy-done.14, f32[384,704]{0,1:T(8,128)S(1)} %fusion.4), kind=kOutput, calls=%fused_computation.13 | convolution fusion | flops 1108918272 | bytes 6078464 | tf_op jit(solution)/shard_map/dot_general | solution.py:16
  80.6 2.1 copy.74
  82.7 4.8 %copy.75 = bf16[16,24,704]{1,0,2:T(8,128)(2,1)} copy(bf16[16,24,704]{2,1,0:T(8,128)(2,1)} %bitcast.132) | data formatting | bytes 1081344 | tf_op jit(solution)/shard_map/reshape | solution.py:94
  88.1 74.0 %all-gather.4.cloned.1.call-done = bf16[16,24,1408]{1,0,2:T(8,128)(2,1)} async-done(((bf16[16,24,704]{1,0,2:T(8,128)(2,1)}), bf16[16,24,1408]{1,0,2:T(8,128)(2,1)}) %all-gather.4.cloned.1.call-update) | async-done | bytes 1081360 | tf_op jit(solution)/shard_map/all_gather | solution.py:98
  162.0 7.1 %copy.76 = bf16[16,24,1408]{2,1,0:T(8,128)(2,1)} copy(bf16[16,24,1408]{1,0,2:T(8,128)(2,1)} %all-gather.4.cloned.1.call-done) | data formatting | bytes 2162688 | tf_op jit(solution)/shard_map/all_gather | solution.py:98
  169.1 3.5 %fusion.6 = bf16[384,1024]{1,0:T(8,128)(2,1)} fusion(bf16[384,1408]{1,0:T(8,128)(2,1)} %bitcast.138, bf16[1,1408,1024]{2,1,0:T(8,128)(2,1)S(1)} %copy-done), kind=kOutput, calls=%fused_computation.11 | convolution fusion | flops 1107689472 | bytes 4751360 | tf_op jit(solution)/shard_map/dot_general | solution.py:101
  172.7 5.8 %all-to-all-start.2 = ((bf16[16,24,1024]{2,1,0:T(8,128)(2,1)}), bf16[16,24,1024]{2,1,0:T(8,128)(2,1)}, u32[]{:S(2)}, u32[]{:S(2)}) async-start(bf16[16,24,1024]{2,1,0:T(8,128)(2,1)} %bitcast.139), calls=%async_computation.2 | async-start | bytes 1572864 | tf_op jit(solution)/shard_map/all_to_all | solution.py:111
  179.3 4.3 %all_gather.17 = f32[32,16]{0,1:T(8,128)S(1)} all-gather(f32[32,8]{0,1:T(8,128)S(1)} %fusion.47), channel_id=1, replica_groups=mesh['dp'=2,'expert'=16] {'dp'}, dimensions={1}, use_global_device_ids=true | all-gather | bytes 3072 | tf_op jit(solution)/shard_map/all_gather | solution.py:65
  183.6 1.7 gather_fusion.2
  185.9 2.9 %fusion.48 = f32[32,704]{1,0:T(8,128)S(1)} fusion(bf16[32,2048]{1,0:T(8,128)(2,1)S(1)} %bitcast.129, bf16[704,2048]{1,0:T(8,128)(2,1)} %param.24), kind=kOutput, calls=%fused_computation.85 | convolution fusion | flops 92274688 | bytes 3104768 | tf_op jit(solution)/shard_map/dot_general | solution.py:16
  189.7 4.9 %all-gather.1 = bf16[2,704,32]{1,2,0:T(8,128)(2,1)S(1)} all-gather(bf16[1,704,32]{1,2,0:T(8,128)(2,1)S(1)} %fusion.17), channel_id=2, replica_groups=mesh['dp'=2,'expert'=16] {'dp'}, dimensions={0}, use_global_device_ids=true | all-gather | bytes 135168 | tf_op jit(solution)/shard_map/all_gather | solution.py:99
  195.7 1.6 all-to-all-done.2
  197.2 2.5 %gather_fusion.1 = bf16[192,1024]{1,0:T(8,128)(2,1)S(1)} fusion(bf16[384,1024]{1,0:T(8,128)(2,1)} %bitcast.22, s32[1024]{0:T(1024)S(1)} %pad_clamp_fusion), kind=kCustom, calls=%fused_computation.1 | custom fusion | bytes 787200 | tf_op jit(solution)/shard_map/jit(_take)/gather | solution.py:114
  202.2 3.1 %fusion.15 = f32[32,1024]{1,0:T(8,128)} fusion(bf16[1408,32]{0,1:T(8,128)(2,1)S(1)} %copy-done.6, bf16[1408,1024]{1,0:T(8,128)(2,1)} %param.26, f32[32,1,1024]{2,1,0:T(1,128)S(1)} %fusion.18, pred[32]{0:T(512)(128)(4,1)S(1)} %copy-done.11), kind=kOutput, calls=%fused_computation.15 | convolution fusion | flops 92340224 | bytes 3235872 | tf_op jit(solution)/shard_map/dot_general | solution.py:104
  205.3 3.4 %all-to-all-start.3 = ((f32[2,16,1024]{2,1,0:T(8,128)}), f32[2,16,1024]{2,1,0:T(8,128)S(1)}, u32[]{:S(2)}, u32[]{:S(2)}) async-start(f32[2,16,1024]{2,1,0:T(8,128)} %bitcast.27), calls=%async_computation.3 | async-start | bytes 262144 | tf_op jit(solution)/shard_map/all_to_all | solution.py:121
  209.6 3.5 %all-to-all-done.3 = f32[2,16,1024]{2,1,0:T(8,128)S(1)} async-done(((f32[2,16,1024]{2,1,0:T(8,128)}), f32[2,16,1024]{2,1,0:T(8,128)S(1)}, u32[]{:S(2)}, u32[]{:S(2)}) %all-to-all-start.3) | async-done | bytes 131104 | tf_op jit(solution)/shard_map/all_to_all | solution.py:121
  (98 shorter events, 16.4 us)
Async XLA Ops:
  7.2 162.0 %copy-start = (bf16[1,1408,1024]{2,1,0:T(8,128)(2,1)S(1)}, bf16[1,1408,1024]{2,1,0:T(8,128)(2,1)}, u32[]{:S(2)}) copy-start(bf16[1,1408,1024]{2,1,0:T(8,128)(2,1)} %param.23) | copy-start | bytes 8650756
  7.2 12.0 %copy-start.7 = (s32[1,2,16,6]{2,1,3,0:T(2,128)S(1)}, s32[1,2,16,6]{2,1,3,0:T(2,128)}, u32[]{:S(2)}) copy-start(s32[1,2,16,6]{2,1,3,0:T(2,128)} %param.19) | copy-start | bytes 2308
  7.2 12.2 %copy-start.15 = (s32[2,1]{0,1:T(1,128)S(1)}, s32[2,1]{0,1:T(1,128)}, u32[]{:S(2)}) copy-start(s32[2,1]{0,1:T(1,128)} %param.20) | copy-start | bytes 28
  13.1 10.4 %copy-start.2 = (bf16[1,1,16,2048]{3,2,1,0:T(8,128)(2,1)S(1)}, bf16[1,1,16,2048]{3,2,1,0:T(8,128)(2,1)}, u32[]{:S(2)}) copy-start(bf16[1,1,16,2048]{3,2,1,0:T(8,128)(2,1)} %param.15) | copy-start | bytes 196612
  13.1 10.8 %copy-start.9 = (f32[2048]{0:T(1024)S(1)}, f32[2048]{0:T(1024)}, u32[]{:S(2)}) copy-start(f32[2048]{0:T(1024)} %param.17) | copy-start | bytes 24580
  15.8 7.4 %all-to-all-start = ((bf16[1,2,16,1024]{3,2,0,1:T(8,128)(2,1)}), bf16[1,2,16,1024]{3,2,0,1:T(8,128)(2,1)S(1)}, u32[]{:S(2)}, u32[]{:S(2)}) async-start(bf16[1,2,16,1024]{3,2,0,1:T(8,128)(2,1)} %bitcast.3), calls=%async_computation | async-start | bytes 131072 | tf_op jit(solution)/shard_map/all_to_all | solution.py:58
  19.1 142.9 %all-gather.4.cloned.1.call-start = ((), (), s32[]{:S(2)}) async-start(), calls=%async_computation.4 | async-start | bytes 8650752 | tf_op jit(solution)/shard_map/all_gather | solution.py:98
  19.5 158.9 %copy-start.10 = (pred[32]{0:T(512)(128)(4,1)}, pred[32]{0:T(512)(128)(4,1)S(1)}, u32[]{:S(2)}) copy-start(pred[32]{0:T(512)(128)(4,1)S(1)} %lt.91) | copy-start | bytes 100
  23.2 0.6 copy-start.4
  33.7 42.6 %copy-start.13 = (bf16[1,704,2048]{2,1,0:T(8,128)(2,1)S(1)}, bf16[1,704,2048]{2,1,0:T(8,128)(2,1)}, u32[]{:S(2)}) copy-start(bf16[1,704,2048]{2,1,0:T(8,128)(2,1)} %param.21) | copy-start | bytes 8650756
  76.2 1.8 copy-start.14
  172.7 6.5 %copy-start.8 = (bf16[2048,8]{0,1:T(8,128)(2,1)S(1)}, bf16[2048,8]{0,1:T(8,128)(2,1)}, u32[]{:S(2)}) copy-start(bf16[2048,8]{0,1:T(8,128)(2,1)} %param.18) | copy-start | bytes 98308
  172.7 24.6 %all-to-all-start.2 = ((bf16[16,24,1024]{2,1,0:T(8,128)(2,1)}), bf16[16,24,1024]{2,1,0:T(8,128)(2,1)}, u32[]{:S(2)}, u32[]{:S(2)}) async-start(bf16[16,24,1024]{2,1,0:T(8,128)(2,1)} %bitcast.139), calls=%async_computation.2 | async-start | bytes 1572864 | tf_op jit(solution)/shard_map/all_to_all | solution.py:111
  185.9 2.9 %copy-start.1 = (bf16[704,2048]{1,0:T(8,128)(2,1)S(1)}, bf16[704,2048]{1,0:T(8,128)(2,1)}, u32[]{:S(2)}) copy-start(bf16[704,2048]{1,0:T(8,128)(2,1)} %param.25) | copy-start | bytes 8650756
  197.2 3.5 %copy-start.12 = (pred[32,6]{1,0:T(8,128)(4,1)S(1)}, pred[32,6]{1,0:T(8,128)(4,1)}, u32[]{:S(2)}) copy-start(pred[32,6]{1,0:T(8,128)(4,1)} %compare_and_fusion) | copy-start | bytes 580
  199.8 2.4 %copy-start.6 = (bf16[1408,32]{0,1:T(8,128)(2,1)S(1)}, bf16[1408,32]{0,1:T(8,128)(2,1)}, u32[]{:S(2)}) copy-start(bf16[1408,32]{0,1:T(8,128)(2,1)} %reshape.455) | copy-start | bytes 270340
  199.8 2.4 %copy-start.11 = (pred[32]{0:T(512)(128)(4,1)S(1)}, pred[32]{0:T(512)(128)(4,1)}, u32[]{:S(2)}) copy-start(pred[32]{0:T(512)(128)(4,1)} %copy-done.10) | copy-start | bytes 100
  202.1 6.5 %copy-start.3 = (bf16[1,1,16,2048]{3,2,1,0:T(8,128)(2,1)S(1)}, bf16[1,1,16,2048]{3,2,1,0:T(8,128)(2,1)}, u32[]{:S(2)}) copy-start(bf16[1,1,16,2048]{3,2,1,0:T(8,128)(2,1)} %param.15) | copy-start | bytes 196612
  202.2 6.8 %copy-start.5 = (bf16[1,2,16,1024]{3,2,0,1:T(8,128)(2,1)S(1)}, bf16[1,2,16,1024]{3,2,0,1:T(8,128)(2,1)}, u32[]{:S(2)}) copy-start(bf16[1,2,16,1024]{3,2,0,1:T(8,128)(2,1)} %copy-done.4) | copy-start | bytes 196612
  205.3 7.8 %all-to-all-start.3 = ((f32[2,16,1024]{2,1,0:T(8,128)}), f32[2,16,1024]{2,1,0:T(8,128)S(1)}, u32[]{:S(2)}, u32[]{:S(2)}) async-start(f32[2,16,1024]{2,1,0:T(8,128)} %bitcast.27), calls=%async_computation.3 | async-start | bytes 262144 | tf_op jit(solution)/shard_map/all_to_all | solution.py:121
Sparse Core Ops, SparseCore 0:
  87.6 74.3 all-gather.3
where the time goes:
time: 225 us; the launch traced here: 224 us
  waiting for transfers between devices  80 us (36%)
  blocking collectives  62.7 us (28%)
  local copies, waits for them, and re-layouts  29.1 us (13%)
  matrix products  18.9 us (8%)
  between operations  14.4 us (6%)
  starting transfers between devices  12.5 us (6%)
  other arithmetic  6.82 us (3%)
    all_gather x1, waiting for transfers between devices, shards(): routed_piece = lax.all_gather(routed_hidden, 'dp', axis=2, tiled=True)  74 us
    all_to_all x1, blocking collectives, shards(): lax.all_to_all(outgoing, 'expert', split_axis=0, concat_axis=0, tiled=True)  42.6 us
    dot_general x4, matrix products, by_rows(): lax.dot_general(left, weight_rows, (((1,), (1,)), ((), ())), preferred_el...  7.98 us
    all_gather x1, local copies, waits for them, and re-layouts, shards(): routed_piece = lax.all_gather(routed_hidden, 'dp', axis=2, tiled=True)  7.09 us
    all_gather x1, blocking collectives, shards(): pieces = lax.all_gather(attention, 'dp', axis=1, tiled=True)  5.88 us
    all_to_all x1, starting transfers between devices, shards(): lax.all_to_all(expert_out, 'expert', split_axis=0, concat_axis=0, tiled=T...  5.79 us
    all_gather x1, blocking collectives, shards(): shared_piece = lax.all_gather(shared_hidden, 'dp', axis=2, tiled=True)  4.95 us
    all_gather x1, blocking collectives, shards(): lax.all_gather(normal_rows[None], 'dp', axis=0, tiled=True)  4.94 us
  transfers between devices with their start and end apart: 4, of which 4 were waited for; matrix products, arithmetic and copies ran while one was open for 5% of the time, Pallas kernels for 0%

commit v1 on v0

--- a/solution.py
+++ b/solution.py
@@ -18,11 +18,26 @@
     )
 
 
-def fill_slots(features, targets, slot_total, top_count):
-    entries = jnp.arange(targets.shape[0], dtype=jnp.int32)
-    source = jnp.full((slot_total,), -1, jnp.int32).at[targets].set(entries, mode="drop")
-    chosen = jnp.take(features, jnp.maximum(source, 0) // top_count, axis=0)
-    return jnp.where((source >= 0)[:, None], chosen, jnp.zeros_like(chosen))
+def gather_axis(x, name, axis):
+    n = lax.axis_size(name)
+    if n == 1:
+        return x
+    me = lax.axis_index(name)
+    pieces = [x]
+    for shift in range(1, n):
+        pieces.append(lax.ppermute(x, name, [(j, (j + shift) % n) for j in range(n)]))
+    if n == 2:
+        first = jnp.where(me == 0, pieces[0], pieces[1])
+        second = jnp.where(me == 0, pieces[1], pieces[0])
+        ordered = [first, second]
+        return jnp.concatenate(ordered, axis=axis)
+    stacked = jnp.stack(pieces, 0)
+    order = (me - jnp.arange(n)) % n
+    ordered = jnp.take(stacked, order, axis=0)
+    ordered = jnp.moveaxis(ordered, 0, axis)
+    shape = list(x.shape)
+    shape[axis] = shape[axis] * n
+    return ordered.reshape(shape)
 
 
 def shards(
@@ -51,25 +66,25 @@
     up_local = expert_up[0]
     down_local = expert_down[0]
     column_width = down_local.shape[1]
-    pieces = lax.all_gather(attention, "dp", axis=1, tiled=True)
+    rows_all = groups * row_count
+
+    pieces = gather_axis(attention, "dp", 1)
     flattened = pieces.reshape(-1, pieces.shape[-1])
     product = jnp.dot(flattened, out_proj, preferred_element_type=jnp.float32).astype(jnp.bfloat16)
     columns = product.reshape(pieces.shape[:-1] + (out_proj.shape[1],))
     projected = lax.all_to_all(columns, "dp", split_axis=1, concat_axis=3, tiled=True)[0, 0]
     stream_in = residual[0, 0].astype(jnp.float32) + projected.astype(jnp.float32)
     normal_rows = rms_scale(stream_in, gain_in).astype(jnp.bfloat16)
-    column = lax.all_gather(normal_rows[None], "dp", axis=0, tiled=True).reshape(
-        groups * row_count, feature_width
-    )
+    column = gather_axis(normal_rows, "dp", 0)
     logit_part = jnp.dot(column, router, preferred_element_type=jnp.float32)
-    logits = lax.all_gather(logit_part, "dp", axis=1, tiled=True)
-    flat_experts = expert_ids[0].reshape(groups * row_count, top_count)
+    logits = gather_axis(logit_part, "dp", 1)
+    flat_experts = expert_ids[0].reshape(rows_all, top_count)
     picked = jnp.take_along_axis(logits, flat_experts, axis=1)
     probabilities = jax.nn.softmax(picked, axis=1)
     row_live = (jnp.arange(row_count, dtype=jnp.int32)[None, :] < live_rows[:, 0][:, None]).reshape(
-        groups * row_count
+        rows_all
     )
-    slot_live = jnp.broadcast_to(row_live[:, None], (groups * row_count, top_count))
+    slot_live = jnp.broadcast_to(row_live[:, None], (rows_all, top_count))
     weights = probabilities.astype(jnp.bfloat16) * slot_live.astype(jnp.bfloat16)
     block_experts = flat_experts.reshape(groups, row_count * top_count)
     block_live = slot_live.reshape(groups, row_count * top_count)
@@ -82,39 +97,32 @@
     offsets = jnp.arange(groups, dtype=jnp.int32)[:, None] * capacity
     target = jnp.where(
         block_live, block_experts * (groups * capacity) + offsets + position, slot_total
-    ).reshape(-1)
-    outgoing = fill_slots(column, target, slot_total, top_count).reshape(
-        experts, groups * capacity, feature_width
-    )
+    ).reshape(rows_all, top_count)
+    slot_hit = target[:, :, None] == jnp.arange(slot_total, dtype=jnp.int32)[None, None, :]
+    fill = jnp.any(slot_hit, axis=1).astype(jnp.bfloat16)
+    outgoing = lax.dot_general(
+        fill, column, (((0,), (0,)), ((), ())), preferred_element_type=jnp.float32
+    ).astype(jnp.bfloat16).reshape(experts, groups * capacity, feature_width)
     slot_rows = lax.all_to_all(outgoing, "expert", split_axis=0, concat_axis=0, tiled=True)
     flattened = slot_rows.reshape(-1, slot_rows.shape[-1])
     gate_value = by_rows(flattened, gate_local)
     up_value = by_rows(flattened, up_local)
     hidden = (jax.nn.silu(gate_value) * up_value).astype(jnp.bfloat16)
-    routed_hidden = hidden.reshape(slot_rows.shape[:-1] + (gate_local.shape[0],))
     shared_gate_value = by_rows(column, shared_gate)
     shared_up_value = by_rows(column, shared_up)
-    shared_hidden = (jax.nn.silu(shared_gate_value) * shared_up_value).astype(jnp.bfloat16)[None]
-    routed_piece = lax.all_gather(routed_hidden, "dp", axis=2, tiled=True)
-    shared_piece = lax.all_gather(shared_hidden, "dp", axis=2, tiled=True)
-    count = routed_piece.shape[2]
-    routed_total = jnp.dot(
-        routed_piece.reshape(-1, count), down_local, preferred_element_type=jnp.float32
-    )
-    shared_total = jnp.dot(
-        shared_piece.reshape(-1, shared_piece.shape[2]),
-        shared_down,
-        preferred_element_type=jnp.float32,
-    )
-    routed_total, shared = (routed_total, shared_total)
+    shared_hidden = (jax.nn.silu(shared_gate_value) * shared_up_value).astype(jnp.bfloat16)
+    routed_piece = gather_axis(hidden, "dp", 1)
+    shared_piece = gather_axis(shared_hidden, "dp", 1)
+    routed_total = jnp.dot(routed_piece, down_local, preferred_element_type=jnp.float32)
+    shared = jnp.dot(shared_piece, shared_down, preferred_element_type=jnp.float32)
     expert_out = routed_total.astype(jnp.bfloat16).reshape(experts, groups * capacity, column_width)
     returned = lax.all_to_all(
         expert_out, "expert", split_axis=0, concat_axis=0, tiled=True
     ).reshape(slot_total, column_width)
-    gathered = jnp.take(returned, jnp.minimum(target, slot_total - 1), axis=0).reshape(
-        groups * row_count, top_count, column_width
-    )
-    routed = jnp.einsum("nk,nkd->nd", weights, gathered, preferred_element_type=jnp.float32)
+    combine = jnp.sum(
+        jnp.where(slot_hit, weights[:, :, None], jnp.zeros((), jnp.bfloat16)), axis=1
+    ).astype(jnp.bfloat16)
+    routed = jnp.dot(combine, returned, preferred_element_type=jnp.float32)
     combined = jnp.where(row_live[:, None], routed + shared, 0.0).reshape(
         groups, row_count, column_width
     )

time: 225 us -> 130 us (0.58)
  waiting for transfers between devices: 80 us -> 35.2 us
  local copies, waits for them, and re-layouts: 29.1 us -> 6.88 us
  blocking collectives: 62.7 us -> 41.9 us
  between operations: 14.4 us -> 0.91 us
  starting transfers between devices: 12.5 us -> 16.5 us
    all_gather x1 -> x0, waiting for transfers between devices: 74 us -> none  [shards(): routed_piece = lax.all_gather(routed_hidden, 'dp', axis=2, tiled=True)]
    all_gather x4 -> x0, blocking collectives: 20.1 us -> none  [the longest x1 5.88 us: shards(): pieces = lax.all_gather(attention, 'dp', axis=1, tiled=True)]
    ppermute x0 -> x5, waiting for transfers between devices: none -> 16.4 us  [gather_axis(): lax.ppermute(x, name, [(j, (j + shift) % n) for j in range(n)])]
    all_to_all x1, waiting for transfers between devices: 1.56 us -> 11.2 us  [shards(): lax.all_to_all(expert_out, 'expert', split_axis=0, concat_axis=0, tiled=T...]
    all_gather x2 -> x0, local copies, waits for them, and re-layouts: 7.19 us -> none  [the longest x1 7.09 us: shards(): routed_piece = lax.all_gather(routed_hidden, 'dp', axis=2, tiled=True)]
    gather x3 -> x0, local copies, waits for them, and re-layouts: 6.6 us -> none  [the longest x2 3.48 us: shards(): jnp.take(returned, jnp.minimum(target, slot_total - 1), axis=0)]
    ppermute x0 -> x5, starting transfers between devices: none -> 5.24 us  [gather_axis(): lax.ppermute(x, name, [(j, (j + shift) % n) for j in range(n)])]
    reshape x2 -> x0, local copies, waits for them, and re-layouts: 4.93 us -> none  [the longest x1 4.81 us: shards(): hidden.reshape(slot_rows.shape[:-1] + (gate_local.shape[0],))]
  transfers between devices with their start and end apart: 4 -> 8, of which waited for: 4 -> 5; matrix products, arithmetic and copies ran while one was open for 5% -> 10% of each run, Pallas kernels for 0% -> 0%
where the time goes in v1:
time: 130 us; the launch traced here: 129 us
  blocking collectives  41.9 us (32%)
  waiting for transfers between devices  35.2 us (27%)
  matrix products  19.9 us (15%)
  starting transfers between devices  16.5 us (13%)
  other arithmetic  7.4 us (6%)
  local copies, waits for them, and re-layouts  6.88 us (5%)
    all_to_all x1, blocking collectives, shards(): lax.all_to_all(outgoing, 'expert', split_axis=0, concat_axis=0, tiled=True)  41.9 us
    ppermute x5, waiting for transfers between devices, gather_axis(): lax.ppermute(x, name, [(j, (j + shift) % n) for j in range(n)])  16.4 us
    all_to_all x1, waiting for transfers between devices, shards(): lax.all_to_all(expert_out, 'expert', split_axis=0, concat_axis=0, tiled=T...  11.2 us
    dot_general x4, matrix products, by_rows(): lax.dot_general(left, weight_rows, (((1,), (1,)), ((), ())), preferred_el...  9.61 us
    ppermute x5, starting transfers between devices, gather_axis(): lax.ppermute(x, name, [(j, (j + shift) % n) for j in range(n)])  5.24 us
    all_to_all x1, starting transfers between devices, shards(): lax.all_to_all(expert_out, 'expert', split_axis=0, concat_axis=0, tiled=T...  4.61 us
    all_to_all x1, waiting for transfers between devices, shards(): lax.all_to_all(columns, 'dp', split_axis=1, concat_axis=3, tiled=True)[0, 0]  4.09 us
    all_to_all x1, waiting for transfers between devices, shards(): lax.all_to_all(combined, 'dp', split_axis=0, concat_axis=2, tiled=True)[0]  3.53 us
  transfers between devices with their start and end apart: 8, of which 5 were waited for; matrix products, arithmetic and copies ran while one was open for 10% of the time, Pallas kernels for 0%

profile of v1, /device:TPU:0, one launch (start us, length us, event | category | flops | bytes accessed | tf_op | source)
XLA Modules:
  0.0 128.7 jit_solution(17526194311899023386)
XLA Ops:
  0.7 3.0 %collective-permute-start = (bf16[1,1,16,1024]{3,2,1,0:T(8,128)(2,1)}, bf16[1,1,16,1024]{3,2,1,0:T(8,128)(2,1)S(1)}, u32[]{:S(2)}, u32[]{:S(2)}) collective-permute-start(bf16[1,1,16,1024]{3,2,1,0:T(8,128)(2,1)} %param.14), channel_id=1, source_target_pairs={{0,16},{16,0},{1,17},{17,1},{2,18},{18,2},{3,19},{19,3},{4,20},{20... | collective-permute-start | bytes 98312 | tf_op jit(solution)/shard_map/ppermute | solution.py:28
  7.9 2.7 %convolution_convert_fusion.1 = bf16[32,1024]{1,0:T(8,128)(2,1)} fusion(bf16[32,1024]{1,0:T(8,128)(2,1)S(1)} %bitcast.92, bf16[1024,1024]{1,0:T(8,128)(2,1)} %param.16), kind=kOutput, calls=%fused_computation.13 | convolution fusion | flops 67141632 | bytes 2228224 | tf_op jit(solution)/shard_map/dot_general | solution.py:73
  10.6 3.3 %all-to-all-start = ((bf16[1,2,16,1024]{3,2,0,1:T(8,128)(2,1)}), bf16[1,2,16,1024]{3,2,0,1:T(8,128)(2,1)S(1)}, u32[]{:S(2)}, u32[]{:S(2)}) async-start(bf16[1,2,16,1024]{3,2,0,1:T(8,128)(2,1)} %bitcast.2), calls=%async_computation | async-start | bytes 131072 | tf_op jit(solution)/shard_map/all_to_all | solution.py:75
  14.0 4.1 %all-to-all-done = bf16[1,2,16,1024]{3,2,0,1:T(8,128)(2,1)S(1)} async-done(((bf16[1,2,16,1024]{3,2,0,1:T(8,128)(2,1)}), bf16[1,2,16,1024]{3,2,0,1:T(8,128)(2,1)S(1)}, u32[]{:S(2)}, u32[]{:S(2)}) %all-to-all-start) | async-done | bytes 65568 | tf_op jit(solution)/shard_map/all_to_all | solution.py:75
  18.6 4.1 %collective-permute-done.1 = bf16[16,2048]{1,0:T(8,128)(2,1)S(1)} collective-permute-done((bf16[16,2048]{1,0:T(8,128)(2,1)S(1)}, bf16[16,2048]{1,0:T(8,128)(2,1)S(1)}, u32[]{:S(2)}, u32[]{:S(2)}) %collective-permute-start.1) | collective-permute-done | bytes 65568 | tf_op jit(solution)/shard_map/ppermute | solution.py:28
  23.4 41.9 %all_to_all.34 = bf16[16,24,2048]{2,1,0:T(8,128)(2,1)S(1)} all-to-all(bf16[16,24,2048]{2,1,0:T(8,128)(2,1)S(1)} %bitcast.83), channel_id=1, replica_groups=mesh['dp'=2,'expert'=16] {'expert'}, dimensions={0} | all-to-all | bytes 3145728 | tf_op jit(solution)/shard_map/all_to_all | solution.py:106
  65.3 1.7 %fusion.4 = f32[384,704]{0,1:T(8,128)S(1)} fusion(bf16[384,2048]{1,0:T(8,128)(2,1)S(1)} %bitcast.84, bf16[1,704,2048]{2,1,0:T(8,128)(2,1)S(1)} %copy-done.4), kind=kOutput, calls=%fused_computation.5 | convolution fusion | flops 1107296256 | bytes 5537792 | tf_op jit(solution)/shard_map/dot_general | solution.py:16
  67.2 2.5 %fusion.12 = bf16[384,704]{0,1:T(8,128)(2,1)} fusion(bf16[384,2048]{1,0:T(8,128)(2,1)S(1)} %bitcast.85, bf16[1,704,2048]{2,1,0:T(8,128)(2,1)S(1)} %copy-done.5, f32[384,704]{0,1:T(8,128)S(1)} %fusion.4), kind=kOutput, calls=%fused_computation.10 | convolution fusion | flops 1108918272 | bytes 6078464 | tf_op jit(solution)/shard_map/dot_general | solution.py:16
  70.0 2.7 %fusion.39 = f32[32,704]{1,0:T(8,128)S(1)} fusion(bf16[704,2048]{1,0:T(8,128)(2,1)} %param.24, bf16[16,2048]{1,0:T(8,128)(2,1)S(1)} %get-tuple-element.9, bf16[16,2048]{1,0:T(8,128)(2,1)S(1)} %get-tuple-element.8), kind=kOutput, calls=%fused_computation.73 | convolution fusion | flops 92536832 | bytes 3104768 | tf_op jit(solution)/shard_map/dot_general | solution.py:16
  72.7 12.2 %collective-permute-done.3 = bf16[384,704]{0,1:T(8,128)(2,1)} collective-permute-done((bf16[384,704]{0,1:T(8,128)(2,1)}, bf16[384,704]{0,1:T(8,128)(2,1)}, u32[]{:S(2)}, u32[]{:S(2)}) %collective-permute-start.3) | collective-permute-done | bytes 540704 | tf_op jit(solution)/shard_map/ppermute | solution.py:28
  84.9 1.3 %broadcast_select_fusion.1 = (bf16[384,704]{0,1:T(8,128)(2,1)S(1)}, bf16[384,704]{0,1:T(8,128)(2,1)S(1)}) fusion(bf16[384,704]{0,1:T(8,128)(2,1)} %fusion.12, bf16[384,704]{0,1:T(8,128)(2,1)} %collective-permute-done.3, pred[]{:T(512)S(6)} %eq.16), kind=kLoop, calls=%fused_computation.18 | loop fusion | flops 540672 | bytes 2162689 | tf_op jit(solution)/shard_map/jit(_where)/select_n | solution.py:30
  86.3 2.3 %fusion.6 = bf16[384,1024]{1,0:T(8,128)(2,1)} fusion(bf16[1,1408,1024]{2,1,0:T(8,128)(2,1)S(1)} %copy-done, bf16[384,704]{0,1:T(8,128)(2,1)S(1)} %get-tuple-element.3, bf16[384,704]{0,1:T(8,128)(2,1)S(1)} %get-tuple-element.2), kind=kOutput, calls=%fused_computation.8 | convolution fusion | flops 1109852160 | bytes 4751360 | tf_op jit(solution)/shard_map/dot_general | solution.py:116
  88.6 4.6 %all-to-all-start.2 = ((bf16[16,24,1024]{2,1,0:T(8,128)(2,1)}), bf16[16,24,1024]{2,1,0:T(8,128)(2,1)}, u32[]{:S(2)}, u32[]{:S(2)}) async-start(bf16[16,24,1024]{2,1,0:T(8,128)(2,1)} %bitcast.90), calls=%async_computation.2 | async-start | bytes 1572864 | tf_op jit(solution)/shard_map/all_to_all | solution.py:119
  93.7 2.7 %multiply_convert_fusion.2 = bf16[32,704]{1,0:T(8,128)(2,1)S(1)} fusion(f32[32,704]{1,0:T(8,128)S(1)} %fusion.39, bf16[704,2048]{1,0:T(8,128)(2,1)} %param.25, bf16[16,2048]{1,0:T(8,128)(2,1)S(1)} %get-tuple-element.9, bf16[16,2048]{1,0:T(8,128)(2,1)S(1)} %get-tuple-element.8), kind=kOutput, calls=%fused_computation.35 | convolution fusion | flops 92672000 | bytes 3149824 | tf_op jit(solution)/shard_map/dot_general | solution.py:16
  96.4 1.8 %collective-permute-start.4 = (bf16[32,704]{1,0:T(8,128)(2,1)S(1)}, bf16[32,704]{1,0:T(8,128)(2,1)S(1)}, u32[]{:S(2)}, u32[]{:S(2)}) collective-permute-start(bf16[32,704]{1,0:T(8,128)(2,1)S(1)} %multiply_convert_fusion.2), channel_id=1, source_target_pairs={{0,16},{16,0},{1,17},{17,1},{2,18},{18,2},{3,19},{19,3},{4,20},{20... | collective-permute-start | bytes 135176 | tf_op jit(solution)/shard_map/ppermute | solution.py:28
  98.2 1.7 %gather_fusion = f32[192]{0:T(256)S(1)} fusion(f32[32,16]{0,1:T(8,128)S(1)} %pad_maximum_fusion.2, s32[192]{0:T(256)S(1)} %reshape.303), kind=kCustom, calls=%fused_computation | custom fusion | bytes 3072 | tf_op jit(solution)/shard_map/jit(take_along_axis)/gather | solution.py:82
  100.8 11.2 %all-to-all-done.2 = bf16[16,24,1024]{2,1,0:T(8,128)(2,1)} async-done(((bf16[16,24,1024]{2,1,0:T(8,128)(2,1)}), bf16[16,24,1024]{2,1,0:T(8,128)(2,1)}, u32[]{:S(2)}, u32[]{:S(2)}) %all-to-all-start.2) | async-done | bytes 786464 | tf_op jit(solution)/shard_map/all_to_all | solution.py:119
  112.0 1.4 %fusion.42 = f32[32,1024]{1,0:T(8,128)S(1)} fusion(bf16[32,384]{1,0:T(8,128)(2,1)S(1)} %fusion.21, bf16[384,1024]{1,0:T(8,128)(2,1)} %bitcast.14), kind=kOutput, calls=%fused_computation.76 | convolution fusion | flops 25165824 | bytes 942080 | tf_op jit(solution)/shard_map/dot_general | solution.py:125
  113.3 3.1 %fusion.15 = f32[32,1024]{1,0:T(8,128)} fusion(f32[32,1024]{1,0:T(8,128)S(1)} %fusion.42, bf16[1408,1024]{1,0:T(8,128)(2,1)} %param.26, bf16[32,704]{1,0:T(8,128)(2,1)S(1)} %get-tuple-element.11, bf16[32,704]{1,0:T(8,128)(2,1)S(1)} %get-tuple-element.10, pred[32]{0:T(512)(128)(4,1)S(1)} %lt.57), kind=kOutput, calls=%fused_computation.12 | convolution fusion | flops 92520448 | bytes 3235872 | tf_op jit(solution)/shard_map/dot_general | solution.py:117
  116.4 3.4 %all-to-all-start.3 = ((f32[2,16,1024]{2,1,0:T(8,128)}), f32[2,16,1024]{2,1,0:T(8,128)S(1)}, u32[]{:S(2)}, u32[]{:S(2)}) async-start(f32[2,16,1024]{2,1,0:T(8,128)} %bitcast.15), calls=%async_computation.3 | async-start | bytes 262144 | tf_op jit(solution)/shard_map/all_to_all | solution.py:129
  120.7 3.5 %all-to-all-done.3 = f32[2,16,1024]{2,1,0:T(8,128)S(1)} async-done(((f32[2,16,1024]{2,1,0:T(8,128)}), f32[2,16,1024]{2,1,0:T(8,128)S(1)}, u32[]{:S(2)}, u32[]{:S(2)}) %all-to-all-start.3) | async-done | bytes 131104 | tf_op jit(solution)/shard_map/all_to_all | solution.py:129
  125.0 1.0 squeeze.17
  126.1 1.2 fusion.24
  127.2 1.4 %multiply_convert_fusion = (bf16[1,1,16,2048]{3,2,1,0:T(8,128)(2,1)}, bf16[1,1,16,2048]{3,2,1,0:T(8,128)(2,1)}) fusion(f32[2048]{0:T(1024)} %param.27, f32[16]{0:T(128)S(1)} %add_rsqrt_fusion, f32[1,1,16,2048]{3,2,1,0:T(8,128)S(1)} %squeeze.17, f32[1,1,16,2048]{3,2,1,0:T(8,128)S(1)} %reshape.295, bf16[1,1,16,2048]{3,2,1,0:T(8,128)(2,1)S(1)} %copy-done.1), kind=kLoop, calls=%fused_computation.30 | loop fusion | flops 229376 | bytes 467008 | tf_op jit(solution)/shard_map/convert_element_type | solution.py:132
  (69 shorter events, 8.8 us)
Async XLA Ops:
  0.6 85.6 %copy-start = (bf16[1,1408,1024]{2,1,0:T(8,128)(2,1)S(1)}, bf16[1,1408,1024]{2,1,0:T(8,128)(2,1)}, u32[]{:S(2)}) copy-start(bf16[1,1408,1024]{2,1,0:T(8,128)(2,1)} %param.23) | copy-start | bytes 8650756
  0.6 17.5 %copy-start.1 = (bf16[1,1,16,2048]{3,2,1,0:T(8,128)(2,1)S(1)}, bf16[1,1,16,2048]{3,2,1,0:T(8,128)(2,1)}, u32[]{:S(2)}) copy-start(bf16[1,1,16,2048]{3,2,1,0:T(8,128)(2,1)} %param.15) | copy-start | bytes 196612
  0.7 17.7 %copy-start.3 = (f32[2048]{0:T(1024)S(1)}, f32[2048]{0:T(1024)}, u32[]{:S(2)}) copy-start(f32[2048]{0:T(1024)} %param.17) | copy-start | bytes 24580
  0.7 6.5 %collective-permute-start = (bf16[1,1,16,1024]{3,2,1,0:T(8,128)(2,1)}, bf16[1,1,16,1024]{3,2,1,0:T(8,128)(2,1)S(1)}, u32[]{:S(2)}, u32[]{:S(2)}) collective-permute-start(bf16[1,1,16,1024]{3,2,1,0:T(8,128)(2,1)} %param.14), channel_id=1, source_target_pairs={{0,16},{16,0},{1,17},{17,1},{2,18},{18,2},{3,19},{19,3},{4,20},{20... | collective-permute-start | bytes 98312 | tf_op jit(solution)/shard_map/ppermute | solution.py:28
  10.6 7.4 %all-to-all-start = ((bf16[1,2,16,1024]{3,2,0,1:T(8,128)(2,1)}), bf16[1,2,16,1024]{3,2,0,1:T(8,128)(2,1)S(1)}, u32[]{:S(2)}, u32[]{:S(2)}) async-start(bf16[1,2,16,1024]{3,2,0,1:T(8,128)(2,1)} %bitcast.2), calls=%async_computation | async-start | bytes 131072 | tf_op jit(solution)/shard_map/all_to_all | solution.py:75
  18.4 4.3 %collective-permute-start.1 = (bf16[16,2048]{1,0:T(8,128)(2,1)S(1)}, bf16[16,2048]{1,0:T(8,128)(2,1)S(1)}, u32[]{:S(2)}, u32[]{:S(2)}) collective-permute-start(bf16[16,2048]{1,0:T(8,128)(2,1)S(1)} %multiply_convert_fusion.1), channel_id=1, source_target_pairs={{0,16},{16,0},{1,17},{17,1},{2,18},{18,2},{3,19},{19,3},{4,20},{20... | collective-permute-start | bytes 196616 | tf_op jit(solution)/shard_map/ppermute | solution.py:28
  22.8 42.6 %copy-start.4 = (bf16[1,704,2048]{2,1,0:T(8,128)(2,1)S(1)}, bf16[1,704,2048]{2,1,0:T(8,128)(2,1)}, u32[]{:S(2)}) copy-start(bf16[1,704,2048]{2,1,0:T(8,128)(2,1)} %param.21) | copy-start | bytes 8650756
  65.3 1.8 %copy-start.5 = (bf16[1,704,2048]{2,1,0:T(8,128)(2,1)S(1)}, bf16[1,704,2048]{2,1,0:T(8,128)(2,1)}, u32[]{:S(2)}) copy-start(bf16[1,704,2048]{2,1,0:T(8,128)(2,1)} %param.22) | copy-start | bytes 8650756
  67.2 2.5 %copy-start.2 = (s32[1,2,16,6]{2,1,3,0:T(2,128)S(1)}, s32[1,2,16,6]{2,1,3,0:T(2,128)}, u32[]{:S(2)}) copy-start(s32[1,2,16,6]{2,1,3,0:T(2,128)} %param.19) | copy-start | bytes 2308
  69.7 15.3 %collective-permute-start.3 = (bf16[384,704]{0,1:T(8,128)(2,1)}, bf16[384,704]{0,1:T(8,128)(2,1)}, u32[]{:S(2)}, u32[]{:S(2)}) collective-permute-start(bf16[384,704]{0,1:T(8,128)(2,1)} %fusion.12), channel_id=1, source_target_pairs={{0,16},{16,0},{1,17},{17,1},{2,18},{18,2},{3,19},{19,3},{4,20},{20... | collective-permute-start | bytes 1622024 | tf_op jit(solution)/shard_map/ppermute | solution.py:28
  86.2 7.0 %copy-start.6 = (bf16[2048,8]{0,1:T(8,128)(2,1)S(1)}, bf16[2048,8]{0,1:T(8,128)(2,1)}, u32[]{:S(2)}) copy-start(bf16[2048,8]{0,1:T(8,128)(2,1)} %param.18) | copy-start | bytes 98308
  88.6 23.4 %all-to-all-start.2 = ((bf16[16,24,1024]{2,1,0:T(8,128)(2,1)}), bf16[16,24,1024]{2,1,0:T(8,128)(2,1)}, u32[]{:S(2)}, u32[]{:S(2)}) async-start(bf16[16,24,1024]{2,1,0:T(8,128)(2,1)} %bitcast.90), calls=%async_computation.2 | async-start | bytes 1572864 | tf_op jit(solution)/shard_map/all_to_all | solution.py:119
  93.4 4.9 %collective-permute-start.2 = (f32[32,8]{0,1:T(8,128)S(1)}, f32[32,8]{0,1:T(8,128)S(1)}, u32[]{:S(2)}, u32[]{:S(2)}) collective-permute-start(f32[32,8]{0,1:T(8,128)S(1)} %fusion.40), channel_id=1, source_target_pairs={{0,16},{16,0},{1,17},{17,1},{2,18},{18,2},{3,19},{19,3},{4,20},{20... | collective-permute-start | bytes 3080 | tf_op jit(solution)/shard_map/ppermute | solution.py:28
  96.4 4.4 %collective-permute-start.4 = (bf16[32,704]{1,0:T(8,128)(2,1)S(1)}, bf16[32,704]{1,0:T(8,128)(2,1)S(1)}, u32[]{:S(2)}, u32[]{:S(2)}) collective-permute-start(bf16[32,704]{1,0:T(8,128)(2,1)S(1)} %multiply_convert_fusion.2), channel_id=1, source_target_pairs={{0,16},{16,0},{1,17},{17,1},{2,18},{18,2},{3,19},{19,3},{4,20},{20... | collective-permute-start | bytes 135176 | tf_op jit(solution)/shard_map/ppermute | solution.py:28
  116.4 7.8 %all-to-all-start.3 = ((f32[2,16,1024]{2,1,0:T(8,128)}), f32[2,16,1024]{2,1,0:T(8,128)S(1)}, u32[]{:S(2)}, u32[]{:S(2)}) async-start(f32[2,16,1024]{2,1,0:T(8,128)} %bitcast.15), calls=%async_computation.3 | async-start | bytes 262144 | tf_op jit(solution)/shard_map/all_to_all | solution.py:129

commit v2 on v0

--- a/solution.py
+++ b/solution.py
@@ -25,7 +25,7 @@
     return jnp.where((source >= 0)[:, None], chosen, jnp.zeros_like(chosen))
 
 
-def shards(
+def shards_general(
     attention,
     residual,
     out_proj,
@@ -125,6 +125,137 @@
     return (stream, normed)
 
 
+def swap_pair(x):
+    return lax.ppermute(x, "dp", [(0, 1), (1, 0)])
+
+
+def halves_swapped(x):
+    half = x.shape[0] // 2
+    return jnp.concatenate([x[half:], x[:half]], axis=0)
+
+
+def in_axis_order(first, mine, peer, axis):
+    return jnp.where(
+        first, jnp.concatenate([mine, peer], axis=axis), jnp.concatenate([peer, mine], axis=axis)
+    )
+
+
+def shards_pair(
+    attention,
+    residual,
+    out_proj,
+    gain_in,
+    router,
+    expert_ids,
+    live_rows,
+    expert_gate,
+    expert_up,
+    expert_down,
+    shared_gate,
+    shared_up,
+    shared_down,
+    gain_out,
+):
+    groups = 2
+    experts = lax.axis_size("expert")
+    me = lax.axis_index("dp")
+    first = me == 0
+    row_count = attention.shape[2]
+    top_count = expert_ids.shape[3]
+    capacity = max(2, (2 * row_count * top_count + experts - 1) // experts)
+    gate_local = expert_gate[0]
+    up_local = expert_up[0]
+    down_local = expert_down[0]
+    column_width = down_local.shape[1]
+    rows_all = groups * row_count
+
+    attention_mine = attention[0, 0]
+    pieces = jnp.concatenate([attention_mine, swap_pair(attention_mine)], axis=0)
+    product = jnp.dot(pieces, out_proj, preferred_element_type=jnp.float32).astype(jnp.bfloat16)
+    projected = in_axis_order(first, product[:row_count], swap_pair(product[row_count:]), 1)
+    stream_in = residual[0, 0].astype(jnp.float32) + projected.astype(jnp.float32)
+    normal_rows = rms_scale(stream_in, gain_in).astype(jnp.bfloat16)
+    column = jnp.concatenate([normal_rows, swap_pair(normal_rows)], axis=0)
+    logit_part = jnp.dot(column, router, preferred_element_type=jnp.float32)
+    logits = in_axis_order(first, logit_part, halves_swapped(swap_pair(logit_part)), 1)
+
+    ids = expert_ids[0]
+    ids_local = jnp.where(first, ids, ids[::-1])
+    counts = live_rows[:, 0]
+    counts_local = jnp.where(first, counts, counts[::-1])
+    group_of_block = jnp.where(first, jnp.arange(groups), jnp.arange(groups)[::-1]).astype(jnp.int32)
+
+    flat_experts = ids_local.reshape(rows_all, top_count)
+    picked = jnp.take_along_axis(logits, flat_experts, axis=1)
+    probabilities = jax.nn.softmax(picked, axis=1)
+    row_live = (jnp.arange(row_count, dtype=jnp.int32)[None, :] < counts_local[:, None]).reshape(
+        rows_all
+    )
+    slot_live = jnp.broadcast_to(row_live[:, None], (rows_all, top_count))
+    weights = probabilities.astype(jnp.bfloat16) * slot_live.astype(jnp.bfloat16)
+    block_experts = flat_experts.reshape(groups, row_count * top_count)
+    block_live = slot_live.reshape(groups, row_count * top_count)
+    onehot = (
+        (block_experts[:, :, None] == jnp.arange(experts, dtype=jnp.int32)) & block_live[:, :, None]
+    ).astype(jnp.int32)
+    before = jnp.cumsum(onehot, axis=1) - onehot
+    position = jnp.sum(before * onehot, axis=2)
+    slot_total = experts * groups * capacity
+    offsets = group_of_block[:, None] * capacity
+    target = jnp.where(
+        block_live, block_experts * (groups * capacity) + offsets + position, slot_total
+    ).reshape(rows_all, top_count)
+    slot_hit = target[:, :, None] == jnp.arange(slot_total, dtype=jnp.int32)[None, None, :]
+    fill = jnp.any(slot_hit, axis=1).astype(jnp.bfloat16)
+    outgoing = lax.dot_general(
+        fill, column, (((0,), (0,)), ((), ())), preferred_element_type=jnp.float32
+    ).astype(jnp.bfloat16).reshape(experts, groups * capacity, column.shape[1])
+    slot_rows = lax.all_to_all(outgoing, "expert", split_axis=0, concat_axis=0, tiled=True)
+    flattened = slot_rows.reshape(-1, slot_rows.shape[-1])
+    gate_value = by_rows(flattened, gate_local)
+    up_value = by_rows(flattened, up_local)
+    hidden = (jax.nn.silu(gate_value) * up_value).astype(jnp.bfloat16)
+    hidden_peer = swap_pair(hidden)
+    shared_gate_value = by_rows(column, shared_gate)
+    shared_up_value = by_rows(column, shared_up)
+    shared_hidden = (jax.nn.silu(shared_gate_value) * shared_up_value).astype(jnp.bfloat16)
+    shared_peer = halves_swapped(swap_pair(shared_hidden))
+
+    unit_count = hidden.shape[1]
+    down_blocks = down_local.reshape(groups, unit_count, column_width)
+    shared_blocks = shared_down.reshape(groups, unit_count, column_width)
+    down_mine = lax.dynamic_index_in_dim(down_blocks, me, 0, keepdims=False)
+    down_peer = lax.dynamic_index_in_dim(down_blocks, 1 - me, 0, keepdims=False)
+    shared_mine = lax.dynamic_index_in_dim(shared_blocks, me, 0, keepdims=False)
+    shared_other = lax.dynamic_index_in_dim(shared_blocks, 1 - me, 0, keepdims=False)
+    routed_total = jnp.dot(hidden, down_mine, preferred_element_type=jnp.float32) + jnp.dot(
+        hidden_peer, down_peer, preferred_element_type=jnp.float32
+    )
+    shared = jnp.dot(shared_hidden, shared_mine, preferred_element_type=jnp.float32) + jnp.dot(
+        shared_peer, shared_other, preferred_element_type=jnp.float32
+    )
+    expert_out = routed_total.astype(jnp.bfloat16).reshape(experts, groups * capacity, column_width)
+    returned = lax.all_to_all(
+        expert_out, "expert", split_axis=0, concat_axis=0, tiled=True
+    ).reshape(slot_total, column_width)
+    combine = jnp.sum(
+        jnp.where(slot_hit, weights[:, :, None], jnp.zeros((), jnp.bfloat16)), axis=1
+    ).astype(jnp.bfloat16)
+    routed = jnp.dot(combine, returned, preferred_element_type=jnp.float32)
+    combined = jnp.where(row_live[:, None], routed + shared, 0.0)
+    summed = in_axis_order(first, combined[:row_count], swap_pair(combined[row_count:]), 1)
+    stream_sum = stream_in + summed
+    stream = stream_sum.astype(jnp.bfloat16)[None, None]
+    normed = rms_scale(stream_sum, gain_out).astype(jnp.bfloat16)[None, None]
+    return (stream, normed)
+
+
+def shards(*args):
+    if lax.axis_size("dp") == 2:
+        return shards_pair(*args)
+    return shards_general(*args)
+
+
 def solution(mesh):
     placed = (
         P("expert", "dp", None, None),

time: 225 us -> 118 us (0.52)
  blocking collectives: 62.7 us -> 0 us
  local copies, waits for them, and re-layouts: 29.1 us -> 4.88 us
  waiting for transfers between devices: 80 us -> 63 us
  between operations: 14.4 us -> 0.88 us
  starting transfers between devices: 12.5 us -> 22.6 us
  matrix products: 18.9 us -> 22.3 us
  other arithmetic: 6.82 us -> 3.61 us
    all_gather x1 -> x0, waiting for transfers between devices: 74 us -> none  [shards(): routed_piece = lax.all_gather(routed_hidden, 'dp', axis=2, tiled=True)]
    all_to_all x1 -> x0, blocking collectives: 42.6 us -> none  [shards(): lax.all_to_all(outgoing, 'expert', split_axis=0, concat_axis=0, tiled=True)]
    all_to_all x3 -> x2, waiting for transfers between devices: 5.98 us -> 40.9 us  [the longest x1 28.3 us: shards_pair(): lax.all_to_all(outgoing, 'expert', split_axis=0, concat_axis=0, tiled=True)]
    ppermute x0 -> x7, waiting for transfers between devices: none -> 22.1 us  [swap_pair(): return lax.ppermute(x, 'dp', [(0, 1), (1, 0)])]
    all_gather x4 -> x0, blocking collectives: 20.1 us -> none  [the longest x1 5.88 us: shards(): pieces = lax.all_gather(attention, 'dp', axis=1, tiled=True)]
    ppermute x0 -> x7, starting transfers between devices: none -> 7.5 us  [swap_pair(): return lax.ppermute(x, 'dp', [(0, 1), (1, 0)])]
    all_gather x2 -> x0, local copies, waits for them, and re-layouts: 7.19 us -> none  [the longest x1 7.09 us: shards(): routed_piece = lax.all_gather(routed_hidden, 'dp', axis=2, tiled=True)]
    gather x8 -> x6, local copies, waits for them, and re-layouts: 8.64 us -> 2.13 us  [shards_pair(): picked = jnp.take_along_axis(logits, flat_experts, axis=1)]
  transfers between devices with their start and end apart: 4 -> 9, of which waited for: 4 -> 6; matrix products, arithmetic and copies ran while one was open for 5% -> 20% of each run, Pallas kernels for 0% -> 0%
where the time goes in v2:
time: 118 us; the launch traced here: 117 us
  waiting for transfers between devices  63 us (53%)
  starting transfers between devices  22.6 us (19%)
  matrix products  22.3 us (19%)
  local copies, waits for them, and re-layouts  4.88 us (4%)
  other arithmetic  3.61 us (3%)
    all_to_all x1, waiting for transfers between devices, shards_pair(): lax.all_to_all(outgoing, 'expert', split_axis=0, concat_axis=0, tiled=True)  28.3 us
    ppermute x7, waiting for transfers between devices, swap_pair(): return lax.ppermute(x, 'dp', [(0, 1), (1, 0)])  22.1 us
    all_to_all x1, waiting for transfers between devices, shards_pair(): lax.all_to_all(expert_out, 'expert', split_axis=0, concat_axis=0, tiled=T...  12.6 us
    dot_general x4, matrix products, by_rows(): lax.dot_general(left, weight_rows, (((1,), (1,)), ((), ())), preferred_el...  11 us
    all_to_all x1, starting transfers between devices, shards_pair(): lax.all_to_all(expert_out, 'expert', split_axis=0, concat_axis=0, tiled=T...  9.01 us
    ppermute x7, starting transfers between devices, swap_pair(): return lax.ppermute(x, 'dp', [(0, 1), (1, 0)])  7.5 us
    all_to_all x1, starting transfers between devices, shards_pair(): lax.all_to_all(outgoing, 'expert', split_axis=0, concat_axis=0, tiled=True)  6.09 us
  transfers between devices with their start and end apart: 9, of which 6 were waited for; matrix products, arithmetic and copies ran while one was open for 20% of the time, Pallas kernels for 0%

profile of v2, /device:TPU:0, one launch (start us, length us, event | category | flops | bytes accessed | tf_op | source)
XLA Modules:
  0.0 117.3 jit_solution(13448888629256575732)
XLA Ops:
  0.7 3.0 %collective-permute-start = (bf16[16,1024]{1,0:T(8,128)(2,1)}, bf16[16,1024]{1,0:T(8,128)(2,1)S(1)}, u32[]{:S(2)}, u32[]{:S(2)}) collective-permute-start(bf16[16,1024]{1,0:T(8,128)(2,1)} %bitcast.81), channel_id=1, source_target_pairs={{0,16},{16,0},{1,17},{17,1},{2,18},{18,2},{3,19},{19,3},{4,20},{20... | collective-permute-start | bytes 98312 | tf_op jit(solution)/shard_map/ppermute | solution.py:129
  3.7 0.7 rev.9
  5.5 0.8 copy.26
  7.3 2.1 %convolution_convert_fusion.1 = bf16[32,1024]{1,0:T(8,128)(2,1)S(1)} fusion(bf16[1024,1024]{1,0:T(8,128)(2,1)} %param.16, bf16[16,1024]{1,0:T(8,128)(2,1)S(1)} %collective-permute-done, bf16[16,1024]{1,0:T(8,128)(2,1)} %bitcast.82), kind=kOutput, calls=%fused_computation.23 | convolution fusion | flops 67272704 | bytes 2228224 | tf_op jit(solution)/shard_map/dot_general | solution.py:174
  10.0 3.4 %collective-permute-done.1 = bf16[16,1024]{1,0:T(8,128)(2,1)S(1)} collective-permute-done((bf16[16,1024]{1,0:T(8,128)(2,1)S(1)}, bf16[16,1024]{1,0:T(8,128)(2,1)S(1)}, u32[]{:S(2)}, u32[]{:S(2)}) %collective-permute-start.1) | collective-permute-done | bytes 32800 | tf_op jit(solution)/shard_map/ppermute | solution.py:129
  14.3 3.7 %collective-permute-done.2 = bf16[16,2048]{1,0:T(8,128)(2,1)S(1)} collective-permute-done((bf16[16,2048]{1,0:T(8,128)(2,1)S(1)}, bf16[16,2048]{1,0:T(8,128)(2,1)S(1)}, u32[]{:S(2)}, u32[]{:S(2)}) %collective-permute-start.2) | collective-permute-done | bytes 65568 | tf_op jit(solution)/shard_map/ppermute | solution.py:129
  18.0 1.8 %convolution_convert_fusion = bf16[384,2048]{1,0:T(8,128)(2,1)} fusion(pred[32,384]{1,0:T(8,128)(4,1)S(1)} %fusion.25, bf16[16,2048]{1,0:T(8,128)(2,1)S(1)} %collective-permute-done.2, bf16[16,2048]{1,0:T(8,128)(2,1)S(1)} %multiply_convert_fusion.1), kind=kOutput, calls=%fused_computation.5 | convolution fusion | flops 51380224 | bytes 1716224 | tf_op jit(solution)/shard_map/dot_general | solution.py:210
  19.8 6.1 %all-to-all-start = ((bf16[16,24,2048]{2,1,0:T(8,128)(2,1)}), bf16[16,24,2048]{2,1,0:T(8,128)(2,1)}, u32[]{:S(2)}, u32[]{:S(2)}) async-start(bf16[16,24,2048]{2,1,0:T(8,128)(2,1)} %bitcast.68), calls=%async_computation | async-start | bytes 3145728 | tf_op jit(solution)/shard_map/all_to_all | solution.py:213
  26.9 2.7 %fusion.54 = f32[32,704]{1,0:T(8,128)S(1)} fusion(bf16[704,2048]{1,0:T(8,128)(2,1)} %param.24, bf16[16,2048]{1,0:T(8,128)(2,1)S(1)} %collective-permute-done.2, bf16[16,2048]{1,0:T(8,128)(2,1)S(1)} %multiply_convert_fusion.1), kind=kOutput, calls=%fused_computation.83 | convolution fusion | flops 92536832 | bytes 3104768 | tf_op jit(solution)/shard_map/dot_general | solution.py:16
  29.6 28.3 %all-to-all-done = bf16[16,24,2048]{2,1,0:T(8,128)(2,1)} async-done(((bf16[16,24,2048]{2,1,0:T(8,128)(2,1)}), bf16[16,24,2048]{2,1,0:T(8,128)(2,1)}, u32[]{:S(2)}, u32[]{:S(2)}) %all-to-all-start) | async-done | bytes 1572896 | tf_op jit(solution)/shard_map/all_to_all | solution.py:213
  57.9 4.1 %fusion.2 = f32[384,704]{0,1:T(8,128)S(1)} fusion(bf16[384,2048]{1,0:T(8,128)(2,1)} %bitcast.9, bf16[1,704,2048]{2,1,0:T(8,128)(2,1)} %param.21), kind=kOutput, calls=%fused_computation.3 | convolution fusion | flops 1107296256 | bytes 5537792 | tf_op jit(solution)/shard_map/dot_general | solution.py:16
  62.0 3.3 %fusion.18 = bf16[384,704]{0,1:T(8,128)(2,1)S(1)} fusion(bf16[384,2048]{1,0:T(8,128)(2,1)} %bitcast.9, bf16[1,704,2048]{2,1,0:T(8,128)(2,1)S(1)} %copy-done.5, f32[384,704]{0,1:T(8,128)S(1)} %fusion.2), kind=kOutput, calls=%fused_computation.19 | convolution fusion | flops 1108918272 | bytes 6078464 | tf_op jit(solution)/shard_map/dot_general | solution.py:16
  65.9 0.9 multiply_convert_fusion.2
  66.8 1.5 %collective-permute-start.5 = (bf16[32,704]{1,0:T(8,128)(2,1)S(1)}, bf16[32,704]{1,0:T(8,128)(2,1)S(1)}, u32[]{:S(2)}, u32[]{:S(2)}) collective-permute-start(bf16[32,704]{1,0:T(8,128)(2,1)S(1)} %multiply_convert_fusion.2), channel_id=1, source_target_pairs={{0,16},{16,0},{1,17},{17,1},{2,18},{18,2},{3,19},{19,3},{4,20},{20... | collective-permute-start | bytes 135176 | tf_op jit(solution)/shard_map/ppermute | solution.py:129
  68.4 0.8 fusion.9
  69.2 11.3 %collective-permute-done.4 = bf16[384,704]{0,1:T(8,128)(2,1)S(1)} collective-permute-done((bf16[384,704]{0,1:T(8,128)(2,1)S(1)}, bf16[384,704]{0,1:T(8,128)(2,1)S(1)}, u32[]{:S(2)}, u32[]{:S(2)}) %collective-permute-start.4) | collective-permute-done | bytes 540704 | tf_op jit(solution)/shard_map/ppermute | solution.py:129
  80.5 1.7 %add_convert_fusion = bf16[384,1024]{1,0:T(8,128)(2,1)} fusion(f32[384,1024]{1,0:T(8,128)S(1)} %fusion.9, bf16[384,704]{0,1:T(8,128)(2,1)S(1)} %collective-permute-done.4, bf16[2,704,1024]{2,1,0:T(8,128)(2,1)S(1)} %bitcast.67, s32[]{:T(128)S(6)} %select_n.142), kind=kOutput, calls=%fused_computation.6 | convolution fusion | flops 554434560 | bytes 4341764 | tf_op jit(solution)/shard_map/dot_general | solution.py:231
  82.2 9.0 %all-to-all-start.1 = ((bf16[16,24,1024]{2,1,0:T(8,128)(2,1)}), bf16[16,24,1024]{2,1,0:T(8,128)(2,1)}, u32[]{:S(2)}, u32[]{:S(2)}) async-start(bf16[16,24,1024]{2,1,0:T(8,128)(2,1)} %bitcast.73), calls=%async_computation.1 | async-start | bytes 1572864 | tf_op jit(solution)/shard_map/all_to_all | solution.py:238
  91.2 1.7 %fusion.6 = f32[32,1024]{1,0:T(8,128)S(1)} fusion(bf16[32,704]{1,0:T(8,128)(2,1)S(1)} %multiply_convert_fusion.2, bf16[2,704,1024]{2,1,0:T(8,128)(2,1)} %bitcast.69, s32[]{:T(128)S(6)} %select_n.141), kind=kOutput, calls=%fused_computation.9 | convolution fusion | flops 46137344 | bytes 1617924 | tf_op jit(solution)/shard_map/dot_general | solution.py:234
  93.1 1.7 %gather_fusion = f32[192]{0:T(256)S(1)} fusion(f32[32,16]{0,1:T(8,128)S(1)} %maximum_select_fusion.4, s32[192]{0:T(256)S(1)} %reshape.356), kind=kCustom, calls=%fused_computation | custom fusion | bytes 3072 | tf_op jit(solution)/shard_map/jit(take_along_axis)/gather | solution.py:189
  95.7 1.7 %fusion.22 = f32[32,1024]{1,0:T(8,128)S(1)} fusion(f32[32,1024]{1,0:T(8,128)S(1)} %fusion.6, bf16[2,704,1024]{2,1,0:T(8,128)(2,1)} %bitcast.70, s32[]{:T(128)S(6)} %select_n.142, bf16[16,704]{1,0:T(8,128)(2,1)S(1)} %get-tuple-element.9, bf16[16,704]{1,0:T(8,128)(2,1)S(1)} %get-tuple-element.8), kind=kOutput, calls=%fused_computation.22 | convolution fusion | flops 46260224 | bytes 1748996 | tf_op jit(solution)/shard_map/dot_general | solution.py:234
  97.4 12.6 %all-to-all-done.1 = bf16[16,24,1024]{2,1,0:T(8,128)(2,1)} async-done(((bf16[16,24,1024]{2,1,0:T(8,128)(2,1)}), bf16[16,24,1024]{2,1,0:T(8,128)(2,1)}, u32[]{:S(2)}, u32[]{:S(2)}) %all-to-all-start.1) | async-done | bytes 786464 | tf_op jit(solution)/shard_map/all_to_all | solution.py:238
  110.0 1.4 %fusion.21 = f32[32,1024]{1,0:T(8,128)S(1)} fusion(f32[32,1024]{1,0:T(8,128)S(1)} %fusion.22, bf16[32,384]{1,0:T(8,128)(2,1)S(1)} %fusion.27, bf16[384,1024]{1,0:T(8,128)(2,1)} %bitcast.16, pred[32]{0:T(512)(128)(4,1)S(1)} %lt.63), kind=kOutput, calls=%fused_computation.21 | convolution fusion | flops 25231360 | bytes 1073184 | tf_op jit(solution)/shard_map/dot_general | solution.py:244
  112.0 3.7 %collective-permute-done.6 = f32[16,1024]{1,0:T(8,128)S(1)} collective-permute-done((f32[16,1024]{1,0:T(8,128)S(1)}, f32[16,1024]{1,0:T(8,128)S(1)}, u32[]{:S(2)}, u32[]{:S(2)}) %collective-permute-start.6) | collective-permute-done | bytes 65568 | tf_op jit(solution)/shard_map/ppermute | solution.py:129
  (68 shorter events, 8.4 us)
Async XLA Ops:
  0.6 67.7 %copy-start = (bf16[1,1408,1024]{2,1,0:T(8,128)(2,1)S(1)}, bf16[1,1408,1024]{2,1,0:T(8,128)(2,1)}, u32[]{:S(2)}) copy-start(bf16[1,1408,1024]{2,1,0:T(8,128)(2,1)} %param.23) | copy-start | bytes 8650756
  0.6 12.8 %copy-start.2 = (bf16[1,1,16,2048]{3,2,1,0:T(8,128)(2,1)S(1)}, bf16[1,1,16,2048]{3,2,1,0:T(8,128)(2,1)}, u32[]{:S(2)}) copy-start(bf16[1,1,16,2048]{3,2,1,0:T(8,128)(2,1)} %param.15) | copy-start | bytes 196612
  0.7 12.9 %copy-start.3 = (f32[2048]{0:T(1024)S(1)}, f32[2048]{0:T(1024)}, u32[]{:S(2)}) copy-start(f32[2048]{0:T(1024)} %param.17) | copy-start | bytes 24580
  0.7 6.6 %collective-permute-start = (bf16[16,1024]{1,0:T(8,128)(2,1)}, bf16[16,1024]{1,0:T(8,128)(2,1)S(1)}, u32[]{:S(2)}, u32[]{:S(2)}) collective-permute-start(bf16[16,1024]{1,0:T(8,128)(2,1)} %bitcast.81), channel_id=1, source_target_pairs={{0,16},{16,0},{1,17},{17,1},{2,18},{18,2},{3,19},{19,3},{4,20},{20... | collective-permute-start | bytes 98312 | tf_op jit(solution)/shard_map/ppermute | solution.py:129
  9.4 4.0 %collective-permute-start.1 = (bf16[16,1024]{1,0:T(8,128)(2,1)S(1)}, bf16[16,1024]{1,0:T(8,128)(2,1)S(1)}, u32[]{:S(2)}, u32[]{:S(2)}) collective-permute-start(bf16[16,1024]{1,0:T(8,128)(2,1)S(1)} %get-tuple-element.6), channel_id=1, source_target_pairs={{0,16},{16,0},{1,17},{17,1},{2,18},{18,2},{3,19},{19,3},{4,20},{20... | collective-permute-start | bytes 98312 | tf_op jit(solution)/shard_map/ppermute | solution.py:129
  13.7 4.3 %collective-permute-start.2 = (bf16[16,2048]{1,0:T(8,128)(2,1)S(1)}, bf16[16,2048]{1,0:T(8,128)(2,1)S(1)}, u32[]{:S(2)}, u32[]{:S(2)}) collective-permute-start(bf16[16,2048]{1,0:T(8,128)(2,1)S(1)} %multiply_convert_fusion.1), channel_id=1, source_target_pairs={{0,16},{16,0},{1,17},{17,1},{2,18},{18,2},{3,19},{19,3},{4,20},{20... | collective-permute-start | bytes 196616 | tf_op jit(solution)/shard_map/ppermute | solution.py:129
  19.8 6.4 %copy-start.6 = (bf16[2048,8]{0,1:T(8,128)(2,1)S(1)}, bf16[2048,8]{0,1:T(8,128)(2,1)}, u32[]{:S(2)}) copy-start(bf16[2048,8]{0,1:T(8,128)(2,1)} %param.18) | copy-start | bytes 98308
  19.8 38.1 %all-to-all-start = ((bf16[16,24,2048]{2,1,0:T(8,128)(2,1)}), bf16[16,24,2048]{2,1,0:T(8,128)(2,1)}, u32[]{:S(2)}, u32[]{:S(2)}) async-start(bf16[16,24,2048]{2,1,0:T(8,128)(2,1)} %bitcast.68), calls=%async_computation | async-start | bytes 3145728 | tf_op jit(solution)/shard_map/all_to_all | solution.py:213
  26.3 66.7 %collective-permute-start.3 = (f32[32,8]{0,1:T(8,128)S(1)}, f32[32,8]{0,1:T(8,128)S(1)}, u32[]{:S(2)}, u32[]{:S(2)}) collective-permute-start(f32[32,8]{0,1:T(8,128)S(1)} %fusion.55), channel_id=1, source_target_pairs={{0,16},{16,0},{1,17},{17,1},{2,18},{18,2},{3,19},{19,3},{4,20},{20... | collective-permute-start | bytes 3080 | tf_op jit(solution)/shard_map/ppermute | solution.py:129
  57.9 4.1 %copy-start.5 = (bf16[1,704,2048]{2,1,0:T(8,128)(2,1)S(1)}, bf16[1,704,2048]{2,1,0:T(8,128)(2,1)}, u32[]{:S(2)}) copy-start(bf16[1,704,2048]{2,1,0:T(8,128)(2,1)} %param.22) | copy-start | bytes 8650756
  62.0 3.9 %copy-start.1 = (bf16[704,2048]{1,0:T(8,128)(2,1)S(1)}, bf16[704,2048]{1,0:T(8,128)(2,1)}, u32[]{:S(2)}) copy-start(bf16[704,2048]{1,0:T(8,128)(2,1)} %param.25) | copy-start | bytes 8650756
  65.3 15.2 %collective-permute-start.4 = (bf16[384,704]{0,1:T(8,128)(2,1)S(1)}, bf16[384,704]{0,1:T(8,128)(2,1)S(1)}, u32[]{:S(2)}, u32[]{:S(2)}) collective-permute-start(bf16[384,704]{0,1:T(8,128)(2,1)S(1)} %fusion.18), channel_id=1, source_target_pairs={{0,16},{16,0},{1,17},{17,1},{2,18},{18,2},{3,19},{19,3},{4,20},{20... | collective-permute-start | bytes 1622024 | tf_op jit(solution)/shard_map/ppermute | solution.py:129
  66.8 28.8 %collective-permute-start.5 = (bf16[32,704]{1,0:T(8,128)(2,1)S(1)}, bf16[32,704]{1,0:T(8,128)(2,1)S(1)}, u32[]{:S(2)}, u32[]{:S(2)}) collective-permute-start(bf16[32,704]{1,0:T(8,128)(2,1)S(1)} %multiply_convert_fusion.2), channel_id=1, source_target_pairs={{0,16},{16,0},{1,17},{17,1},{2,18},{18,2},{3,19},{19,3},{4,20},{20... | collective-permute-start | bytes 135176 | tf_op jit(solution)/shard_map/ppermute | solution.py:129
  82.2 27.8 %all-to-all-start.1 = ((bf16[16,24,1024]{2,1,0:T(8,128)(2,1)}), bf16[16,24,1024]{2,1,0:T(8,128)(2,1)}, u32[]{:S(2)}, u32[]{:S(2)}) async-start(bf16[16,24,1024]{2,1,0:T(8,128)(2,1)} %bitcast.73), calls=%async_computation.1 | async-start | bytes 1572864 | tf_op jit(solution)/shard_map/all_to_all | solution.py:238
  95.7 20.9 %copy-start.4 = (f32[2048]{0:T(1024)S(1)}, f32[2048]{0:T(1024)}, u32[]{:S(2)}) copy-start(f32[2048]{0:T(1024)} %param.27) | copy-start | bytes 24580
  111.4 4.3 %collective-permute-start.6 = (f32[16,1024]{1,0:T(8,128)S(1)}, f32[16,1024]{1,0:T(8,128)S(1)}, u32[]{:S(2)}, u32[]{:S(2)}) collective-permute-start(f32[16,1024]{1,0:T(8,128)S(1)} %get-tuple-element.4), channel_id=1, source_target_pairs={{0,16},{16,0},{1,17},{17,1},{2,18},{18,2},{3,19},{19,3},{4,20},{20... | collective-permute-start | bytes 196616 | tf_op jit(solution)/shard_map/ppermute | solution.py:129

commit v3 on v2

--- a/solution.py
+++ b/solution.py
@@ -212,25 +212,34 @@
     ).astype(jnp.bfloat16).reshape(experts, groups * capacity, column.shape[1])
     slot_rows = lax.all_to_all(outgoing, "expert", split_axis=0, concat_axis=0, tiled=True)
     flattened = slot_rows.reshape(-1, slot_rows.shape[-1])
-    gate_value = by_rows(flattened, gate_local)
-    up_value = by_rows(flattened, up_local)
-    hidden = (jax.nn.silu(gate_value) * up_value).astype(jnp.bfloat16)
-    hidden_peer = swap_pair(hidden)
+    unit_count = gate_local.shape[0]
+    split = min(unit_count, 384) if unit_count > 384 else unit_count
+    bounds = [(0, split)] + ([(split, unit_count)] if split < unit_count else [])
+    down_blocks = down_local.reshape(groups, unit_count, column_width)
+    down_mine = lax.dynamic_index_in_dim(down_blocks, me, 0, keepdims=False)
+    down_peer = lax.dynamic_index_in_dim(down_blocks, 1 - me, 0, keepdims=False)
+    chunks = []
+    for low, high in bounds:
+        gate_value = by_rows(flattened, gate_local[low:high])
+        up_value = by_rows(flattened, up_local[low:high])
+        hidden = (jax.nn.silu(gate_value) * up_value).astype(jnp.bfloat16)
+        chunks.append((low, high, hidden, swap_pair(hidden)))
     shared_gate_value = by_rows(column, shared_gate)
     shared_up_value = by_rows(column, shared_up)
     shared_hidden = (jax.nn.silu(shared_gate_value) * shared_up_value).astype(jnp.bfloat16)
     shared_peer = halves_swapped(swap_pair(shared_hidden))
 
-    unit_count = hidden.shape[1]
-    down_blocks = down_local.reshape(groups, unit_count, column_width)
-    shared_blocks = shared_down.reshape(groups, unit_count, column_width)
-    down_mine = lax.dynamic_index_in_dim(down_blocks, me, 0, keepdims=False)
-    down_peer = lax.dynamic_index_in_dim(down_blocks, 1 - me, 0, keepdims=False)
+    routed_total = None
+    for low, high, hidden, _ in chunks:
+        part = jnp.dot(hidden, down_mine[low:high], preferred_element_type=jnp.float32)
+        routed_total = part if routed_total is None else routed_total + part
+    for low, high, _, hidden_peer in chunks:
+        routed_total = routed_total + jnp.dot(
+            hidden_peer, down_peer[low:high], preferred_element_type=jnp.float32
+        )
+    shared_blocks = shared_down.reshape(groups, shared_hidden.shape[1], column_width)
     shared_mine = lax.dynamic_index_in_dim(shared_blocks, me, 0, keepdims=False)
     shared_other = lax.dynamic_index_in_dim(shared_blocks, 1 - me, 0, keepdims=False)
-    routed_total = jnp.dot(hidden, down_mine, preferred_element_type=jnp.float32) + jnp.dot(
-        hidden_peer, down_peer, preferred_element_type=jnp.float32
-    )
     shared = jnp.dot(shared_hidden, shared_mine, preferred_element_type=jnp.float32) + jnp.dot(
         shared_peer, shared_other, preferred_element_type=jnp.float32
     )

time: 118 us -> 118 us (level)
  waiting for transfers between devices: 63 us -> 58.4 us
  matrix products: 22.3 us -> 26 us
    dot_general x4 -> x6, matrix products: 11 us -> 14 us  [by_rows(): lax.dot_general(left, weight_rows, (((1,), (1,)), ((), ())), preferred_el...]
    all_to_all x1, waiting for transfers between devices: 28.3 us -> 25.8 us  [shards_pair(): lax.all_to_all(outgoing, 'expert', split_axis=0, concat_axis=0, tiled=True)]
    ppermute x7 -> x8, waiting for transfers between devices: 22.1 us -> 20 us  [swap_pair(): return lax.ppermute(x, 'dp', [(0, 1), (1, 0)])]
    ppermute x7 -> x8, starting transfers between devices: 7.5 us -> 8.76 us  [swap_pair(): return lax.ppermute(x, 'dp', [(0, 1), (1, 0)])]
    dot_general x2 -> x4, matrix products: 2.52 us -> 3.25 us  [the longest x2 2.07 us: shards_pair(): jnp.dot(hidden_peer, down_peer[low:high], preferred_element_type=jnp.floa...]
  transfers between devices with their start and end apart: 9 -> 10, of which waited for: 6 -> 6; matrix products, arithmetic and copies ran while one was open for 20% -> 23% of each run, Pallas kernels for 0% -> 0%
where the time goes in v3:
time: 118 us; the launch traced here: 117 us
  waiting for transfers between devices  58.4 us (49%)
  matrix products  26 us (22%)
  starting transfers between devices  23.5 us (20%)
  local copies, waits for them, and re-layouts  4.88 us (4%)
  other arithmetic  3.61 us (3%)
    all_to_all x1, waiting for transfers between devices, shards_pair(): lax.all_to_all(outgoing, 'expert', split_axis=0, concat_axis=0, tiled=True)  25.8 us
    ppermute x8, waiting for transfers between devices, swap_pair(): return lax.ppermute(x, 'dp', [(0, 1), (1, 0)])  20 us
    dot_general x6, matrix products, by_rows(): lax.dot_general(left, weight_rows, (((1,), (1,)), ((), ())), preferred_el...  14 us
    all_to_all x1, waiting for transfers between devices, shards_pair(): lax.all_to_all(expert_out, 'expert', split_axis=0, concat_axis=0, tiled=T...  12.6 us
    ppermute x8, starting transfers between devices, swap_pair(): return lax.ppermute(x, 'dp', [(0, 1), (1, 0)])  8.76 us
    all_to_all x1, starting transfers between devices, shards_pair(): lax.all_to_all(expert_out, 'expert', split_axis=0, concat_axis=0, tiled=T...  8.68 us
    all_to_all x1, starting transfers between devices, shards_pair(): lax.all_to_all(outgoing, 'expert', split_axis=0, concat_axis=0, tiled=True)  6.08 us
  transfers between devices with their start and end apart: 10, of which 6 were waited for; matrix products, arithmetic and copies ran while one was open for 23% of the time, Pallas kernels for 0%

profile of v3, /device:TPU:0, one launch (start us, length us, event | category | flops | bytes accessed | tf_op | source)
XLA Modules:
  0.0 117.4 jit_solution(14567396285225985086)
XLA Ops:
  0.7 3.0 %collective-permute-start = (bf16[16,1024]{1,0:T(8,128)(2,1)}, bf16[16,1024]{1,0:T(8,128)(2,1)S(1)}, u32[]{:S(2)}, u32[]{:S(2)}) collective-permute-start(bf16[16,1024]{1,0:T(8,128)(2,1)} %bitcast.105), channel_id=1, source_target_pairs={{0,16},{16,0},{1,17},{17,1},{2,18},{18,2},{3,19},{19,3},{4,20},{20... | collective-permute-start | bytes 98312 | tf_op jit(solution)/shard_map/ppermute | solution.py:129
  7.3 2.1 %convolution_convert_fusion.1 = bf16[32,1024]{1,0:T(8,128)(2,1)S(1)} fusion(bf16[1024,1024]{1,0:T(8,128)(2,1)} %param.16, bf16[16,1024]{1,0:T(8,128)(2,1)S(1)} %collective-permute-done, bf16[16,1024]{1,0:T(8,128)(2,1)} %bitcast.106), kind=kOutput, calls=%fused_computation.28 | convolution fusion | flops 67272704 | bytes 2228224 | tf_op jit(solution)/shard_map/dot_general | solution.py:174
  10.0 3.4 %collective-permute-done.1 = bf16[16,1024]{1,0:T(8,128)(2,1)S(1)} collective-permute-done((bf16[16,1024]{1,0:T(8,128)(2,1)S(1)}, bf16[16,1024]{1,0:T(8,128)(2,1)S(1)}, u32[]{:S(2)}, u32[]{:S(2)}) %collective-permute-start.1) | collective-permute-done | bytes 32800 | tf_op jit(solution)/shard_map/ppermute | solution.py:129
  14.3 3.7 %collective-permute-done.2 = bf16[16,2048]{1,0:T(8,128)(2,1)S(1)} collective-permute-done((bf16[16,2048]{1,0:T(8,128)(2,1)S(1)}, bf16[16,2048]{1,0:T(8,128)(2,1)S(1)}, u32[]{:S(2)}, u32[]{:S(2)}) %collective-permute-start.2) | collective-permute-done | bytes 65568 | tf_op jit(solution)/shard_map/ppermute | solution.py:129
  18.0 1.8 %convolution_convert_fusion = bf16[384,2048]{1,0:T(8,128)(2,1)} fusion(pred[32,384]{1,0:T(8,128)(4,1)S(1)} %fusion.38, bf16[16,2048]{1,0:T(8,128)(2,1)S(1)} %collective-permute-done.2, bf16[16,2048]{1,0:T(8,128)(2,1)S(1)} %multiply_convert_fusion.1), kind=kOutput, calls=%fused_computation.1 | convolution fusion | flops 51380224 | bytes 1716224 | tf_op jit(solution)/shard_map/dot_general | solution.py:210
  19.8 6.1 %all-to-all-start = ((bf16[16,24,2048]{2,1,0:T(8,128)(2,1)}), bf16[16,24,2048]{2,1,0:T(8,128)(2,1)}, u32[]{:S(2)}, u32[]{:S(2)}) async-start(bf16[16,24,2048]{2,1,0:T(8,128)(2,1)} %bitcast.92), calls=%async_computation | async-start | bytes 3145728 | tf_op jit(solution)/shard_map/all_to_all | solution.py:213
  26.9 3.0 %fusion.69 = f32[32,704]{1,0:T(8,128)S(1)} fusion(bf16[704,2048]{1,0:T(8,128)(2,1)} %param.24, bf16[16,2048]{1,0:T(8,128)(2,1)S(1)} %collective-permute-done.2, bf16[16,2048]{1,0:T(8,128)(2,1)S(1)} %multiply_convert_fusion.1), kind=kOutput, calls=%fused_computation.98 | convolution fusion | flops 92536832 | bytes 3104768 | tf_op jit(solution)/shard_map/dot_general | solution.py:16
  29.9 0.9 multiply_convert_fusion.2
  30.8 1.3 %collective-permute-start.6 = (bf16[32,704]{1,0:T(8,128)(2,1)S(1)}, bf16[32,704]{1,0:T(8,128)(2,1)S(1)}, u32[]{:S(2)}, u32[]{:S(2)}) collective-permute-start(bf16[32,704]{1,0:T(8,128)(2,1)S(1)} %multiply_convert_fusion.2), channel_id=1, source_target_pairs={{0,16},{16,0},{1,17},{17,1},{2,18},{18,2},{3,19},{19,3},{4,20},{20... | collective-permute-start | bytes 135176 | tf_op jit(solution)/shard_map/ppermute | solution.py:129
  32.1 25.8 %all-to-all-done = bf16[16,24,2048]{2,1,0:T(8,128)(2,1)} async-done(((bf16[16,24,2048]{2,1,0:T(8,128)(2,1)}), bf16[16,24,2048]{2,1,0:T(8,128)(2,1)}, u32[]{:S(2)}, u32[]{:S(2)}) %all-to-all-start) | async-done | bytes 1572896 | tf_op jit(solution)/shard_map/all_to_all | solution.py:213
  57.9 2.8 %fusion.14 = f32[384,320]{0,1:T(8,128)S(1)} fusion(bf16[384,2048]{1,0:T(8,128)(2,1)} %bitcast.9, bf16[1,704,2048]{2,1,0:T(8,128)(2,1)} %param.21), kind=kOutput, calls=%fused_computation.17 | convolution fusion | flops 503316480 | bytes 3375104 | tf_op jit(solution)/shard_map/dot_general | solution.py:16
  60.7 2.6 %fusion.2 = f32[384,384]{1,0:T(8,128)S(1)} fusion(bf16[384,2048]{1,0:T(8,128)(2,1)} %bitcast.9, bf16[1,704,2048]{2,1,0:T(8,128)(2,1)S(1)} %copy-done.5), kind=kOutput, calls=%fused_computation.4 | convolution fusion | flops 603979776 | bytes 3735552 | tf_op jit(solution)/shard_map/dot_general | solution.py:16
  63.3 2.3 %fusion.27 = bf16[384,320]{0,1:T(8,128)(2,1)S(1)} fusion(bf16[384,2048]{1,0:T(8,128)(2,1)} %bitcast.9, bf16[1,704,2048]{2,1,0:T(8,128)(2,1)S(1)} %copy-done.6, f32[384,320]{0,1:T(8,128)S(1)} %fusion.14), kind=kOutput, calls=%fused_computation.24 | convolution fusion | flops 504053760 | bytes 3620864 | tf_op jit(solution)/shard_map/dot_general | solution.py:16
  66.2 2.4 %fusion.24 = bf16[384,384]{1,0:T(8,128)(2,1)S(1)} fusion(bf16[384,2048]{1,0:T(8,128)(2,1)} %bitcast.9, bf16[1,704,2048]{2,1,0:T(8,128)(2,1)S(1)} %copy-done.6, f32[384,384]{1,0:T(8,128)S(1)} %fusion.2), kind=kOutput, calls=%fused_computation.23 | convolution fusion | flops 604864512 | bytes 4030464 | tf_op jit(solution)/shard_map/dot_general | solution.py:16
  68.6 1.5 %collective-permute-start.4 = (bf16[384,384]{1,0:T(8,128)(2,1)S(1)}, bf16[384,384]{1,0:T(8,128)(2,1)S(1)}, u32[]{:S(2)}, u32[]{:S(2)}) collective-permute-start(bf16[384,384]{1,0:T(8,128)(2,1)S(1)} %fusion.24), channel_id=1, source_target_pairs={{0,16},{16,0},{1,17},{17,1},{2,18},{18,2},{3,19},{19,3},{4,20},{20... | collective-permute-start | bytes 884744 | tf_op jit(solution)/shard_map/ppermute | solution.py:129
  71.3 9.2 %collective-permute-done.4 = bf16[384,384]{1,0:T(8,128)(2,1)S(1)} collective-permute-done((bf16[384,384]{1,0:T(8,128)(2,1)S(1)}, bf16[384,384]{1,0:T(8,128)(2,1)S(1)}, u32[]{:S(2)}, u32[]{:S(2)}) %collective-permute-start.4) | collective-permute-done | bytes 294944 | tf_op jit(solution)/shard_map/ppermute | solution.py:129
  81.2 1.5 %add_convert_fusion = bf16[384,1024]{1,0:T(8,128)(2,1)} fusion(f32[384,1024]{1,0:T(8,128)S(1)} %fusion.34, f32[384,1024]{1,0:T(8,128)S(1)} %fusion.35, f32[384,1024]{1,0:T(8,128)S(1)} %fusion.37, bf16[384,320]{0,1:T(8,128)(2,1)S(1)} %collective-permute-done.5, bf16[2,704,1024]{2,1,0:T(8,128)(2,1)S(1)} %bitcast.89, s32[]{:T(128)S(6)} %select_n.142, s32[]{:T(128)S(6)} %add.147), kind=kOutput, calls=%fused_computation.6 | convolution fusion | flops 253231104 | bytes 6406152 | tf_op jit(solution)/shard_map/dot_general | solution.py:237
  82.7 8.7 %all-to-all-start.1 = ((bf16[16,24,1024]{2,1,0:T(8,128)(2,1)}), bf16[16,24,1024]{2,1,0:T(8,128)(2,1)}, u32[]{:S(2)}, u32[]{:S(2)}) async-start(bf16[16,24,1024]{2,1,0:T(8,128)(2,1)} %bitcast.93), calls=%async_computation.1 | async-start | bytes 1572864 | tf_op jit(solution)/shard_map/all_to_all | solution.py:247
  91.4 1.7 %fusion.8 = f32[32,1024]{1,0:T(8,128)S(1)} fusion(bf16[32,704]{1,0:T(8,128)(2,1)S(1)} %multiply_convert_fusion.2, bf16[2,704,1024]{2,1,0:T(8,128)(2,1)} %bitcast.94, s32[]{:T(128)S(6)} %select_n.141), kind=kOutput, calls=%fused_computation.11 | convolution fusion | flops 46137344 | bytes 1617924 | tf_op jit(solution)/shard_map/dot_general | solution.py:243
  93.3 1.7 %gather_fusion = f32[192]{0:T(256)S(1)} fusion(f32[32,16]{0,1:T(8,128)S(1)} %maximum_select_fusion.4, s32[192]{0:T(256)S(1)} %reshape.364), kind=kCustom, calls=%fused_computation | custom fusion | bytes 3072 | tf_op jit(solution)/shard_map/jit(take_along_axis)/gather | solution.py:189
  95.8 1.7 %fusion.31 = f32[32,1024]{1,0:T(8,128)S(1)} fusion(f32[32,1024]{1,0:T(8,128)S(1)} %fusion.8, bf16[2,704,1024]{2,1,0:T(8,128)(2,1)} %bitcast.95, s32[]{:T(128)S(6)} %select_n.142, bf16[16,704]{1,0:T(8,128)(2,1)S(1)} %get-tuple-element.9, bf16[16,704]{1,0:T(8,128)(2,1)S(1)} %get-tuple-element.8), kind=kOutput, calls=%fused_computation.27 | convolution fusion | flops 46260224 | bytes 1748996 | tf_op jit(solution)/shard_map/dot_general | solution.py:243
  97.5 12.6 %all-to-all-done.1 = bf16[16,24,1024]{2,1,0:T(8,128)(2,1)} async-done(((bf16[16,24,1024]{2,1,0:T(8,128)(2,1)}), bf16[16,24,1024]{2,1,0:T(8,128)(2,1)}, u32[]{:S(2)}, u32[]{:S(2)}) %all-to-all-start.1) | async-done | bytes 786464 | tf_op jit(solution)/shard_map/all_to_all | solution.py:247
  110.1 1.4 %fusion.30 = f32[32,1024]{1,0:T(8,128)S(1)} fusion(f32[32,1024]{1,0:T(8,128)S(1)} %fusion.31, bf16[32,384]{1,0:T(8,128)(2,1)S(1)} %fusion.40, bf16[384,1024]{1,0:T(8,128)(2,1)} %bitcast.20, pred[32]{0:T(512)(128)(4,1)S(1)} %lt.63), kind=kOutput, calls=%fused_computation.26 | convolution fusion | flops 25231360 | bytes 1073184 | tf_op jit(solution)/shard_map/dot_general | solution.py:253
  112.2 3.7 %collective-permute-done.7 = f32[16,1024]{1,0:T(8,128)S(1)} collective-permute-done((f32[16,1024]{1,0:T(8,128)S(1)}, f32[16,1024]{1,0:T(8,128)S(1)}, u32[]{:S(2)}, u32[]{:S(2)}) %collective-permute-start.7) | collective-permute-done | bytes 65568 | tf_op jit(solution)/shard_map/ppermute | solution.py:129
  (76 shorter events, 11.7 us)
Async XLA Ops:
  0.6 69.5 %copy-start = (bf16[1,1408,1024]{2,1,0:T(8,128)(2,1)S(1)}, bf16[1,1408,1024]{2,1,0:T(8,128)(2,1)}, u32[]{:S(2)}) copy-start(bf16[1,1408,1024]{2,1,0:T(8,128)(2,1)} %param.23) | copy-start | bytes 8650756
  0.6 12.8 %copy-start.2 = (bf16[1,1,16,2048]{3,2,1,0:T(8,128)(2,1)S(1)}, bf16[1,1,16,2048]{3,2,1,0:T(8,128)(2,1)}, u32[]{:S(2)}) copy-start(bf16[1,1,16,2048]{3,2,1,0:T(8,128)(2,1)} %param.15) | copy-start | bytes 196612
  0.7 12.9 %copy-start.3 = (f32[2048]{0:T(1024)S(1)}, f32[2048]{0:T(1024)}, u32[]{:S(2)}) copy-start(f32[2048]{0:T(1024)} %param.17) | copy-start | bytes 24580
  0.7 6.6 %collective-permute-start = (bf16[16,1024]{1,0:T(8,128)(2,1)}, bf16[16,1024]{1,0:T(8,128)(2,1)S(1)}, u32[]{:S(2)}, u32[]{:S(2)}) collective-permute-start(bf16[16,1024]{1,0:T(8,128)(2,1)} %bitcast.105), channel_id=1, source_target_pairs={{0,16},{16,0},{1,17},{17,1},{2,18},{18,2},{3,19},{19,3},{4,20},{20... | collective-permute-start | bytes 98312 | tf_op jit(solution)/shard_map/ppermute | solution.py:129
  9.4 4.0 %collective-permute-start.1 = (bf16[16,1024]{1,0:T(8,128)(2,1)S(1)}, bf16[16,1024]{1,0:T(8,128)(2,1)S(1)}, u32[]{:S(2)}, u32[]{:S(2)}) collective-permute-start(bf16[16,1024]{1,0:T(8,128)(2,1)S(1)} %get-tuple-element.6), channel_id=1, source_target_pairs={{0,16},{16,0},{1,17},{17,1},{2,18},{18,2},{3,19},{19,3},{4,20},{20... | collective-permute-start | bytes 98312 | tf_op jit(solution)/shard_map/ppermute | solution.py:129
  13.7 4.3 %collective-permute-start.2 = (bf16[16,2048]{1,0:T(8,128)(2,1)S(1)}, bf16[16,2048]{1,0:T(8,128)(2,1)S(1)}, u32[]{:S(2)}, u32[]{:S(2)}) collective-permute-start(bf16[16,2048]{1,0:T(8,128)(2,1)S(1)} %multiply_convert_fusion.1), channel_id=1, source_target_pairs={{0,16},{16,0},{1,17},{17,1},{2,18},{18,2},{3,19},{19,3},{4,20},{20... | collective-permute-start | bytes 196616 | tf_op jit(solution)/shard_map/ppermute | solution.py:129
  19.8 6.4 %copy-start.7 = (bf16[2048,8]{0,1:T(8,128)(2,1)S(1)}, bf16[2048,8]{0,1:T(8,128)(2,1)}, u32[]{:S(2)}) copy-start(bf16[2048,8]{0,1:T(8,128)(2,1)} %param.18) | copy-start | bytes 98308
  19.8 38.1 %all-to-all-start = ((bf16[16,24,2048]{2,1,0:T(8,128)(2,1)}), bf16[16,24,2048]{2,1,0:T(8,128)(2,1)}, u32[]{:S(2)}, u32[]{:S(2)}) async-start(bf16[16,24,2048]{2,1,0:T(8,128)(2,1)} %bitcast.92), calls=%async_computation | async-start | bytes 3145728 | tf_op jit(solution)/shard_map/all_to_all | solution.py:213
  26.3 3.6 %copy-start.1 = (bf16[704,2048]{1,0:T(8,128)(2,1)S(1)}, bf16[704,2048]{1,0:T(8,128)(2,1)}, u32[]{:S(2)}) copy-start(bf16[704,2048]{1,0:T(8,128)(2,1)} %param.25) | copy-start | bytes 8650756
  26.3 66.8 %collective-permute-start.3 = (f32[32,8]{0,1:T(8,128)S(1)}, f32[32,8]{0,1:T(8,128)S(1)}, u32[]{:S(2)}, u32[]{:S(2)}) collective-permute-start(f32[32,8]{0,1:T(8,128)S(1)} %fusion.70), channel_id=1, source_target_pairs={{0,16},{16,0},{1,17},{17,1},{2,18},{18,2},{3,19},{19,3},{4,20},{20... | collective-permute-start | bytes 3080 | tf_op jit(solution)/shard_map/ppermute | solution.py:129
  30.8 65.0 %collective-permute-start.6 = (bf16[32,704]{1,0:T(8,128)(2,1)S(1)}, bf16[32,704]{1,0:T(8,128)(2,1)S(1)}, u32[]{:S(2)}, u32[]{:S(2)}) collective-permute-start(bf16[32,704]{1,0:T(8,128)(2,1)S(1)} %multiply_convert_fusion.2), channel_id=1, source_target_pairs={{0,16},{16,0},{1,17},{17,1},{2,18},{18,2},{3,19},{19,3},{4,20},{20... | collective-permute-start | bytes 135176 | tf_op jit(solution)/shard_map/ppermute | solution.py:129
  57.9 2.8 %copy-start.5 = (bf16[1,704,2048]{2,1,0:T(8,128)(2,1)S(1)}, bf16[1,704,2048]{2,1,0:T(8,128)(2,1)}, u32[]{:S(2)}) copy-start(bf16[1,704,2048]{2,1,0:T(8,128)(2,1)} %param.21) | copy-start | bytes 8650756
  60.7 2.6 %copy-start.6 = (bf16[1,704,2048]{2,1,0:T(8,128)(2,1)S(1)}, bf16[1,704,2048]{2,1,0:T(8,128)(2,1)}, u32[]{:S(2)}) copy-start(bf16[1,704,2048]{2,1,0:T(8,128)(2,1)} %param.22) | copy-start | bytes 8650756
  65.6 15.6 %collective-permute-start.5 = (bf16[384,320]{0,1:T(8,128)(2,1)S(1)}, bf16[384,320]{0,1:T(8,128)(2,1)S(1)}, u32[]{:S(2)}, u32[]{:S(2)}) collective-permute-start(bf16[384,320]{0,1:T(8,128)(2,1)S(1)} %fusion.27), channel_id=1, source_target_pairs={{0,16},{16,0},{1,17},{17,1},{2,18},{18,2},{3,19},{19,3},{4,20},{20... | collective-permute-start | bytes 737288 | tf_op jit(solution)/shard_map/ppermute | solution.py:129
  68.6 12.0 %collective-permute-start.4 = (bf16[384,384]{1,0:T(8,128)(2,1)S(1)}, bf16[384,384]{1,0:T(8,128)(2,1)S(1)}, u32[]{:S(2)}, u32[]{:S(2)}) collective-permute-start(bf16[384,384]{1,0:T(8,128)(2,1)S(1)} %fusion.24), channel_id=1, source_target_pairs={{0,16},{16,0},{1,17},{17,1},{2,18},{18,2},{3,19},{19,3},{4,20},{20... | collective-permute-start | bytes 884744 | tf_op jit(solution)/shard_map/ppermute | solution.py:129
  82.7 27.5 %all-to-all-start.1 = ((bf16[16,24,1024]{2,1,0:T(8,128)(2,1)}), bf16[16,24,1024]{2,1,0:T(8,128)(2,1)}, u32[]{:S(2)}, u32[]{:S(2)}) async-start(bf16[16,24,1024]{2,1,0:T(8,128)(2,1)} %bitcast.93), calls=%async_computation.1 | async-start | bytes 1572864 | tf_op jit(solution)/shard_map/all_to_all | solution.py:247
  95.8 20.9 %copy-start.4 = (f32[2048]{0:T(1024)S(1)}, f32[2048]{0:T(1024)}, u32[]{:S(2)}) copy-start(f32[2048]{0:T(1024)} %param.27) | copy-start | bytes 24580
  111.5 4.3 %collective-permute-start.7 = (f32[16,1024]{1,0:T(8,128)S(1)}, f32[16,1024]{1,0:T(8,128)S(1)}, u32[]{:S(2)}, u32[]{:S(2)}) collective-permute-start(f32[16,1024]{1,0:T(8,128)S(1)} %get-tuple-element.4), channel_id=1, source_target_pairs={{0,16},{16,0},{1,17},{17,1},{2,18},{18,2},{3,19},{19,3},{4,20},{20... | collective-permute-start | bytes 196616 | tf_op jit(solution)/shard_map/ppermute | solution.py:129

commit v4 on v2

--- a/solution.py
+++ b/solution.py
@@ -170,12 +170,14 @@
     rows_all = groups * row_count
 
     attention_mine = attention[0, 0]
+    residual_mine = residual[0, 0]
     pieces = jnp.concatenate([attention_mine, swap_pair(attention_mine)], axis=0)
+    residual_all = jnp.concatenate([residual_mine, swap_pair(residual_mine)], axis=0)
     product = jnp.dot(pieces, out_proj, preferred_element_type=jnp.float32).astype(jnp.bfloat16)
-    projected = in_axis_order(first, product[:row_count], swap_pair(product[row_count:]), 1)
-    stream_in = residual[0, 0].astype(jnp.float32) + projected.astype(jnp.float32)
-    normal_rows = rms_scale(stream_in, gain_in).astype(jnp.bfloat16)
-    column = jnp.concatenate([normal_rows, swap_pair(normal_rows)], axis=0)
+    projected = in_axis_order(first, product, halves_swapped(swap_pair(product)), 1)
+    stream_all = residual_all.astype(jnp.float32) + projected.astype(jnp.float32)
+    column = rms_scale(stream_all, gain_in).astype(jnp.bfloat16)
+    stream_in = stream_all[:row_count]
     logit_part = jnp.dot(column, router, preferred_element_type=jnp.float32)
     logits = in_axis_order(first, logit_part, halves_swapped(swap_pair(logit_part)), 1)
 

time: 118 us -> 115 us (0.975)
  waiting for transfers between devices: 63 us -> 56.2 us
  starting transfers between devices: 22.6 us -> 25.9 us
    ppermute x7, waiting for transfers between devices: 22.1 us -> 16.3 us  [swap_pair(): return lax.ppermute(x, 'dp', [(0, 1), (1, 0)])]
    ppermute x7, starting transfers between devices: 7.5 us -> 10.4 us  [swap_pair(): return lax.ppermute(x, 'dp', [(0, 1), (1, 0)])]
    convert_element_type x3 -> x1, other arithmetic: 1.47 us -> 0.09 us  [shards_pair(): column = rms_scale(stream_all, gain_in).astype(jnp.bfloat16)]
  transfers between devices with their start and end apart: 9 -> 9, of which waited for: 6 -> 5; matrix products, arithmetic and copies ran while one was open for 20% -> 23% of each run, Pallas kernels for 0% -> 0%
where the time goes in v4:
time: 115 us
  waiting for transfers between devices  56.2 us (49%)
  starting transfers between devices  25.9 us (23%)
  matrix products  22.3 us (19%)
  local copies, waits for them, and re-layouts  5.49 us (5%)
  other arithmetic  3.81 us (3%)
    all_to_all x1, waiting for transfers between devices, shards_pair(): lax.all_to_all(outgoing, 'expert', split_axis=0, concat_axis=0, tiled=True)  27.3 us
    ppermute x7, waiting for transfers between devices, swap_pair(): return lax.ppermute(x, 'dp', [(0, 1), (1, 0)])  16.3 us
    all_to_all x1, waiting for transfers between devices, shards_pair(): lax.all_to_all(expert_out, 'expert', split_axis=0, concat_axis=0, tiled=T...  12.6 us
    dot_general x4, matrix products, by_rows(): lax.dot_general(left, weight_rows, (((1,), (1,)), ((), ())), preferred_el...  11 us
    ppermute x7, starting transfers between devices, swap_pair(): return lax.ppermute(x, 'dp', [(0, 1), (1, 0)])  10.4 us
    all_to_all x1, starting transfers between devices, shards_pair(): lax.all_to_all(expert_out, 'expert', split_axis=0, concat_axis=0, tiled=T...  9.01 us
    all_to_all x1, starting transfers between devices, shards_pair(): lax.all_to_all(outgoing, 'expert', split_axis=0, concat_axis=0, tiled=True)  6.52 us
  transfers between devices with their start and end apart: 9, of which 5 were waited for; matrix products, arithmetic and copies ran while one was open for 23% of the time, Pallas kernels for 0%

profile of v4, /device:TPU:0, one launch (start us, length us, event | category | flops | bytes accessed | tf_op | source)
XLA Modules:
  0.0 114.7 jit_solution(7414331226156517540)
XLA Ops:
  0.7 3.0 %collective-permute-start.1 = (bf16[16,1024]{1,0:T(8,128)(2,1)}, bf16[16,1024]{1,0:T(8,128)(2,1)S(1)}, u32[]{:S(2)}, u32[]{:S(2)}) collective-permute-start(bf16[16,1024]{1,0:T(8,128)(2,1)} %bitcast.72), channel_id=1, source_target_pairs={{0,16},{16,0},{1,17},{17,1},{2,18},{18,2},{3,19},{19,3},{4,20},{20... | collective-permute-start | bytes 98312 | tf_op jit(solution)/shard_map/ppermute | solution.py:129
  7.4 2.1 %convolution_convert_fusion.1 = bf16[32,1024]{1,0:T(8,128)(2,1)S(1)} fusion(bf16[1024,1024]{1,0:T(8,128)(2,1)} %param.16, bf16[16,1024]{1,0:T(8,128)(2,1)S(1)} %collective-permute-done.1, bf16[16,1024]{1,0:T(8,128)(2,1)} %bitcast.73), kind=kOutput, calls=%fused_computation.24 | convolution fusion | flops 67272704 | bytes 2228224 | tf_op jit(solution)/shard_map/dot_general | solution.py:176
  9.5 2.0 %collective-permute-start.2 = (bf16[32,1024]{1,0:T(8,128)(2,1)S(1)}, bf16[32,1024]{1,0:T(8,128)(2,1)S(1)}, u32[]{:S(2)}, u32[]{:S(2)}) collective-permute-start(bf16[32,1024]{1,0:T(8,128)(2,1)S(1)} %convolution_convert_fusion.1), channel_id=1, source_target_pairs={{0,16},{16,0},{1,17},{17,1},{2,18},{18,2},{3,19},{19,3},{4,20},{20... | collective-permute-start | bytes 196616 | tf_op jit(solution)/shard_map/ppermute | solution.py:129
  11.6 2.2 %collective-permute-done.2 = bf16[32,1024]{1,0:T(8,128)(2,1)S(1)} collective-permute-done((bf16[32,1024]{1,0:T(8,128)(2,1)S(1)}, bf16[32,1024]{1,0:T(8,128)(2,1)S(1)}, u32[]{:S(2)}, u32[]{:S(2)}) %collective-permute-start.2) | collective-permute-done | bytes 65568 | tf_op jit(solution)/shard_map/ppermute | solution.py:129
  14.5 1.0 multiply_reduce_fusion
  15.6 1.8 %convolution_convert_fusion = bf16[384,2048]{1,0:T(8,128)(2,1)} fusion(pred[32,384]{1,0:T(8,128)(4,1)S(1)} %fusion.26, bf16[32,2048]{1,0:T(8,128)(2,1)S(1)} %multiply_convert_fusion), kind=kOutput, calls=%fused_computation.5 | convolution fusion | flops 51118080 | bytes 1716224 | tf_op jit(solution)/shard_map/dot_general | solution.py:212
  17.4 6.5 %all-to-all-start = ((bf16[16,24,2048]{2,1,0:T(8,128)(2,1)}), bf16[16,24,2048]{2,1,0:T(8,128)(2,1)}, u32[]{:S(2)}, u32[]{:S(2)}) async-start(bf16[16,24,2048]{2,1,0:T(8,128)(2,1)} %bitcast.61), calls=%async_computation | async-start | bytes 3145728 | tf_op jit(solution)/shard_map/all_to_all | solution.py:215
  24.4 1.5 %collective-permute-start.3 = (f32[32,8]{0,1:T(8,128)S(1)}, f32[32,8]{0,1:T(8,128)S(1)}, u32[]{:S(2)}, u32[]{:S(2)}) collective-permute-start(f32[32,8]{0,1:T(8,128)S(1)} %fusion.54), channel_id=1, source_target_pairs={{0,16},{16,0},{1,17},{17,1},{2,18},{18,2},{3,19},{19,3},{4,20},{20... | collective-permute-start | bytes 3080 | tf_op jit(solution)/shard_map/ppermute | solution.py:129
  25.9 2.7 %fusion.55 = f32[32,704]{1,0:T(8,128)S(1)} fusion(bf16[32,2048]{1,0:T(8,128)(2,1)S(1)} %multiply_convert_fusion, bf16[704,2048]{1,0:T(8,128)(2,1)} %param.24), kind=kOutput, calls=%fused_computation.81 | convolution fusion | flops 92274688 | bytes 3104768 | tf_op jit(solution)/shard_map/dot_general | solution.py:16
  28.6 27.3 %all-to-all-done = bf16[16,24,2048]{2,1,0:T(8,128)(2,1)} async-done(((bf16[16,24,2048]{2,1,0:T(8,128)(2,1)}), bf16[16,24,2048]{2,1,0:T(8,128)(2,1)}, u32[]{:S(2)}, u32[]{:S(2)}) %all-to-all-start) | async-done | bytes 1572896 | tf_op jit(solution)/shard_map/all_to_all | solution.py:215
  55.9 4.1 %fusion.2 = f32[384,704]{0,1:T(8,128)S(1)} fusion(bf16[384,2048]{1,0:T(8,128)(2,1)} %bitcast.7, bf16[1,704,2048]{2,1,0:T(8,128)(2,1)} %param.21), kind=kOutput, calls=%fused_computation.3 | convolution fusion | flops 1107296256 | bytes 5537792 | tf_op jit(solution)/shard_map/dot_general | solution.py:16
  60.1 3.3 %fusion.18 = bf16[384,704]{0,1:T(8,128)(2,1)S(1)} fusion(bf16[384,2048]{1,0:T(8,128)(2,1)} %bitcast.7, bf16[1,704,2048]{2,1,0:T(8,128)(2,1)S(1)} %copy-done.7, f32[384,704]{0,1:T(8,128)S(1)} %fusion.2), kind=kOutput, calls=%fused_computation.19 | convolution fusion | flops 1108918272 | bytes 6078464 | tf_op jit(solution)/shard_map/dot_general | solution.py:16
  63.4 1.6 %collective-permute-start.4 = (bf16[384,704]{0,1:T(8,128)(2,1)S(1)}, bf16[384,704]{0,1:T(8,128)(2,1)S(1)}, u32[]{:S(2)}, u32[]{:S(2)}) collective-permute-start(bf16[384,704]{0,1:T(8,128)(2,1)S(1)} %fusion.18), channel_id=1, source_target_pairs={{0,16},{16,0},{1,17},{17,1},{2,18},{18,2},{3,19},{19,3},{4,20},{20... | collective-permute-start | bytes 1622024 | tf_op jit(solution)/shard_map/ppermute | solution.py:129
  64.9 0.9 fusion.25
  67.2 11.3 %collective-permute-done.4 = bf16[384,704]{0,1:T(8,128)(2,1)S(1)} collective-permute-done((bf16[384,704]{0,1:T(8,128)(2,1)S(1)}, bf16[384,704]{0,1:T(8,128)(2,1)S(1)}, u32[]{:S(2)}, u32[]{:S(2)}) %collective-permute-start.4) | collective-permute-done | bytes 540704 | tf_op jit(solution)/shard_map/ppermute | solution.py:129
  78.6 1.7 %add_convert_fusion = bf16[384,1024]{1,0:T(8,128)(2,1)} fusion(f32[384,1024]{1,0:T(8,128)S(1)} %fusion.9, bf16[384,704]{0,1:T(8,128)(2,1)S(1)} %collective-permute-done.4, bf16[2,704,1024]{2,1,0:T(8,128)(2,1)S(1)} %bitcast.60, s32[]{:T(128)S(6)} %select_n.121), kind=kOutput, calls=%fused_computation.6 | convolution fusion | flops 554434560 | bytes 4341764 | tf_op jit(solution)/shard_map/dot_general | solution.py:233
  80.3 9.0 %all-to-all-start.1 = ((bf16[16,24,1024]{2,1,0:T(8,128)(2,1)}), bf16[16,24,1024]{2,1,0:T(8,128)(2,1)}, u32[]{:S(2)}, u32[]{:S(2)}) async-start(bf16[16,24,1024]{2,1,0:T(8,128)(2,1)} %bitcast.64), calls=%async_computation.1 | async-start | bytes 1572864 | tf_op jit(solution)/shard_map/all_to_all | solution.py:240
  89.3 1.7 %fusion.6 = f32[32,1024]{1,0:T(8,128)S(1)} fusion(bf16[32,704]{1,0:T(8,128)(2,1)S(1)} %fusion.25, bf16[2,704,1024]{2,1,0:T(8,128)(2,1)} %bitcast.62, s32[]{:T(128)S(6)} %select_n.120), kind=kOutput, calls=%fused_computation.9 | convolution fusion | flops 46137344 | bytes 1617924 | tf_op jit(solution)/shard_map/dot_general | solution.py:236
  91.2 1.7 %gather_fusion = f32[192]{0:T(256)S(1)} fusion(f32[32,16]{0,1:T(8,128)S(1)} %maximum_select_fusion.2, s32[192]{0:T(256)S(1)} %reshape.219), kind=kCustom, calls=%fused_computation | custom fusion | bytes 3072 | tf_op jit(solution)/shard_map/jit(take_along_axis)/gather | solution.py:191
  93.7 1.7 %fusion.22 = f32[32,1024]{1,0:T(8,128)S(1)} fusion(f32[32,1024]{1,0:T(8,128)S(1)} %fusion.6, bf16[2,704,1024]{2,1,0:T(8,128)(2,1)} %bitcast.63, s32[]{:T(128)S(6)} %select_n.121, bf16[16,704]{1,0:T(8,128)(2,1)S(1)} %get-tuple-element.13, bf16[16,704]{1,0:T(8,128)(2,1)S(1)} %get-tuple-element.12), kind=kOutput, calls=%fused_computation.22 | convolution fusion | flops 46260224 | bytes 1748996 | tf_op jit(solution)/shard_map/dot_general | solution.py:236
  95.5 12.6 %all-to-all-done.1 = bf16[16,24,1024]{2,1,0:T(8,128)(2,1)} async-done(((bf16[16,24,1024]{2,1,0:T(8,128)(2,1)}), bf16[16,24,1024]{2,1,0:T(8,128)(2,1)}, u32[]{:S(2)}, u32[]{:S(2)}) %all-to-all-start.1) | async-done | bytes 786464 | tf_op jit(solution)/shard_map/all_to_all | solution.py:240
  108.1 1.4 %fusion.21 = f32[32,1024]{1,0:T(8,128)S(1)} fusion(f32[32,1024]{1,0:T(8,128)S(1)} %fusion.22, bf16[32,384]{1,0:T(8,128)(2,1)S(1)} %fusion.28, bf16[384,1024]{1,0:T(8,128)(2,1)} %bitcast.14, pred[32]{0:T(512)(128)(4,1)S(1)} %lt.63), kind=kOutput, calls=%fused_computation.21 | convolution fusion | flops 25231360 | bytes 1073184 | tf_op jit(solution)/shard_map/dot_general | solution.py:246
  109.5 1.6 %collective-permute-start.6 = (f32[16,1024]{1,0:T(8,128)S(1)}, f32[16,1024]{1,0:T(8,128)S(1)}, u32[]{:S(2)}, u32[]{:S(2)}) collective-permute-start(f32[16,1024]{1,0:T(8,128)S(1)} %get-tuple-element.8), channel_id=1, source_target_pairs={{0,16},{16,0},{1,17},{17,1},{2,18},{18,2},{3,19},{19,3},{4,20},{20... | collective-permute-start | bytes 196616 | tf_op jit(solution)/shard_map/ppermute | solution.py:129
  111.0 2.7 %collective-permute-done.6 = f32[16,1024]{1,0:T(8,128)S(1)} collective-permute-done((f32[16,1024]{1,0:T(8,128)S(1)}, f32[16,1024]{1,0:T(8,128)S(1)}, u32[]{:S(2)}, u32[]{:S(2)}) %collective-permute-start.6) | collective-permute-done | bytes 65568 | tf_op jit(solution)/shard_map/ppermute | solution.py:129
  (69 shorter events, 8.3 us)
Async XLA Ops:
  0.6 65.8 %copy-start = (bf16[1,1408,1024]{2,1,0:T(8,128)(2,1)S(1)}, bf16[1,1408,1024]{2,1,0:T(8,128)(2,1)}, u32[]{:S(2)}) copy-start(bf16[1,1408,1024]{2,1,0:T(8,128)(2,1)} %param.23) | copy-start | bytes 8650756
  0.6 13.8 %copy-start.2 = (bf16[1,1,16,2048]{3,2,1,0:T(8,128)(2,1)S(1)}, bf16[1,1,16,2048]{3,2,1,0:T(8,128)(2,1)}, u32[]{:S(2)}) copy-start(bf16[1,1,16,2048]{3,2,1,0:T(8,128)(2,1)} %param.15) | copy-start | bytes 196612
  0.7 6.7 %collective-permute-start.1 = (bf16[16,1024]{1,0:T(8,128)(2,1)}, bf16[16,1024]{1,0:T(8,128)(2,1)S(1)}, u32[]{:S(2)}, u32[]{:S(2)}) collective-permute-start(bf16[16,1024]{1,0:T(8,128)(2,1)} %bitcast.72), channel_id=1, source_target_pairs={{0,16},{16,0},{1,17},{17,1},{2,18},{18,2},{3,19},{19,3},{4,20},{20... | collective-permute-start | bytes 98312 | tf_op jit(solution)/shard_map/ppermute | solution.py:129
  3.7 10.1 %collective-permute-start = (bf16[16,2048]{1,0:T(8,128)(2,1)}, bf16[16,2048]{1,0:T(8,128)(2,1)S(1)}, u32[]{:S(2)}, u32[]{:S(2)}) collective-permute-start(bf16[16,2048]{1,0:T(8,128)(2,1)} %bitcast.70), channel_id=1, source_target_pairs={{0,16},{16,0},{1,17},{17,1},{2,18},{18,2},{3,19},{19,3},{4,20},{20... | collective-permute-start | bytes 196616 | tf_op jit(solution)/shard_map/ppermute | solution.py:129
  7.0 8.5 %copy-start.5 = (f32[2048]{0:T(1024)S(1)}, f32[2048]{0:T(1024)}, u32[]{:S(2)}) copy-start(f32[2048]{0:T(1024)} %param.17) | copy-start | bytes 24580
  9.5 4.3 %collective-permute-start.2 = (bf16[32,1024]{1,0:T(8,128)(2,1)S(1)}, bf16[32,1024]{1,0:T(8,128)(2,1)S(1)}, u32[]{:S(2)}, u32[]{:S(2)}) collective-permute-start(bf16[32,1024]{1,0:T(8,128)(2,1)S(1)} %convolution_convert_fusion.1), channel_id=1, source_target_pairs={{0,16},{16,0},{1,17},{17,1},{2,18},{18,2},{3,19},{19,3},{4,20},{20... | collective-permute-start | bytes 196616 | tf_op jit(solution)/shard_map/ppermute | solution.py:129
  13.8 0.6 copy-start.3
  17.4 6.8 %copy-start.4 = (bf16[2048,8]{0,1:T(8,128)(2,1)S(1)}, bf16[2048,8]{0,1:T(8,128)(2,1)}, u32[]{:S(2)}) copy-start(bf16[2048,8]{0,1:T(8,128)(2,1)} %param.18) | copy-start | bytes 98308
  17.4 38.6 %all-to-all-start = ((bf16[16,24,2048]{2,1,0:T(8,128)(2,1)}), bf16[16,24,2048]{2,1,0:T(8,128)(2,1)}, u32[]{:S(2)}, u32[]{:S(2)}) async-start(bf16[16,24,2048]{2,1,0:T(8,128)(2,1)} %bitcast.61), calls=%async_computation | async-start | bytes 3145728 | tf_op jit(solution)/shard_map/all_to_all | solution.py:215
  24.4 66.7 %collective-permute-start.3 = (f32[32,8]{0,1:T(8,128)S(1)}, f32[32,8]{0,1:T(8,128)S(1)}, u32[]{:S(2)}, u32[]{:S(2)}) collective-permute-start(f32[32,8]{0,1:T(8,128)S(1)} %fusion.54), channel_id=1, source_target_pairs={{0,16},{16,0},{1,17},{17,1},{2,18},{18,2},{3,19},{19,3},{4,20},{20... | collective-permute-start | bytes 3080 | tf_op jit(solution)/shard_map/ppermute | solution.py:129
  55.9 4.1 %copy-start.7 = (bf16[1,704,2048]{2,1,0:T(8,128)(2,1)S(1)}, bf16[1,704,2048]{2,1,0:T(8,128)(2,1)}, u32[]{:S(2)}) copy-start(bf16[1,704,2048]{2,1,0:T(8,128)(2,1)} %param.22) | copy-start | bytes 8650756
  60.1 4.9 %copy-start.1 = (bf16[704,2048]{1,0:T(8,128)(2,1)S(1)}, bf16[704,2048]{1,0:T(8,128)(2,1)}, u32[]{:S(2)}) copy-start(bf16[704,2048]{1,0:T(8,128)(2,1)} %param.25) | copy-start | bytes 8650756
  63.4 15.2 %collective-permute-start.4 = (bf16[384,704]{0,1:T(8,128)(2,1)S(1)}, bf16[384,704]{0,1:T(8,128)(2,1)S(1)}, u32[]{:S(2)}, u32[]{:S(2)}) collective-permute-start(bf16[384,704]{0,1:T(8,128)(2,1)S(1)} %fusion.18), channel_id=1, source_target_pairs={{0,16},{16,0},{1,17},{17,1},{2,18},{18,2},{3,19},{19,3},{4,20},{20... | collective-permute-start | bytes 1622024 | tf_op jit(solution)/shard_map/ppermute | solution.py:129
  65.9 27.9 %collective-permute-start.5 = (bf16[32,704]{1,0:T(8,128)(2,1)S(1)}, bf16[32,704]{1,0:T(8,128)(2,1)S(1)}, u32[]{:S(2)}, u32[]{:S(2)}) collective-permute-start(bf16[32,704]{1,0:T(8,128)(2,1)S(1)} %fusion.25), channel_id=1, source_target_pairs={{0,16},{16,0},{1,17},{17,1},{2,18},{18,2},{3,19},{19,3},{4,20},{20... | collective-permute-start | bytes 135176 | tf_op jit(solution)/shard_map/ppermute | solution.py:129
  80.3 27.8 %all-to-all-start.1 = ((bf16[16,24,1024]{2,1,0:T(8,128)(2,1)}), bf16[16,24,1024]{2,1,0:T(8,128)(2,1)}, u32[]{:S(2)}, u32[]{:S(2)}) async-start(bf16[16,24,1024]{2,1,0:T(8,128)(2,1)} %bitcast.64), calls=%async_computation.1 | async-start | bytes 1572864 | tf_op jit(solution)/shard_map/all_to_all | solution.py:240
  93.7 20.2 %copy-start.6 = (f32[2048]{0:T(1024)S(1)}, f32[2048]{0:T(1024)}, u32[]{:S(2)}) copy-start(f32[2048]{0:T(1024)} %param.27) | copy-start | bytes 24580
  109.5 4.3 %collective-permute-start.6 = (f32[16,1024]{1,0:T(8,128)S(1)}, f32[16,1024]{1,0:T(8,128)S(1)}, u32[]{:S(2)}, u32[]{:S(2)}) collective-permute-start(f32[16,1024]{1,0:T(8,128)S(1)} %get-tuple-element.8), channel_id=1, source_target_pairs={{0,16},{16,0},{1,17},{17,1},{2,18},{18,2},{3,19},{19,3},{4,20},{20... | collective-permute-start | bytes 196616 | tf_op jit(solution)/shard_map/ppermute | solution.py:129

commit v5 on v4

--- a/solution.py
+++ b/solution.py
@@ -1,6 +1,8 @@
 import jax
 import jax.numpy as jnp
 from jax import lax
+from jax.experimental import pallas as pl
+from jax.experimental.pallas import tpu as pltpu
 from jax.sharding import PartitionSpec as P
 
 
@@ -125,6 +127,32 @@
     return (stream, normed)
 
 
+def gate_up_kernel(rows_ref, gate_ref, up_ref, hidden_ref):
+    rows = rows_ref[...]
+    contract = (((1,), (1,)), ((), ()))
+    gate_value = lax.dot_general(rows, gate_ref[...], contract, preferred_element_type=jnp.float32)
+    up_value = lax.dot_general(rows, up_ref[...], contract, preferred_element_type=jnp.float32)
+    silu = gate_value / (1.0 + jnp.exp(-gate_value))
+    hidden_ref[...] = (silu * up_value).astype(hidden_ref.dtype)
+
+
+def gate_up(rows, gate_weight, up_weight):
+    count, width = rows.shape
+    units = gate_weight.shape[0]
+    in_vmem = pl.BlockSpec(memory_space=pltpu.VMEM)
+    return pl.pallas_call(
+        gate_up_kernel,
+        out_shape=jax.ShapeDtypeStruct((count, units), jnp.bfloat16),
+        in_specs=[in_vmem, in_vmem, in_vmem],
+        out_specs=in_vmem,
+        cost_estimate=pl.CostEstimate(
+            flops=4 * count * width * units,
+            transcendentals=count * units,
+            bytes_accessed=2 * (count * width + 2 * units * width + count * units),
+        ),
+    )(rows, gate_weight, up_weight)
+
+
 def swap_pair(x):
     return lax.ppermute(x, "dp", [(0, 1), (1, 0)])
 
@@ -214,9 +242,7 @@
     ).astype(jnp.bfloat16).reshape(experts, groups * capacity, column.shape[1])
     slot_rows = lax.all_to_all(outgoing, "expert", split_axis=0, concat_axis=0, tiled=True)
     flattened = slot_rows.reshape(-1, slot_rows.shape[-1])
-    gate_value = by_rows(flattened, gate_local)
-    up_value = by_rows(flattened, up_local)
-    hidden = (jax.nn.silu(gate_value) * up_value).astype(jnp.bfloat16)
+    hidden = gate_up(flattened, gate_local, up_local)
     hidden_peer = swap_pair(hidden)
     shared_gate_value = by_rows(column, shared_gate)
     shared_up_value = by_rows(column, shared_up)

time: 115 us -> 117 us (1.017)
  Pallas kernels: 0 us -> 6.64 us
  matrix products: 22.3 us -> 16.8 us
  local copies, waits for them, and re-layouts: 5.49 us -> 7.57 us
  waiting for transfers between devices: 56.2 us -> 54.6 us
    pallas_call x0 -> x1, Pallas kernels: none -> 6.64 us  [gate_up(): pl.pallas_call(gate_up_kernel, out_shape=jax.ShapeDtypeStruct((count, uni...]
    dot_general x4 -> x2, matrix products: 11 us -> 5.44 us  [by_rows(): lax.dot_general(left, weight_rows, (((1,), (1,)), ((), ())), preferred_el...]
    pallas_call x0 -> x1, local copies, waits for them, and re-layouts: none -> 2.08 us  [gate_up(): pl.pallas_call(gate_up_kernel, out_shape=jax.ShapeDtypeStruct((count, uni...]
    ppermute x7, waiting for transfers between devices: 16.3 us -> 14.7 us  [swap_pair(): return lax.ppermute(x, 'dp', [(0, 1), (1, 0)])]
  transfers between devices with their start and end apart: 9 -> 9, of which waited for: 5 -> 5; matrix products, arithmetic and copies ran while one was open for 23% -> 19% of each run, Pallas kernels for 0% -> 6%
where the time goes in v5:
time: 117 us; the launch traced here: 116 us
  waiting for transfers between devices  54.6 us (47%)
  starting transfers between devices  25.7 us (22%)
  matrix products  16.8 us (14%)
  local copies, waits for them, and re-layouts  7.57 us (6%)
  Pallas kernels  6.64 us (6%)
  other arithmetic  3.82 us (3%)
    all_to_all x1, waiting for transfers between devices, shards_pair(): lax.all_to_all(outgoing, 'expert', split_axis=0, concat_axis=0, tiled=True)  27.3 us
    ppermute x7, waiting for transfers between devices, swap_pair(): return lax.ppermute(x, 'dp', [(0, 1), (1, 0)])  14.7 us
    all_to_all x1, waiting for transfers between devices, shards_pair(): lax.all_to_all(expert_out, 'expert', split_axis=0, concat_axis=0, tiled=T...  12.6 us
    ppermute x7, starting transfers between devices, swap_pair(): return lax.ppermute(x, 'dp', [(0, 1), (1, 0)])  10.3 us
    all_to_all x1, starting transfers between devices, shards_pair(): lax.all_to_all(expert_out, 'expert', split_axis=0, concat_axis=0, tiled=T...  9.01 us
    pallas_call x1, Pallas kernels, gate_up(): pl.pallas_call(gate_up_kernel, out_shape=jax.ShapeDtypeStruct((count, uni...  6.64 us
    all_to_all x1, starting transfers between devices, shards_pair(): lax.all_to_all(outgoing, 'expert', split_axis=0, concat_axis=0, tiled=True)  6.38 us
    dot_general x2, matrix products, by_rows(): lax.dot_general(left, weight_rows, (((1,), (1,)), ((), ())), preferred_el...  5.44 us
  transfers between devices with their start and end apart: 9, of which 5 were waited for; matrix products, arithmetic and copies ran while one was open for 19% of the time, Pallas kernels for 6%

profile of v5, /device:TPU:0, one launch (start us, length us, event | category | flops | bytes accessed | tf_op | source)
XLA Modules:
  0.0 116.0 jit_solution(2433512277133059006)
XLA Ops:
  0.7 3.0 %collective-permute-start.1 = (bf16[16,1024]{1,0:T(8,128)(2,1)}, bf16[16,1024]{1,0:T(8,128)(2,1)S(1)}, u32[]{:S(2)}, u32[]{:S(2)}) collective-permute-start(bf16[16,1024]{1,0:T(8,128)(2,1)} %bitcast.62), channel_id=1, source_target_pairs={{0,16},{16,0},{1,17},{17,1},{2,18},{18,2},{3,19},{19,3},{4,20},{20... | collective-permute-start | bytes 98312 | tf_op jit(solution)/shard_map/ppermute | solution.py:157
  7.4 2.1 %convolution_convert_fusion.1 = bf16[32,1024]{1,0:T(8,128)(2,1)S(1)} fusion(bf16[1024,1024]{1,0:T(8,128)(2,1)} %param.16, bf16[16,1024]{1,0:T(8,128)(2,1)S(1)} %collective-permute-done.1, bf16[16,1024]{1,0:T(8,128)(2,1)} %bitcast.63), kind=kOutput, calls=%fused_computation.18 | convolution fusion | flops 67272704 | bytes 2228224 | tf_op jit(solution)/shard_map/dot_general | solution.py:204
  9.5 2.0 %collective-permute-start.2 = (bf16[32,1024]{1,0:T(8,128)(2,1)S(1)}, bf16[32,1024]{1,0:T(8,128)(2,1)S(1)}, u32[]{:S(2)}, u32[]{:S(2)}) collective-permute-start(bf16[32,1024]{1,0:T(8,128)(2,1)S(1)} %convolution_convert_fusion.1), channel_id=1, source_target_pairs={{0,16},{16,0},{1,17},{17,1},{2,18},{18,2},{3,19},{19,3},{4,20},{20... | collective-permute-start | bytes 196616 | tf_op jit(solution)/shard_map/ppermute | solution.py:157
  11.6 2.2 %collective-permute-done.2 = bf16[32,1024]{1,0:T(8,128)(2,1)S(1)} collective-permute-done((bf16[32,1024]{1,0:T(8,128)(2,1)S(1)}, bf16[32,1024]{1,0:T(8,128)(2,1)S(1)}, u32[]{:S(2)}, u32[]{:S(2)}) %collective-permute-start.2) | collective-permute-done | bytes 65568 | tf_op jit(solution)/shard_map/ppermute | solution.py:157
  14.5 1.0 multiply_reduce_fusion
  15.6 1.8 %convolution_convert_fusion = bf16[384,2048]{1,0:T(8,128)(2,1)} fusion(pred[32,384]{1,0:T(8,128)(4,1)S(1)} %fusion.16, bf16[32,2048]{1,0:T(8,128)(2,1)S(1)} %multiply_convert_fusion), kind=kOutput, calls=%fused_computation.1 | convolution fusion | flops 51118080 | bytes 1716224 | tf_op jit(solution)/shard_map/dot_general | solution.py:240
  17.4 6.4 %all-to-all-start = ((bf16[16,24,2048]{2,1,0:T(8,128)(2,1)}), bf16[16,24,2048]{2,1,0:T(8,128)(2,1)}, u32[]{:S(2)}, u32[]{:S(2)}) async-start(bf16[16,24,2048]{2,1,0:T(8,128)(2,1)} %bitcast.51), calls=%async_computation | async-start | bytes 3145728 | tf_op jit(solution)/shard_map/all_to_all | solution.py:243
  24.2 1.5 %collective-permute-start.3 = (f32[32,8]{0,1:T(8,128)S(1)}, f32[32,8]{0,1:T(8,128)S(1)}, u32[]{:S(2)}, u32[]{:S(2)}) collective-permute-start(f32[32,8]{0,1:T(8,128)S(1)} %fusion.44), channel_id=1, source_target_pairs={{0,16},{16,0},{1,17},{17,1},{2,18},{18,2},{3,19},{19,3},{4,20},{20... | collective-permute-start | bytes 3080 | tf_op jit(solution)/shard_map/ppermute | solution.py:157
  25.8 2.7 %fusion.45 = f32[32,704]{1,0:T(8,128)S(1)} fusion(bf16[32,2048]{1,0:T(8,128)(2,1)S(1)} %multiply_convert_fusion, bf16[704,2048]{1,0:T(8,128)(2,1)} %param.24), kind=kOutput, calls=%fused_computation.75 | convolution fusion | flops 92274688 | bytes 3104768 | tf_op jit(solution)/shard_map/dot_general | solution.py:18
  28.5 27.3 %all-to-all-done = bf16[16,24,2048]{2,1,0:T(8,128)(2,1)} async-done(((bf16[16,24,2048]{2,1,0:T(8,128)(2,1)}), bf16[16,24,2048]{2,1,0:T(8,128)(2,1)}, u32[]{:S(2)}, u32[]{:S(2)}) %all-to-all-start) | async-done | bytes 1572896 | tf_op jit(solution)/shard_map/all_to_all | solution.py:243
  55.8 6.6 %shard_map.149 = bf16[384,704]{1,0:T(8,128)(2,1)} custom-call(bf16[384,2048]{1,0:T(8,128)(2,1)} %bitcast.7.rows_ref, bf16[704,2048]{1,0:T(8,128)(2,1)} %bitcast.65, bf16[704,2048]{1,0:T(8,128)(2,1)} %bitcast.66), custom_call_target="tpu_custom_call" | custom-call | flops 2214592512 | bytes 7880704 | tf_op jit(solution)/shard_map/pallas_call | solution.py:143
  62.5 2.1 %copy.37 = bf16[384,704]{0,1:T(8,128)(2,1)} copy(bf16[384,704]{1,0:T(8,128)(2,1)} %shard_map.149) | data formatting | bytes 1081344 | tf_op jit(solution)/shard_map/pallas_call | solution.py:143
  64.5 1.5 %collective-permute-start.4 = (bf16[384,704]{0,1:T(8,128)(2,1)}, bf16[384,704]{0,1:T(8,128)(2,1)S(1)}, u32[]{:S(2)}, u32[]{:S(2)}) collective-permute-start(bf16[384,704]{0,1:T(8,128)(2,1)} %copy.37), channel_id=1, source_target_pairs={{0,16},{16,0},{1,17},{17,1},{2,18},{18,2},{3,19},{19,3},{4,20},{20... | collective-permute-start | bytes 1622024 | tf_op jit(solution)/shard_map/ppermute | solution.py:157
  66.1 2.7 %fusion.15 = bf16[32,704]{1,0:T(8,128)(2,1)S(1)} fusion(bf16[32,2048]{1,0:T(8,128)(2,1)S(1)} %multiply_convert_fusion, bf16[704,2048]{1,0:T(8,128)(2,1)} %param.25, f32[32,704]{1,0:T(8,128)S(1)} %fusion.45), kind=kOutput, calls=%fused_computation.19 | convolution fusion | flops 92409856 | bytes 3149824 | tf_op jit(solution)/shard_map/dot_general | solution.py:18
  70.2 9.7 %collective-permute-done.4 = bf16[384,704]{0,1:T(8,128)(2,1)S(1)} collective-permute-done((bf16[384,704]{0,1:T(8,128)(2,1)}, bf16[384,704]{0,1:T(8,128)(2,1)S(1)}, u32[]{:S(2)}, u32[]{:S(2)}) %collective-permute-start.4) | collective-permute-done | bytes 540704 | tf_op jit(solution)/shard_map/ppermute | solution.py:157
  79.9 1.7 %add_convert_fusion = bf16[384,1024]{1,0:T(8,128)(2,1)} fusion(f32[384,1024]{1,0:T(8,128)S(1)} %fusion.5, bf16[384,704]{0,1:T(8,128)(2,1)S(1)} %collective-permute-done.4, bf16[2,704,1024]{2,1,0:T(8,128)(2,1)S(1)} %bitcast.50, s32[]{:T(128)S(6)} %select_n.121), kind=kOutput, calls=%fused_computation.2 | convolution fusion | flops 554434560 | bytes 4341764 | tf_op jit(solution)/shard_map/dot_general | solution.py:259
  81.6 9.0 %all-to-all-start.1 = ((bf16[16,24,1024]{2,1,0:T(8,128)(2,1)}), bf16[16,24,1024]{2,1,0:T(8,128)(2,1)}, u32[]{:S(2)}, u32[]{:S(2)}) async-start(bf16[16,24,1024]{2,1,0:T(8,128)(2,1)} %bitcast.54), calls=%async_computation.1 | async-start | bytes 1572864 | tf_op jit(solution)/shard_map/all_to_all | solution.py:266
  90.6 1.7 %fusion.2 = f32[32,1024]{1,0:T(8,128)S(1)} fusion(bf16[32,704]{1,0:T(8,128)(2,1)S(1)} %fusion.15, bf16[2,704,1024]{2,1,0:T(8,128)(2,1)} %bitcast.52, s32[]{:T(128)S(6)} %select_n.120), kind=kOutput, calls=%fused_computation.5 | convolution fusion | flops 46137344 | bytes 1617924 | tf_op jit(solution)/shard_map/dot_general | solution.py:262
  92.5 1.7 %gather_fusion = f32[192]{0:T(256)S(1)} fusion(f32[32,16]{0,1:T(8,128)S(1)} %maximum_select_fusion.2, s32[192]{0:T(256)S(1)} %reshape.219), kind=kCustom, calls=%fused_computation | custom fusion | bytes 3072 | tf_op jit(solution)/shard_map/jit(take_along_axis)/gather | solution.py:219
  95.1 1.7 %fusion.12 = f32[32,1024]{1,0:T(8,128)S(1)} fusion(f32[32,1024]{1,0:T(8,128)S(1)} %fusion.2, bf16[2,704,1024]{2,1,0:T(8,128)(2,1)} %bitcast.53, s32[]{:T(128)S(6)} %select_n.121, bf16[16,704]{1,0:T(8,128)(2,1)S(1)} %get-tuple-element.13, bf16[16,704]{1,0:T(8,128)(2,1)S(1)} %get-tuple-element.12), kind=kOutput, calls=%fused_computation.16 | convolution fusion | flops 46260224 | bytes 1748996 | tf_op jit(solution)/shard_map/dot_general | solution.py:262
  96.8 12.6 %all-to-all-done.1 = bf16[16,24,1024]{2,1,0:T(8,128)(2,1)} async-done(((bf16[16,24,1024]{2,1,0:T(8,128)(2,1)}), bf16[16,24,1024]{2,1,0:T(8,128)(2,1)}, u32[]{:S(2)}, u32[]{:S(2)}) %all-to-all-start.1) | async-done | bytes 786464 | tf_op jit(solution)/shard_map/all_to_all | solution.py:266
  109.4 1.4 %fusion.11 = f32[32,1024]{1,0:T(8,128)S(1)} fusion(f32[32,1024]{1,0:T(8,128)S(1)} %fusion.12, bf16[32,384]{1,0:T(8,128)(2,1)S(1)} %fusion.18, bf16[384,1024]{1,0:T(8,128)(2,1)} %bitcast.14, pred[32]{0:T(512)(128)(4,1)S(1)} %lt.63), kind=kOutput, calls=%fused_computation.15 | convolution fusion | flops 25231360 | bytes 1073184 | tf_op jit(solution)/shard_map/dot_general | solution.py:272
  110.8 1.6 %collective-permute-start.6 = (f32[16,1024]{1,0:T(8,128)S(1)}, f32[16,1024]{1,0:T(8,128)S(1)}, u32[]{:S(2)}, u32[]{:S(2)}) collective-permute-start(f32[16,1024]{1,0:T(8,128)S(1)} %get-tuple-element.8), channel_id=1, source_target_pairs={{0,16},{16,0},{1,17},{17,1},{2,18},{18,2},{3,19},{19,3},{4,20},{20... | collective-permute-start | bytes 196616 | tf_op jit(solution)/shard_map/ppermute | solution.py:157
  112.4 2.7 %collective-permute-done.6 = f32[16,1024]{1,0:T(8,128)S(1)} collective-permute-done((f32[16,1024]{1,0:T(8,128)S(1)}, f32[16,1024]{1,0:T(8,128)S(1)}, u32[]{:S(2)}, u32[]{:S(2)}) %collective-permute-start.6) | collective-permute-done | bytes 65568 | tf_op jit(solution)/shard_map/ppermute | solution.py:157
  (67 shorter events, 8.2 us)
Async XLA Ops:
  0.6 68.8 %copy-start = (bf16[1,1408,1024]{2,1,0:T(8,128)(2,1)S(1)}, bf16[1,1408,1024]{2,1,0:T(8,128)(2,1)}, u32[]{:S(2)}) copy-start(bf16[1,1408,1024]{2,1,0:T(8,128)(2,1)} %param.23) | copy-start | bytes 8650756
  0.6 13.8 %copy-start.2 = (bf16[1,1,16,2048]{3,2,1,0:T(8,128)(2,1)S(1)}, bf16[1,1,16,2048]{3,2,1,0:T(8,128)(2,1)}, u32[]{:S(2)}) copy-start(bf16[1,1,16,2048]{3,2,1,0:T(8,128)(2,1)} %param.15) | copy-start | bytes 196612
  0.7 14.9 %copy-start.5 = (f32[2048]{0:T(1024)S(1)}, f32[2048]{0:T(1024)}, u32[]{:S(2)}) copy-start(f32[2048]{0:T(1024)} %param.17) | copy-start | bytes 24580
  0.7 6.7 %collective-permute-start.1 = (bf16[16,1024]{1,0:T(8,128)(2,1)}, bf16[16,1024]{1,0:T(8,128)(2,1)S(1)}, u32[]{:S(2)}, u32[]{:S(2)}) collective-permute-start(bf16[16,1024]{1,0:T(8,128)(2,1)} %bitcast.62), channel_id=1, source_target_pairs={{0,16},{16,0},{1,17},{17,1},{2,18},{18,2},{3,19},{19,3},{4,20},{20... | collective-permute-start | bytes 98312 | tf_op jit(solution)/shard_map/ppermute | solution.py:157
  3.7 10.1 %collective-permute-start = (bf16[16,2048]{1,0:T(8,128)(2,1)}, bf16[16,2048]{1,0:T(8,128)(2,1)S(1)}, u32[]{:S(2)}, u32[]{:S(2)}) collective-permute-start(bf16[16,2048]{1,0:T(8,128)(2,1)} %bitcast.60), channel_id=1, source_target_pairs={{0,16},{16,0},{1,17},{17,1},{2,18},{18,2},{3,19},{19,3},{4,20},{20... | collective-permute-start | bytes 196616 | tf_op jit(solution)/shard_map/ppermute | solution.py:157
  9.5 4.3 %collective-permute-start.2 = (bf16[32,1024]{1,0:T(8,128)(2,1)S(1)}, bf16[32,1024]{1,0:T(8,128)(2,1)S(1)}, u32[]{:S(2)}, u32[]{:S(2)}) collective-permute-start(bf16[32,1024]{1,0:T(8,128)(2,1)S(1)} %convolution_convert_fusion.1), channel_id=1, source_target_pairs={{0,16},{16,0},{1,17},{17,1},{2,18},{18,2},{3,19},{19,3},{4,20},{20... | collective-permute-start | bytes 196616 | tf_op jit(solution)/shard_map/ppermute | solution.py:157
  13.8 0.6 copy-start.3
  14.5 9.6 %copy-start.4 = (bf16[2048,8]{0,1:T(8,128)(2,1)S(1)}, bf16[2048,8]{0,1:T(8,128)(2,1)}, u32[]{:S(2)}) copy-start(bf16[2048,8]{0,1:T(8,128)(2,1)} %param.18) | copy-start | bytes 98308
  17.4 38.4 %all-to-all-start = ((bf16[16,24,2048]{2,1,0:T(8,128)(2,1)}), bf16[16,24,2048]{2,1,0:T(8,128)(2,1)}, u32[]{:S(2)}, u32[]{:S(2)}) async-start(bf16[16,24,2048]{2,1,0:T(8,128)(2,1)} %bitcast.51), calls=%async_computation | async-start | bytes 3145728 | tf_op jit(solution)/shard_map/all_to_all | solution.py:243
  24.2 68.1 %collective-permute-start.3 = (f32[32,8]{0,1:T(8,128)S(1)}, f32[32,8]{0,1:T(8,128)S(1)}, u32[]{:S(2)}, u32[]{:S(2)}) collective-permute-start(f32[32,8]{0,1:T(8,128)S(1)} %fusion.44), channel_id=1, source_target_pairs={{0,16},{16,0},{1,17},{17,1},{2,18},{18,2},{3,19},{19,3},{4,20},{20... | collective-permute-start | bytes 3080 | tf_op jit(solution)/shard_map/ppermute | solution.py:157
  64.5 4.8 %copy-start.1 = (bf16[384,704]{1,0:T(8,128)(2,1)S(1)}, bf16[384,704]{1,0:T(8,128)(2,1)}, u32[]{:S(2)}) copy-start(bf16[384,704]{1,0:T(8,128)(2,1)} %shard_map.149) | copy-start | bytes 1622020
  64.5 15.4 %collective-permute-start.4 = (bf16[384,704]{0,1:T(8,128)(2,1)}, bf16[384,704]{0,1:T(8,128)(2,1)S(1)}, u32[]{:S(2)}, u32[]{:S(2)}) collective-permute-start(bf16[384,704]{0,1:T(8,128)(2,1)} %copy.37), channel_id=1, source_target_pairs={{0,16},{16,0},{1,17},{17,1},{2,18},{18,2},{3,19},{19,3},{4,20},{20... | collective-permute-start | bytes 1622024 | tf_op jit(solution)/shard_map/ppermute | solution.py:157
  68.8 26.3 %collective-permute-start.5 = (bf16[32,704]{1,0:T(8,128)(2,1)S(1)}, bf16[32,704]{1,0:T(8,128)(2,1)S(1)}, u32[]{:S(2)}, u32[]{:S(2)}) collective-permute-start(bf16[32,704]{1,0:T(8,128)(2,1)S(1)} %fusion.15), channel_id=1, source_target_pairs={{0,16},{16,0},{1,17},{17,1},{2,18},{18,2},{3,19},{19,3},{4,20},{20... | collective-permute-start | bytes 135176 | tf_op jit(solution)/shard_map/ppermute | solution.py:157
  81.6 27.8 %all-to-all-start.1 = ((bf16[16,24,1024]{2,1,0:T(8,128)(2,1)}), bf16[16,24,1024]{2,1,0:T(8,128)(2,1)}, u32[]{:S(2)}, u32[]{:S(2)}) async-start(bf16[16,24,1024]{2,1,0:T(8,128)(2,1)} %bitcast.54), calls=%async_computation.1 | async-start | bytes 1572864 | tf_op jit(solution)/shard_map/all_to_all | solution.py:266
  94.2 21.1 %copy-start.6 = (f32[2048]{0:T(1024)S(1)}, f32[2048]{0:T(1024)}, u32[]{:S(2)}) copy-start(f32[2048]{0:T(1024)} %param.27) | copy-start | bytes 24580
  110.8 4.3 %collective-permute-start.6 = (f32[16,1024]{1,0:T(8,128)S(1)}, f32[16,1024]{1,0:T(8,128)S(1)}, u32[]{:S(2)}, u32[]{:S(2)}) collective-permute-start(f32[16,1024]{1,0:T(8,128)S(1)} %get-tuple-element.8), channel_id=1, source_target_pairs={{0,16},{16,0},{1,17},{17,1},{2,18},{18,2},{3,19},{19,3},{4,20},{20... | collective-permute-start | bytes 196616 | tf_op jit(solution)/shard_map/ppermute | solution.py:157

commit v6 on v4

--- a/solution.py
+++ b/solution.py
@@ -171,10 +171,23 @@
 
     attention_mine = attention[0, 0]
     residual_mine = residual[0, 0]
-    pieces = jnp.concatenate([attention_mine, swap_pair(attention_mine)], axis=0)
+    attention_peer = swap_pair(attention_mine)
     residual_all = jnp.concatenate([residual_mine, swap_pair(residual_mine)], axis=0)
-    product = jnp.dot(pieces, out_proj, preferred_element_type=jnp.float32).astype(jnp.bfloat16)
-    projected = in_axis_order(first, product, halves_swapped(swap_pair(product)), 1)
+    product_mine = jnp.dot(attention_mine, out_proj, preferred_element_type=jnp.float32).astype(
+        jnp.bfloat16
+    )
+    from_peer_for_peer = swap_pair(product_mine)
+    product_peer = jnp.dot(attention_peer, out_proj, preferred_element_type=jnp.float32).astype(
+        jnp.bfloat16
+    )
+    from_peer_for_mine = swap_pair(product_peer)
+    projected = jnp.concatenate(
+        [
+            in_axis_order(first, product_mine, from_peer_for_mine, 1),
+            in_axis_order(first, product_peer, from_peer_for_peer, 1),
+        ],
+        axis=0,
+    )
     stream_all = residual_all.astype(jnp.float32) + projected.astype(jnp.float32)
     column = rms_scale(stream_all, gain_in).astype(jnp.bfloat16)
     stream_in = stream_all[:row_count]
@@ -243,9 +256,12 @@
     combine = jnp.sum(
         jnp.where(slot_hit, weights[:, :, None], jnp.zeros((), jnp.bfloat16)), axis=1
     ).astype(jnp.bfloat16)
-    routed = jnp.dot(combine, returned, preferred_element_type=jnp.float32)
-    combined = jnp.where(row_live[:, None], routed + shared, 0.0)
-    summed = in_axis_order(first, combined[:row_count], swap_pair(combined[row_count:]), 1)
+    routed_peer = jnp.dot(combine[row_count:], returned, preferred_element_type=jnp.float32)
+    combined_peer = jnp.where(row_live[row_count:, None], routed_peer + shared[row_count:], 0.0)
+    from_peer = swap_pair(combined_peer)
+    routed_mine = jnp.dot(combine[:row_count], returned, preferred_element_type=jnp.float32)
+    combined_mine = jnp.where(row_live[:row_count, None], routed_mine + shared[:row_count], 0.0)
+    summed = in_axis_order(first, combined_mine, from_peer, 1)
     stream_sum = stream_in + summed
     stream = stream_sum.astype(jnp.bfloat16)[None, None]
     normed = rms_scale(stream_sum, gain_out).astype(jnp.bfloat16)[None, None]

time: 115 us -> 115 us (level)
  matrix products: 22.3 us -> 25.6 us
  starting transfers between devices: 25.9 us -> 23.5 us
  waiting for transfers between devices: 56.2 us -> 58.3 us
  local copies, waits for them, and re-layouts: 5.49 us -> 3.53 us
  other arithmetic: 3.81 us -> 2.35 us
    dot_general x2 -> x4, matrix products: 3.44 us -> 6.68 us  [the longest x1 2 us: shards_pair(): jnp.dot(attention_mine, out_proj, preferred_element_type=jnp.float32)]
    ppermute x7 -> x8, starting transfers between devices: 10.4 us -> 8.57 us  [swap_pair(): return lax.ppermute(x, 'dp', [(0, 1), (1, 0)])]
    unnamed x17 -> x19, local copies, waits for them, and re-layouts: 1.44 us -> 0.13 us
    ppermute x7 -> x8, waiting for transfers between devices: 16.3 us -> 17.4 us  [swap_pair(): return lax.ppermute(x, 'dp', [(0, 1), (1, 0)])]
  transfers between devices with their start and end apart: 9 -> 10, of which waited for: 5 -> 5; matrix products, arithmetic and copies ran while one was open for 23% -> 24% of each run, Pallas kernels for 0% -> 0%
where the time goes in v6:
time: 115 us; the launch traced here: 114 us
  waiting for transfers between devices  58.3 us (51%)
  matrix products  25.6 us (22%)
  starting transfers between devices  23.5 us (20%)
  local copies, waits for them, and re-layouts  3.53 us (3%)
  other arithmetic  2.35 us (2%)
    all_to_all x1, waiting for transfers between devices, shards_pair(): lax.all_to_all(outgoing, 'expert', split_axis=0, concat_axis=0, tiled=True)  28.3 us
    ppermute x8, waiting for transfers between devices, swap_pair(): return lax.ppermute(x, 'dp', [(0, 1), (1, 0)])  17.4 us
    all_to_all x1, waiting for transfers between devices, shards_pair(): lax.all_to_all(expert_out, 'expert', split_axis=0, concat_axis=0, tiled=T...  12.6 us
    dot_general x4, matrix products, by_rows(): lax.dot_general(left, weight_rows, (((1,), (1,)), ((), ())), preferred_el...  11 us
    all_to_all x1, starting transfers between devices, shards_pair(): lax.all_to_all(expert_out, 'expert', split_axis=0, concat_axis=0, tiled=T...  9.01 us
    ppermute x8, starting transfers between devices, swap_pair(): return lax.ppermute(x, 'dp', [(0, 1), (1, 0)])  8.57 us
    all_to_all x1, starting transfers between devices, shards_pair(): lax.all_to_all(outgoing, 'expert', split_axis=0, concat_axis=0, tiled=True)  5.95 us
  transfers between devices with their start and end apart: 10, of which 5 were waited for; matrix products, arithmetic and copies ran while one was open for 24% of the time, Pallas kernels for 0%

profile of v6, /device:TPU:0, one launch (start us, length us, event | category | flops | bytes accessed | tf_op | source)
XLA Modules:
  0.0 114.1 jit_solution(1130054291945073072)
XLA Ops:
  0.7 3.0 %collective-permute-start.1 = (bf16[16,1024]{1,0:T(8,128)(2,1)}, bf16[16,1024]{1,0:T(8,128)(2,1)S(1)}, u32[]{:S(2)}, u32[]{:S(2)}) collective-permute-start(bf16[16,1024]{1,0:T(8,128)(2,1)} %bitcast.81), channel_id=1, source_target_pairs={{0,16},{16,0},{1,17},{17,1},{2,18},{18,2},{3,19},{19,3},{4,20},{20... | collective-permute-start | bytes 98312 | tf_op jit(solution)/shard_map/ppermute | solution.py:129
  3.7 2.0 %convolution_convert_fusion.2 = bf16[16,1024]{1,0:T(8,128)(2,1)S(1)} fusion(bf16[1024,1024]{1,0:T(8,128)(2,1)} %param.16, bf16[1,1,16,1024]{3,2,1,0:T(8,128)(2,1)} %param.14), kind=kOutput, calls=%fused_computation.24 | convolution fusion | flops 33570816 | bytes 2162688 | tf_op jit(solution)/shard_map/dot_general | solution.py:176
  5.9 1.9 %collective-permute-start = (bf16[16,2048]{1,0:T(8,128)(2,1)S(1)}, bf16[16,2048]{1,0:T(8,128)(2,1)S(1)}, u32[]{:S(2)}, u32[]{:S(2)}) collective-permute-start(bf16[16,2048]{1,0:T(8,128)(2,1)S(1)} %bitcast.73), channel_id=1, source_target_pairs={{0,16},{16,0},{1,17},{17,1},{2,18},{18,2},{3,19},{19,3},{4,20},{20... | collective-permute-start | bytes 196616 | tf_op jit(solution)/shard_map/ppermute | solution.py:129
  9.5 2.0 %convolution_convert_fusion.1 = bf16[16,1024]{1,0:T(8,128)(2,1)S(1)} fusion(bf16[16,1024]{1,0:T(8,128)(2,1)S(1)} %collective-permute-done.1, bf16[1024,1024]{1,0:T(8,128)(2,1)} %param.16), kind=kOutput, calls=%fused_computation.23 | convolution fusion | flops 33570816 | bytes 2162688 | tf_op jit(solution)/shard_map/dot_general | solution.py:180
  11.7 3.7 %collective-permute-done.2 = bf16[16,1024]{1,0:T(8,128)(2,1)S(1)} collective-permute-done((bf16[16,1024]{1,0:T(8,128)(2,1)S(1)}, bf16[16,1024]{1,0:T(8,128)(2,1)S(1)}, u32[]{:S(2)}, u32[]{:S(2)}) %collective-permute-start.2) | collective-permute-done | bytes 32800 | tf_op jit(solution)/shard_map/ppermute | solution.py:129
  15.7 1.8 %convolution_convert_fusion = bf16[384,2048]{1,0:T(8,128)(2,1)} fusion(pred[32,384]{1,0:T(8,128)(4,1)S(1)} %fusion.25, bf16[32,2048]{1,0:T(8,128)(2,1)S(1)} %multiply_convert_fusion), kind=kOutput, calls=%fused_computation.5 | convolution fusion | flops 51118080 | bytes 1716224 | tf_op jit(solution)/shard_map/dot_general | solution.py:225
  17.5 5.9 %all-to-all-start = ((bf16[16,24,2048]{2,1,0:T(8,128)(2,1)}), bf16[16,24,2048]{2,1,0:T(8,128)(2,1)}, u32[]{:S(2)}, u32[]{:S(2)}) async-start(bf16[16,24,2048]{2,1,0:T(8,128)(2,1)} %bitcast.69), calls=%async_computation | async-start | bytes 3145728 | tf_op jit(solution)/shard_map/all_to_all | solution.py:228
  24.5 2.7 %fusion.59 = f32[32,704]{1,0:T(8,128)S(1)} fusion(bf16[32,2048]{1,0:T(8,128)(2,1)S(1)} %multiply_convert_fusion, bf16[704,2048]{1,0:T(8,128)(2,1)} %param.24), kind=kOutput, calls=%fused_computation.86 | convolution fusion | flops 92274688 | bytes 3104768 | tf_op jit(solution)/shard_map/dot_general | solution.py:16
  27.2 28.3 %all-to-all-done = bf16[16,24,2048]{2,1,0:T(8,128)(2,1)} async-done(((bf16[16,24,2048]{2,1,0:T(8,128)(2,1)}), bf16[16,24,2048]{2,1,0:T(8,128)(2,1)}, u32[]{:S(2)}, u32[]{:S(2)}) %all-to-all-start) | async-done | bytes 1572896 | tf_op jit(solution)/shard_map/all_to_all | solution.py:228
  55.5 4.1 %fusion.2 = f32[384,704]{0,1:T(8,128)S(1)} fusion(bf16[384,2048]{1,0:T(8,128)(2,1)} %bitcast.8, bf16[1,704,2048]{2,1,0:T(8,128)(2,1)} %param.21), kind=kOutput, calls=%fused_computation.3 | convolution fusion | flops 1107296256 | bytes 5537792 | tf_op jit(solution)/shard_map/dot_general | solution.py:16
  59.6 3.3 %fusion.18 = bf16[384,704]{0,1:T(8,128)(2,1)S(1)} fusion(bf16[384,2048]{1,0:T(8,128)(2,1)} %bitcast.8, bf16[1,704,2048]{2,1,0:T(8,128)(2,1)S(1)} %copy-done.8, f32[384,704]{0,1:T(8,128)S(1)} %fusion.2), kind=kOutput, calls=%fused_computation.19 | convolution fusion | flops 1108918272 | bytes 6078464 | tf_op jit(solution)/shard_map/dot_general | solution.py:16
  63.5 0.9 fusion.24
  64.5 1.5 %collective-permute-start.6 = (bf16[32,704]{1,0:T(8,128)(2,1)S(1)}, bf16[32,704]{1,0:T(8,128)(2,1)S(1)}, u32[]{:S(2)}, u32[]{:S(2)}) collective-permute-start(bf16[32,704]{1,0:T(8,128)(2,1)S(1)} %fusion.24), channel_id=1, source_target_pairs={{0,16},{16,0},{1,17},{17,1},{2,18},{18,2},{3,19},{19,3},{4,20},{20... | collective-permute-start | bytes 135176 | tf_op jit(solution)/shard_map/ppermute | solution.py:129
  66.0 0.8 fusion.9
  66.8 11.3 %collective-permute-done.5 = bf16[384,704]{0,1:T(8,128)(2,1)S(1)} collective-permute-done((bf16[384,704]{0,1:T(8,128)(2,1)S(1)}, bf16[384,704]{0,1:T(8,128)(2,1)S(1)}, u32[]{:S(2)}, u32[]{:S(2)}) %collective-permute-start.5) | collective-permute-done | bytes 540704 | tf_op jit(solution)/shard_map/ppermute | solution.py:129
  78.1 1.7 %add_convert_fusion = bf16[384,1024]{1,0:T(8,128)(2,1)} fusion(f32[384,1024]{1,0:T(8,128)S(1)} %fusion.9, bf16[384,704]{0,1:T(8,128)(2,1)S(1)} %collective-permute-done.5, bf16[2,704,1024]{2,1,0:T(8,128)(2,1)S(1)} %bitcast.68, s32[]{:T(128)S(6)} %select_n.126), kind=kOutput, calls=%fused_computation.6 | convolution fusion | flops 554434560 | bytes 4341764 | tf_op jit(solution)/shard_map/dot_general | solution.py:246
  79.8 9.0 %all-to-all-start.1 = ((bf16[16,24,1024]{2,1,0:T(8,128)(2,1)}), bf16[16,24,1024]{2,1,0:T(8,128)(2,1)}, u32[]{:S(2)}, u32[]{:S(2)}) async-start(bf16[16,24,1024]{2,1,0:T(8,128)(2,1)} %bitcast.72), calls=%async_computation.1 | async-start | bytes 1572864 | tf_op jit(solution)/shard_map/all_to_all | solution.py:253
  88.9 1.7 %fusion.6 = f32[32,1024]{1,0:T(8,128)S(1)} fusion(bf16[32,704]{1,0:T(8,128)(2,1)S(1)} %fusion.24, bf16[2,704,1024]{2,1,0:T(8,128)(2,1)} %bitcast.70, s32[]{:T(128)S(6)} %select_n.125), kind=kOutput, calls=%fused_computation.9 | convolution fusion | flops 46137344 | bytes 1617924 | tf_op jit(solution)/shard_map/dot_general | solution.py:249
  90.7 1.7 %gather_fusion = f32[192]{0:T(256)S(1)} fusion(f32[32,16]{0,1:T(8,128)S(1)} %maximum_select_fusion.3, s32[192]{0:T(256)S(1)} %reshape.226), kind=kCustom, calls=%fused_computation | custom fusion | bytes 3072 | tf_op jit(solution)/shard_map/jit(take_along_axis)/gather | solution.py:204
  93.3 1.7 %fusion.21 = f32[32,1024]{1,0:T(8,128)S(1)} fusion(f32[32,1024]{1,0:T(8,128)S(1)} %fusion.6, bf16[2,704,1024]{2,1,0:T(8,128)(2,1)} %bitcast.71, s32[]{:T(128)S(6)} %select_n.126, bf16[16,704]{1,0:T(8,128)(2,1)S(1)} %get-tuple-element.9, bf16[16,704]{1,0:T(8,128)(2,1)S(1)} %get-tuple-element.8), kind=kOutput, calls=%fused_computation.20 | convolution fusion | flops 46260224 | bytes 1748996 | tf_op jit(solution)/shard_map/dot_general | solution.py:249
  95.0 12.6 %all-to-all-done.1 = bf16[16,24,1024]{2,1,0:T(8,128)(2,1)} async-done(((bf16[16,24,1024]{2,1,0:T(8,128)(2,1)}), bf16[16,24,1024]{2,1,0:T(8,128)(2,1)}, u32[]{:S(2)}, u32[]{:S(2)}) %all-to-all-start.1) | async-done | bytes 786464 | tf_op jit(solution)/shard_map/all_to_all | solution.py:253
  107.6 1.4 %fusion.31 = f32[16,1024]{1,0:T(8,128)S(1)} fusion(f32[32,1024]{1,0:T(8,128)S(1)} %fusion.21, pred[16]{0:T(512)(128)(4,1)S(1)} %get-tuple-element.12, bf16[384,1024]{1,0:T(8,128)(2,1)} %bitcast.15, bf16[32,384]{1,0:T(8,128)(2,1)S(1)} %fusion.27), kind=kOutput, calls=%fused_computation.42 | convolution fusion | flops 12615680 | bytes 930304 | tf_op jit(solution)/shard_map/dot_general | solution.py:259
  109.6 1.4 %fusion.32 = f32[16,1024]{1,0:T(8,128)S(1)} fusion(f32[32,1024]{1,0:T(8,128)S(1)} %fusion.21, pred[16]{0:T(512)(128)(4,1)S(1)} %get-tuple-element.13, bf16[384,1024]{1,0:T(8,128)(2,1)} %bitcast.15, bf16[32,384]{1,0:T(8,128)(2,1)S(1)} %fusion.27), kind=kOutput, calls=%fused_computation.44 | convolution fusion | flops 12615680 | bytes 930304 | tf_op jit(solution)/shard_map/dot_general | solution.py:262
  110.9 2.4 %collective-permute-done.7 = f32[16,1024]{1,0:T(8,128)S(1)} collective-permute-done((f32[16,1024]{1,0:T(8,128)S(1)}, f32[16,1024]{1,0:T(8,128)S(1)}, u32[]{:S(2)}, u32[]{:S(2)}) %collective-permute-start.7) | collective-permute-done | bytes 65568 | tf_op jit(solution)/shard_map/ppermute | solution.py:129
  (76 shorter events, 6.5 us)
Async XLA Ops:
  0.6 65.4 %copy-start = (bf16[1,1408,1024]{2,1,0:T(8,128)(2,1)S(1)}, bf16[1,1408,1024]{2,1,0:T(8,128)(2,1)}, u32[]{:S(2)}) copy-start(bf16[1,1408,1024]{2,1,0:T(8,128)(2,1)} %param.23) | copy-start | bytes 8650756
  0.6 5.2 %copy-start.2 = (bf16[1,1,16,2048]{3,2,1,0:T(8,128)(2,1)S(1)}, bf16[1,1,16,2048]{3,2,1,0:T(8,128)(2,1)}, u32[]{:S(2)}) copy-start(bf16[1,1,16,2048]{3,2,1,0:T(8,128)(2,1)} %param.15) | copy-start | bytes 196612
  0.7 7.1 %copy-start.6 = (s32[1,2,16,6]{2,1,3,0:T(2,128)S(1)}, s32[1,2,16,6]{2,1,3,0:T(2,128)}, u32[]{:S(2)}) copy-start(s32[1,2,16,6]{2,1,3,0:T(2,128)} %param.19) | copy-start | bytes 2308
  0.7 7.4 %copy-start.7 = (s32[2,1]{0,1:T(1,128)S(1)}, s32[2,1]{0,1:T(1,128)}, u32[]{:S(2)}) copy-start(s32[2,1]{0,1:T(1,128)} %param.20) | copy-start | bytes 28
  0.7 8.8 %collective-permute-start.1 = (bf16[16,1024]{1,0:T(8,128)(2,1)}, bf16[16,1024]{1,0:T(8,128)(2,1)S(1)}, u32[]{:S(2)}, u32[]{:S(2)}) collective-permute-start(bf16[16,1024]{1,0:T(8,128)(2,1)} %bitcast.81), channel_id=1, source_target_pairs={{0,16},{16,0},{1,17},{17,1},{2,18},{18,2},{3,19},{19,3},{4,20},{20... | collective-permute-start | bytes 98312 | tf_op jit(solution)/shard_map/ppermute | solution.py:129
  5.7 9.9 %copy-start.4 = (f32[2048]{0:T(1024)S(1)}, f32[2048]{0:T(1024)}, u32[]{:S(2)}) copy-start(f32[2048]{0:T(1024)} %param.17) | copy-start | bytes 24580
  5.7 6.0 %collective-permute-start.3 = (bf16[16,1024]{1,0:T(8,128)(2,1)S(1)}, bf16[16,1024]{1,0:T(8,128)(2,1)S(1)}, u32[]{:S(2)}, u32[]{:S(2)}) collective-permute-start(bf16[16,1024]{1,0:T(8,128)(2,1)S(1)} %convolution_convert_fusion.2), channel_id=1, source_target_pairs={{0,16},{16,0},{1,17},{17,1},{2,18},{18,2},{3,19},{19,3},{4,20},{20... | collective-permute-start | bytes 98312 | tf_op jit(solution)/shard_map/ppermute | solution.py:129
  5.9 9.6 %collective-permute-start = (bf16[16,2048]{1,0:T(8,128)(2,1)S(1)}, bf16[16,2048]{1,0:T(8,128)(2,1)S(1)}, u32[]{:S(2)}, u32[]{:S(2)}) collective-permute-start(bf16[16,2048]{1,0:T(8,128)(2,1)S(1)} %bitcast.73), channel_id=1, source_target_pairs={{0,16},{16,0},{1,17},{17,1},{2,18},{18,2},{3,19},{19,3},{4,20},{20... | collective-permute-start | bytes 196616 | tf_op jit(solution)/shard_map/ppermute | solution.py:129
  11.5 3.9 %collective-permute-start.2 = (bf16[16,1024]{1,0:T(8,128)(2,1)S(1)}, bf16[16,1024]{1,0:T(8,128)(2,1)S(1)}, u32[]{:S(2)}, u32[]{:S(2)}) collective-permute-start(bf16[16,1024]{1,0:T(8,128)(2,1)S(1)} %convolution_convert_fusion.1), channel_id=1, source_target_pairs={{0,16},{16,0},{1,17},{17,1},{2,18},{18,2},{3,19},{19,3},{4,20},{20... | collective-permute-start | bytes 98312 | tf_op jit(solution)/shard_map/ppermute | solution.py:129
  15.7 8.1 %copy-start.3 = (bf16[2048,8]{0,1:T(8,128)(2,1)S(1)}, bf16[2048,8]{0,1:T(8,128)(2,1)}, u32[]{:S(2)}) copy-start(bf16[2048,8]{0,1:T(8,128)(2,1)} %param.18) | copy-start | bytes 98308
  17.5 38.0 %all-to-all-start = ((bf16[16,24,2048]{2,1,0:T(8,128)(2,1)}), bf16[16,24,2048]{2,1,0:T(8,128)(2,1)}, u32[]{:S(2)}, u32[]{:S(2)}) async-start(bf16[16,24,2048]{2,1,0:T(8,128)(2,1)} %bitcast.69), calls=%async_computation | async-start | bytes 3145728 | tf_op jit(solution)/shard_map/all_to_all | solution.py:228
  23.9 66.7 %collective-permute-start.4 = (f32[32,8]{0,1:T(8,128)S(1)}, f32[32,8]{0,1:T(8,128)S(1)}, u32[]{:S(2)}, u32[]{:S(2)}) collective-permute-start(f32[32,8]{0,1:T(8,128)S(1)} %fusion.58), channel_id=1, source_target_pairs={{0,16},{16,0},{1,17},{17,1},{2,18},{18,2},{3,19},{19,3},{4,20},{20... | collective-permute-start | bytes 3080 | tf_op jit(solution)/shard_map/ppermute | solution.py:129
  55.5 4.1 %copy-start.8 = (bf16[1,704,2048]{2,1,0:T(8,128)(2,1)S(1)}, bf16[1,704,2048]{2,1,0:T(8,128)(2,1)}, u32[]{:S(2)}) copy-start(bf16[1,704,2048]{2,1,0:T(8,128)(2,1)} %param.22) | copy-start | bytes 8650756
  59.6 3.9 %copy-start.1 = (bf16[704,2048]{1,0:T(8,128)(2,1)S(1)}, bf16[704,2048]{1,0:T(8,128)(2,1)}, u32[]{:S(2)}) copy-start(bf16[704,2048]{1,0:T(8,128)(2,1)} %param.25) | copy-start | bytes 8650756
  62.9 15.2 %collective-permute-start.5 = (bf16[384,704]{0,1:T(8,128)(2,1)S(1)}, bf16[384,704]{0,1:T(8,128)(2,1)S(1)}, u32[]{:S(2)}, u32[]{:S(2)}) collective-permute-start(bf16[384,704]{0,1:T(8,128)(2,1)S(1)} %fusion.18), channel_id=1, source_target_pairs={{0,16},{16,0},{1,17},{17,1},{2,18},{18,2},{3,19},{19,3},{4,20},{20... | collective-permute-start | bytes 1622024 | tf_op jit(solution)/shard_map/ppermute | solution.py:129
  64.5 28.8 %collective-permute-start.6 = (bf16[32,704]{1,0:T(8,128)(2,1)S(1)}, bf16[32,704]{1,0:T(8,128)(2,1)S(1)}, u32[]{:S(2)}, u32[]{:S(2)}) collective-permute-start(bf16[32,704]{1,0:T(8,128)(2,1)S(1)} %fusion.24), channel_id=1, source_target_pairs={{0,16},{16,0},{1,17},{17,1},{2,18},{18,2},{3,19},{19,3},{4,20},{20... | collective-permute-start | bytes 135176 | tf_op jit(solution)/shard_map/ppermute | solution.py:129
  79.8 27.8 %all-to-all-start.1 = ((bf16[16,24,1024]{2,1,0:T(8,128)(2,1)}), bf16[16,24,1024]{2,1,0:T(8,128)(2,1)}, u32[]{:S(2)}, u32[]{:S(2)}) async-start(bf16[16,24,1024]{2,1,0:T(8,128)(2,1)} %bitcast.72), calls=%async_computation.1 | async-start | bytes 1572864 | tf_op jit(solution)/shard_map/all_to_all | solution.py:253
  93.0 20.5 %copy-start.5 = (f32[2048]{0:T(1024)S(1)}, f32[2048]{0:T(1024)}, u32[]{:S(2)}) copy-start(f32[2048]{0:T(1024)} %param.27) | copy-start | bytes 24580
  109.0 4.3 %collective-permute-start.7 = (f32[16,1024]{1,0:T(8,128)S(1)}, f32[16,1024]{1,0:T(8,128)S(1)}, u32[]{:S(2)}, u32[]{:S(2)}) collective-permute-start(f32[16,1024]{1,0:T(8,128)S(1)} %fusion.31), channel_id=1, source_target_pairs={{0,16},{16,0},{1,17},{17,1},{2,18},{18,2},{3,19},{19,3},{4,20},{20... | collective-permute-start | bytes 196616 | tf_op jit(solution)/shard_map/ppermute | solution.py:129

commit v7 on v5

--- a/solution.py
+++ b/solution.py
@@ -130,21 +130,27 @@
 def gate_up_kernel(rows_ref, gate_ref, up_ref, hidden_ref):
     rows = rows_ref[...]
     contract = (((1,), (1,)), ((), ()))
-    gate_value = lax.dot_general(rows, gate_ref[...], contract, preferred_element_type=jnp.float32)
-    up_value = lax.dot_general(rows, up_ref[...], contract, preferred_element_type=jnp.float32)
+    gate_value = lax.dot_general(gate_ref[...], rows, contract, preferred_element_type=jnp.float32)
+    up_value = lax.dot_general(up_ref[...], rows, contract, preferred_element_type=jnp.float32)
     silu = gate_value / (1.0 + jnp.exp(-gate_value))
     hidden_ref[...] = (silu * up_value).astype(hidden_ref.dtype)
 
 
-def gate_up(rows, gate_weight, up_weight):
+def gate_up_transposed(rows, gate_weight, up_weight):
     count, width = rows.shape
     units = gate_weight.shape[0]
-    in_vmem = pl.BlockSpec(memory_space=pltpu.VMEM)
+    tile = units // 4 if units % 64 == 0 else units
     return pl.pallas_call(
         gate_up_kernel,
-        out_shape=jax.ShapeDtypeStruct((count, units), jnp.bfloat16),
-        in_specs=[in_vmem, in_vmem, in_vmem],
-        out_specs=in_vmem,
+        out_shape=jax.ShapeDtypeStruct((units, count), jnp.bfloat16),
+        grid=(units // tile,),
+        in_specs=[
+            pl.BlockSpec((count, width), lambda i: (0, 0)),
+            pl.BlockSpec((tile, width), lambda i: (i, 0)),
+            pl.BlockSpec((tile, width), lambda i: (i, 0)),
+        ],
+        out_specs=pl.BlockSpec((tile, count), lambda i: (i, 0)),
+        compiler_params=pltpu.CompilerParams(vmem_limit_bytes=48 * 1024 * 1024),
         cost_estimate=pl.CostEstimate(
             flops=4 * count * width * units,
             transcendentals=count * units,
@@ -242,23 +248,24 @@
     ).astype(jnp.bfloat16).reshape(experts, groups * capacity, column.shape[1])
     slot_rows = lax.all_to_all(outgoing, "expert", split_axis=0, concat_axis=0, tiled=True)
     flattened = slot_rows.reshape(-1, slot_rows.shape[-1])
-    hidden = gate_up(flattened, gate_local, up_local)
-    hidden_peer = swap_pair(hidden)
+    hidden_t = gate_up_transposed(flattened, gate_local, up_local)
+    hidden_peer_t = swap_pair(hidden_t)
     shared_gate_value = by_rows(column, shared_gate)
     shared_up_value = by_rows(column, shared_up)
     shared_hidden = (jax.nn.silu(shared_gate_value) * shared_up_value).astype(jnp.bfloat16)
     shared_peer = halves_swapped(swap_pair(shared_hidden))
 
-    unit_count = hidden.shape[1]
+    unit_count = hidden_t.shape[0]
     down_blocks = down_local.reshape(groups, unit_count, column_width)
     shared_blocks = shared_down.reshape(groups, unit_count, column_width)
     down_mine = lax.dynamic_index_in_dim(down_blocks, me, 0, keepdims=False)
     down_peer = lax.dynamic_index_in_dim(down_blocks, 1 - me, 0, keepdims=False)
     shared_mine = lax.dynamic_index_in_dim(shared_blocks, me, 0, keepdims=False)
     shared_other = lax.dynamic_index_in_dim(shared_blocks, 1 - me, 0, keepdims=False)
-    routed_total = jnp.dot(hidden, down_mine, preferred_element_type=jnp.float32) + jnp.dot(
-        hidden_peer, down_peer, preferred_element_type=jnp.float32
-    )
+    by_units = (((0,), (0,)), ((), ()))
+    routed_total = lax.dot_general(
+        hidden_t, down_mine, by_units, preferred_element_type=jnp.float32
+    ) + lax.dot_general(hidden_peer_t, down_peer, by_units, preferred_element_type=jnp.float32)
     shared = jnp.dot(shared_hidden, shared_mine, preferred_element_type=jnp.float32) + jnp.dot(
         shared_peer, shared_other, preferred_element_type=jnp.float32
     )

time: 117 us -> 116 us (level)
  matrix products: 16.8 us -> 14.9 us
  waiting for transfers between devices: 54.6 us -> 56.2 us
    pallas_call x1 -> x0, local copies, waits for them, and re-layouts: 2.08 us -> none  [gate_up(): pl.pallas_call(gate_up_kernel, out_shape=jax.ShapeDtypeStruct((count, uni...]
    unnamed x15 -> x17, local copies, waits for them, and re-layouts: 1.43 us -> 3.25 us
    dot_general x2, matrix products: 5.44 us -> 3.63 us  [by_rows(): lax.dot_general(left, weight_rows, (((1,), (1,)), ((), ())), preferred_el...]
    ppermute x7, waiting for transfers between devices: 14.7 us -> 16.3 us  [swap_pair(): return lax.ppermute(x, 'dp', [(0, 1), (1, 0)])]
  transfers between devices with their start and end apart: 9 -> 9, of which waited for: 5 -> 5; matrix products, arithmetic and copies ran while one was open for 19% -> 16% of each run, Pallas kernels for 6% -> 5%
where the time goes in v7:
time: 116 us; the launch traced here: 115 us
  waiting for transfers between devices  56.2 us (48%)
  starting transfers between devices  25.8 us (22%)
  matrix products  14.9 us (13%)
  local copies, waits for them, and re-layouts  7.3 us (6%)
  Pallas kernels  6.3 us (5%)
  other arithmetic  3.82 us (3%)
    all_to_all x1, waiting for transfers between devices, shards_pair(): lax.all_to_all(outgoing, 'expert', split_axis=0, concat_axis=0, tiled=True)  27.3 us
    ppermute x7, waiting for transfers between devices, swap_pair(): return lax.ppermute(x, 'dp', [(0, 1), (1, 0)])  16.3 us
    all_to_all x1, waiting for transfers between devices, shards_pair(): lax.all_to_all(expert_out, 'expert', split_axis=0, concat_axis=0, tiled=T...  12.6 us
    ppermute x7, starting transfers between devices, swap_pair(): return lax.ppermute(x, 'dp', [(0, 1), (1, 0)])  10.4 us
    all_to_all x1, starting transfers between devices, shards_pair(): lax.all_to_all(expert_out, 'expert', split_axis=0, concat_axis=0, tiled=T...  9.01 us
    all_to_all x1, starting transfers between devices, shards_pair(): lax.all_to_all(outgoing, 'expert', split_axis=0, concat_axis=0, tiled=True)  6.38 us
    pallas_call x1, Pallas kernels, gate_up_transposed(): pl.pallas_call(gate_up_kernel, out_shape=jax.ShapeDtypeStruct((units, cou...  6.3 us
    dot_general x2, matrix products, by_rows(): lax.dot_general(left, weight_rows, (((1,), (1,)), ((), ())), preferred_el...  3.63 us
  transfers between devices with their start and end apart: 9, of which 5 were waited for; matrix products, arithmetic and copies ran while one was open for 16% of the time, Pallas kernels for 5%

profile of v7, /device:TPU:0, one launch (start us, length us, event | category | flops | bytes accessed | tf_op | source)
XLA Modules:
  0.0 115.2 jit_solution(2944885500538010961)
XLA Ops:
  0.7 3.0 %collective-permute-start.1 = (bf16[16,1024]{1,0:T(8,128)(2,1)}, bf16[16,1024]{1,0:T(8,128)(2,1)S(1)}, u32[]{:S(2)}, u32[]{:S(2)}) collective-permute-start(bf16[16,1024]{1,0:T(8,128)(2,1)} %bitcast.63), channel_id=1, source_target_pairs={{0,16},{16,0},{1,17},{17,1},{2,18},{18,2},{3,19},{19,3},{4,20},{20... | collective-permute-start | bytes 98312 | tf_op jit(solution)/shard_map/ppermute | solution.py:163
  7.4 2.1 %convolution_convert_fusion.1 = bf16[32,1024]{1,0:T(8,128)(2,1)S(1)} fusion(bf16[1024,1024]{1,0:T(8,128)(2,1)} %param.16, bf16[16,1024]{1,0:T(8,128)(2,1)S(1)} %collective-permute-done.1, bf16[16,1024]{1,0:T(8,128)(2,1)} %bitcast.64), kind=kOutput, calls=%fused_computation.18 | convolution fusion | flops 67272704 | bytes 2228224 | tf_op jit(solution)/shard_map/dot_general | solution.py:210
  9.5 2.0 %collective-permute-start.2 = (bf16[32,1024]{1,0:T(8,128)(2,1)S(1)}, bf16[32,1024]{1,0:T(8,128)(2,1)S(1)}, u32[]{:S(2)}, u32[]{:S(2)}) collective-permute-start(bf16[32,1024]{1,0:T(8,128)(2,1)S(1)} %convolution_convert_fusion.1), channel_id=1, source_target_pairs={{0,16},{16,0},{1,17},{17,1},{2,18},{18,2},{3,19},{19,3},{4,20},{20... | collective-permute-start | bytes 196616 | tf_op jit(solution)/shard_map/ppermute | solution.py:163
  11.6 2.2 %collective-permute-done.2 = bf16[32,1024]{1,0:T(8,128)(2,1)S(1)} collective-permute-done((bf16[32,1024]{1,0:T(8,128)(2,1)S(1)}, bf16[32,1024]{1,0:T(8,128)(2,1)S(1)}, u32[]{:S(2)}, u32[]{:S(2)}) %collective-permute-start.2) | collective-permute-done | bytes 65568 | tf_op jit(solution)/shard_map/ppermute | solution.py:163
  14.5 1.0 multiply_reduce_fusion
  15.6 1.8 %convolution_convert_fusion = bf16[384,2048]{1,0:T(8,128)(2,1)} fusion(pred[32,384]{1,0:T(8,128)(4,1)S(1)} %fusion.16, bf16[32,2048]{1,0:T(8,128)(2,1)S(1)} %multiply_convert_fusion), kind=kOutput, calls=%fused_computation.1 | convolution fusion | flops 51118080 | bytes 1716224 | tf_op jit(solution)/shard_map/dot_general | solution.py:246
  17.4 6.4 %all-to-all-start = ((bf16[16,24,2048]{2,1,0:T(8,128)(2,1)}), bf16[16,24,2048]{2,1,0:T(8,128)(2,1)}, u32[]{:S(2)}, u32[]{:S(2)}) async-start(bf16[16,24,2048]{2,1,0:T(8,128)(2,1)} %bitcast.52), calls=%async_computation | async-start | bytes 3145728 | tf_op jit(solution)/shard_map/all_to_all | solution.py:249
  24.2 1.5 %collective-permute-start.3 = (f32[32,8]{0,1:T(8,128)S(1)}, f32[32,8]{0,1:T(8,128)S(1)}, u32[]{:S(2)}, u32[]{:S(2)}) collective-permute-start(f32[32,8]{0,1:T(8,128)S(1)} %fusion.44), channel_id=1, source_target_pairs={{0,16},{16,0},{1,17},{17,1},{2,18},{18,2},{3,19},{19,3},{4,20},{20... | collective-permute-start | bytes 3080 | tf_op jit(solution)/shard_map/ppermute | solution.py:163
  25.8 2.7 %fusion.45 = f32[32,704]{1,0:T(8,128)S(1)} fusion(bf16[32,2048]{1,0:T(8,128)(2,1)S(1)} %multiply_convert_fusion, bf16[704,2048]{1,0:T(8,128)(2,1)} %param.24), kind=kOutput, calls=%fused_computation.75 | convolution fusion | flops 92274688 | bytes 3104768 | tf_op jit(solution)/shard_map/dot_general | solution.py:18
  28.5 27.3 %all-to-all-done = bf16[16,24,2048]{2,1,0:T(8,128)(2,1)} async-done(((bf16[16,24,2048]{2,1,0:T(8,128)(2,1)}), bf16[16,24,2048]{2,1,0:T(8,128)(2,1)}, u32[]{:S(2)}, u32[]{:S(2)}) %all-to-all-start) | async-done | bytes 1572896 | tf_op jit(solution)/shard_map/all_to_all | solution.py:249
  55.8 1.8 %copy-done.1 = bf16[1,704,2048]{2,1,0:T(8,128)(2,1)S(1)} copy-done((bf16[1,704,2048]{2,1,0:T(8,128)(2,1)S(1)}, bf16[1,704,2048]{2,1,0:T(8,128)(2,1)}, u32[]{:S(2)}) %copy-start.1) | copy-done | bytes 2883608
  57.6 6.3 %shard_map.149 = bf16[704,384]{1,0:T(8,128)(2,1)S(1)} custom-call(bf16[384,2048]{1,0:T(8,128)(2,1)} %bitcast.7.rows_ref, bf16[704,2048]{1,0:T(8,128)(2,1)S(1)} %bitcast.51, bf16[704,2048]{1,0:T(8,128)(2,1)} %bitcast.66), custom_call_target="tpu_custom_call" | custom-call | flops 2214592512 | bytes 7880704 | tf_op jit(solution)/shard_map/pallas_call | solution.py:143
  63.9 1.6 %collective-permute-start.4 = (bf16[704,384]{1,0:T(8,128)(2,1)S(1)}, bf16[704,384]{1,0:T(8,128)(2,1)S(1)}, u32[]{:S(2)}, u32[]{:S(2)}) collective-permute-start(bf16[704,384]{1,0:T(8,128)(2,1)S(1)} %shard_map.149), channel_id=1, source_target_pairs={{0,16},{16,0},{1,17},{17,1},{2,18},{18,2},{3,19},{19,3},{4,20},{20... | collective-permute-start | bytes 1622024 | tf_op jit(solution)/shard_map/ppermute | solution.py:163
  65.5 0.9 fusion.15
  67.8 11.3 %collective-permute-done.4 = bf16[704,384]{1,0:T(8,128)(2,1)S(1)} collective-permute-done((bf16[704,384]{1,0:T(8,128)(2,1)S(1)}, bf16[704,384]{1,0:T(8,128)(2,1)S(1)}, u32[]{:S(2)}, u32[]{:S(2)}) %collective-permute-start.4) | collective-permute-done | bytes 540704 | tf_op jit(solution)/shard_map/ppermute | solution.py:163
  79.2 1.7 %add_convert_fusion = bf16[384,1024]{1,0:T(8,128)(2,1)} fusion(f32[384,1024]{1,0:T(8,128)S(1)} %fusion.5, bf16[704,384]{1,0:T(8,128)(2,1)S(1)} %collective-permute-done.4, bf16[2,704,1024]{2,1,0:T(8,128)(2,1)S(1)} %bitcast.50, s32[]{:T(128)S(6)} %select_n.121), kind=kOutput, calls=%fused_computation.2 | convolution fusion | flops 554434560 | bytes 4341764 | tf_op jit(solution)/shard_map/dot_general | solution.py:268
  80.9 9.0 %all-to-all-start.1 = ((bf16[16,24,1024]{2,1,0:T(8,128)(2,1)}), bf16[16,24,1024]{2,1,0:T(8,128)(2,1)}, u32[]{:S(2)}, u32[]{:S(2)}) async-start(bf16[16,24,1024]{2,1,0:T(8,128)(2,1)} %bitcast.55), calls=%async_computation.1 | async-start | bytes 1572864 | tf_op jit(solution)/shard_map/all_to_all | solution.py:273
  89.9 1.7 %fusion.2 = f32[32,1024]{1,0:T(8,128)S(1)} fusion(bf16[32,704]{1,0:T(8,128)(2,1)S(1)} %fusion.15, bf16[2,704,1024]{2,1,0:T(8,128)(2,1)} %bitcast.53, s32[]{:T(128)S(6)} %select_n.120), kind=kOutput, calls=%fused_computation.5 | convolution fusion | flops 46137344 | bytes 1617924 | tf_op jit(solution)/shard_map/dot_general | solution.py:269
  91.8 1.7 %gather_fusion = f32[192]{0:T(256)S(1)} fusion(f32[32,16]{0,1:T(8,128)S(1)} %maximum_select_fusion.2, s32[192]{0:T(256)S(1)} %reshape.219), kind=kCustom, calls=%fused_computation | custom fusion | bytes 3072 | tf_op jit(solution)/shard_map/jit(take_along_axis)/gather | solution.py:225
  94.3 1.7 %fusion.12 = f32[32,1024]{1,0:T(8,128)S(1)} fusion(f32[32,1024]{1,0:T(8,128)S(1)} %fusion.2, bf16[2,704,1024]{2,1,0:T(8,128)(2,1)} %bitcast.54, s32[]{:T(128)S(6)} %select_n.121, bf16[16,704]{1,0:T(8,128)(2,1)S(1)} %get-tuple-element.13, bf16[16,704]{1,0:T(8,128)(2,1)S(1)} %get-tuple-element.12), kind=kOutput, calls=%fused_computation.16 | convolution fusion | flops 46260224 | bytes 1748996 | tf_op jit(solution)/shard_map/dot_general | solution.py:269
  96.1 12.6 %all-to-all-done.1 = bf16[16,24,1024]{2,1,0:T(8,128)(2,1)} async-done(((bf16[16,24,1024]{2,1,0:T(8,128)(2,1)}), bf16[16,24,1024]{2,1,0:T(8,128)(2,1)}, u32[]{:S(2)}, u32[]{:S(2)}) %all-to-all-start.1) | async-done | bytes 786464 | tf_op jit(solution)/shard_map/all_to_all | solution.py:273
  108.6 1.4 %fusion.11 = f32[32,1024]{1,0:T(8,128)S(1)} fusion(f32[32,1024]{1,0:T(8,128)S(1)} %fusion.12, bf16[32,384]{1,0:T(8,128)(2,1)S(1)} %fusion.18, bf16[384,1024]{1,0:T(8,128)(2,1)} %bitcast.14, pred[32]{0:T(512)(128)(4,1)S(1)} %lt.63), kind=kOutput, calls=%fused_computation.15 | convolution fusion | flops 25231360 | bytes 1073184 | tf_op jit(solution)/shard_map/dot_general | solution.py:279
  110.0 1.6 %collective-permute-start.6 = (f32[16,1024]{1,0:T(8,128)S(1)}, f32[16,1024]{1,0:T(8,128)S(1)}, u32[]{:S(2)}, u32[]{:S(2)}) collective-permute-start(f32[16,1024]{1,0:T(8,128)S(1)} %get-tuple-element.8), channel_id=1, source_target_pairs={{0,16},{16,0},{1,17},{17,1},{2,18},{18,2},{3,19},{19,3},{4,20},{20... | collective-permute-start | bytes 196616 | tf_op jit(solution)/shard_map/ppermute | solution.py:163
  111.6 2.7 %collective-permute-done.6 = f32[16,1024]{1,0:T(8,128)S(1)} collective-permute-done((f32[16,1024]{1,0:T(8,128)S(1)}, f32[16,1024]{1,0:T(8,128)S(1)}, u32[]{:S(2)}, u32[]{:S(2)}) %collective-permute-start.6) | collective-permute-done | bytes 65568 | tf_op jit(solution)/shard_map/ppermute | solution.py:163
  (68 shorter events, 8.2 us)
Async XLA Ops:
  0.6 66.4 %copy-start = (bf16[1,1408,1024]{2,1,0:T(8,128)(2,1)S(1)}, bf16[1,1408,1024]{2,1,0:T(8,128)(2,1)}, u32[]{:S(2)}) copy-start(bf16[1,1408,1024]{2,1,0:T(8,128)(2,1)} %param.23) | copy-start | bytes 8650756
  0.6 13.8 %copy-start.3 = (bf16[1,1,16,2048]{3,2,1,0:T(8,128)(2,1)S(1)}, bf16[1,1,16,2048]{3,2,1,0:T(8,128)(2,1)}, u32[]{:S(2)}) copy-start(bf16[1,1,16,2048]{3,2,1,0:T(8,128)(2,1)} %param.15) | copy-start | bytes 196612
  0.7 14.9 %copy-start.6 = (f32[2048]{0:T(1024)S(1)}, f32[2048]{0:T(1024)}, u32[]{:S(2)}) copy-start(f32[2048]{0:T(1024)} %param.17) | copy-start | bytes 24580
  0.7 6.7 %collective-permute-start.1 = (bf16[16,1024]{1,0:T(8,128)(2,1)}, bf16[16,1024]{1,0:T(8,128)(2,1)S(1)}, u32[]{:S(2)}, u32[]{:S(2)}) collective-permute-start(bf16[16,1024]{1,0:T(8,128)(2,1)} %bitcast.63), channel_id=1, source_target_pairs={{0,16},{16,0},{1,17},{17,1},{2,18},{18,2},{3,19},{19,3},{4,20},{20... | collective-permute-start | bytes 98312 | tf_op jit(solution)/shard_map/ppermute | solution.py:163
  3.7 10.1 %collective-permute-start = (bf16[16,2048]{1,0:T(8,128)(2,1)}, bf16[16,2048]{1,0:T(8,128)(2,1)S(1)}, u32[]{:S(2)}, u32[]{:S(2)}) collective-permute-start(bf16[16,2048]{1,0:T(8,128)(2,1)} %bitcast.61), channel_id=1, source_target_pairs={{0,16},{16,0},{1,17},{17,1},{2,18},{18,2},{3,19},{19,3},{4,20},{20... | collective-permute-start | bytes 196616 | tf_op jit(solution)/shard_map/ppermute | solution.py:163
  9.5 4.3 %collective-permute-start.2 = (bf16[32,1024]{1,0:T(8,128)(2,1)S(1)}, bf16[32,1024]{1,0:T(8,128)(2,1)S(1)}, u32[]{:S(2)}, u32[]{:S(2)}) collective-permute-start(bf16[32,1024]{1,0:T(8,128)(2,1)S(1)} %convolution_convert_fusion.1), channel_id=1, source_target_pairs={{0,16},{16,0},{1,17},{17,1},{2,18},{18,2},{3,19},{19,3},{4,20},{20... | collective-permute-start | bytes 196616 | tf_op jit(solution)/shard_map/ppermute | solution.py:163
  13.8 0.6 copy-start.4
  14.5 9.6 %copy-start.5 = (bf16[2048,8]{0,1:T(8,128)(2,1)S(1)}, bf16[2048,8]{0,1:T(8,128)(2,1)}, u32[]{:S(2)}) copy-start(bf16[2048,8]{0,1:T(8,128)(2,1)} %param.18) | copy-start | bytes 98308
  17.4 38.4 %all-to-all-start = ((bf16[16,24,2048]{2,1,0:T(8,128)(2,1)}), bf16[16,24,2048]{2,1,0:T(8,128)(2,1)}, u32[]{:S(2)}, u32[]{:S(2)}) async-start(bf16[16,24,2048]{2,1,0:T(8,128)(2,1)} %bitcast.52), calls=%async_computation | async-start | bytes 3145728 | tf_op jit(solution)/shard_map/all_to_all | solution.py:249
  24.2 67.4 %collective-permute-start.3 = (f32[32,8]{0,1:T(8,128)S(1)}, f32[32,8]{0,1:T(8,128)S(1)}, u32[]{:S(2)}, u32[]{:S(2)}) collective-permute-start(f32[32,8]{0,1:T(8,128)S(1)} %fusion.44), channel_id=1, source_target_pairs={{0,16},{16,0},{1,17},{17,1},{2,18},{18,2},{3,19},{19,3},{4,20},{20... | collective-permute-start | bytes 3080 | tf_op jit(solution)/shard_map/ppermute | solution.py:163
  55.8 1.8 %copy-start.1 = (bf16[1,704,2048]{2,1,0:T(8,128)(2,1)S(1)}, bf16[1,704,2048]{2,1,0:T(8,128)(2,1)}, u32[]{:S(2)}) copy-start(bf16[1,704,2048]{2,1,0:T(8,128)(2,1)} %param.21) | copy-start | bytes 8650756
  57.6 7.9 %copy-start.2 = (bf16[704,2048]{1,0:T(8,128)(2,1)S(1)}, bf16[704,2048]{1,0:T(8,128)(2,1)}, u32[]{:S(2)}) copy-start(bf16[704,2048]{1,0:T(8,128)(2,1)} %param.25) | copy-start | bytes 8650756
  63.9 15.2 %collective-permute-start.4 = (bf16[704,384]{1,0:T(8,128)(2,1)S(1)}, bf16[704,384]{1,0:T(8,128)(2,1)S(1)}, u32[]{:S(2)}, u32[]{:S(2)}) collective-permute-start(bf16[704,384]{1,0:T(8,128)(2,1)S(1)} %shard_map.149), channel_id=1, source_target_pairs={{0,16},{16,0},{1,17},{17,1},{2,18},{18,2},{3,19},{19,3},{4,20},{20... | collective-permute-start | bytes 1622024 | tf_op jit(solution)/shard_map/ppermute | solution.py:163
  66.5 27.9 %collective-permute-start.5 = (bf16[32,704]{1,0:T(8,128)(2,1)S(1)}, bf16[32,704]{1,0:T(8,128)(2,1)S(1)}, u32[]{:S(2)}, u32[]{:S(2)}) collective-permute-start(bf16[32,704]{1,0:T(8,128)(2,1)S(1)} %fusion.15), channel_id=1, source_target_pairs={{0,16},{16,0},{1,17},{17,1},{2,18},{18,2},{3,19},{19,3},{4,20},{20... | collective-permute-start | bytes 135176 | tf_op jit(solution)/shard_map/ppermute | solution.py:163
  80.9 27.8 %all-to-all-start.1 = ((bf16[16,24,1024]{2,1,0:T(8,128)(2,1)}), bf16[16,24,1024]{2,1,0:T(8,128)(2,1)}, u32[]{:S(2)}, u32[]{:S(2)}) async-start(bf16[16,24,1024]{2,1,0:T(8,128)(2,1)} %bitcast.55), calls=%async_computation.1 | async-start | bytes 1572864 | tf_op jit(solution)/shard_map/all_to_all | solution.py:273
  93.4 21.1 %copy-start.7 = (f32[2048]{0:T(1024)S(1)}, f32[2048]{0:T(1024)}, u32[]{:S(2)}) copy-start(f32[2048]{0:T(1024)} %param.27) | copy-start | bytes 24580
  110.0 4.3 %collective-permute-start.6 = (f32[16,1024]{1,0:T(8,128)S(1)}, f32[16,1024]{1,0:T(8,128)S(1)}, u32[]{:S(2)}, u32[]{:S(2)}) collective-permute-start(f32[16,1024]{1,0:T(8,128)S(1)} %get-tuple-element.8), channel_id=1, source_target_pairs={{0,16},{16,0},{1,17},{17,1},{2,18},{18,2},{3,19},{19,3},{4,20},{20... | collective-permute-start | bytes 196616 | tf_op jit(solution)/shard_map/ppermute | solution.py:163

commit v8 on v4

--- a/solution.py
+++ b/solution.py
@@ -243,9 +243,12 @@
     combine = jnp.sum(
         jnp.where(slot_hit, weights[:, :, None], jnp.zeros((), jnp.bfloat16)), axis=1
     ).astype(jnp.bfloat16)
-    routed = jnp.dot(combine, returned, preferred_element_type=jnp.float32)
-    combined = jnp.where(row_live[:, None], routed + shared, 0.0)
-    summed = in_axis_order(first, combined[:row_count], swap_pair(combined[row_count:]), 1)
+    routed_peer = jnp.dot(combine[row_count:], returned, preferred_element_type=jnp.float32)
+    combined_peer = jnp.where(row_live[row_count:, None], routed_peer + shared[row_count:], 0.0)
+    from_peer = swap_pair(combined_peer)
+    routed_mine = jnp.dot(combine[:row_count], returned, preferred_element_type=jnp.float32)
+    combined_mine = jnp.where(row_live[:row_count, None], routed_mine + shared[:row_count], 0.0)
+    summed = in_axis_order(first, combined_mine, from_peer, 1)
     stream_sum = stream_in + summed
     stream = stream_sum.astype(jnp.bfloat16)[None, None]
     normed = rms_scale(stream_sum, gain_out).astype(jnp.bfloat16)[None, None]

time: 115 us -> 115 us (level)
  waiting for transfers between devices: 56.2 us -> 54.9 us
  matrix products: 22.3 us -> 23.6 us
    ppermute x7, waiting for transfers between devices: 16.3 us -> 15 us  [swap_pair(): return lax.ppermute(x, 'dp', [(0, 1), (1, 0)])]
    dot_general x1 -> x2, matrix products: 1.37 us -> 2.7 us  [the longest x1 1.35 us: shards_pair(): jnp.dot(combine[row_count:], returned, preferred_element_type=jnp.float32)]
  transfers between devices with their start and end apart: 9 -> 9, of which waited for: 5 -> 5; matrix products, arithmetic and copies ran while one was open for 23% -> 24% of each run, Pallas kernels for 0% -> 0%
where the time goes in v8:
time: 115 us
  waiting for transfers between devices  54.9 us (48%)
  starting transfers between devices  25.9 us (23%)
  matrix products  23.6 us (21%)
  local copies, waits for them, and re-layouts  5.49 us (5%)
  other arithmetic  3.81 us (3%)
    all_to_all x1, waiting for transfers between devices, shards_pair(): lax.all_to_all(outgoing, 'expert', split_axis=0, concat_axis=0, tiled=True)  27.3 us
    ppermute x7, waiting for transfers between devices, swap_pair(): return lax.ppermute(x, 'dp', [(0, 1), (1, 0)])  15 us
    all_to_all x1, waiting for transfers between devices, shards_pair(): lax.all_to_all(expert_out, 'expert', split_axis=0, concat_axis=0, tiled=T...  12.6 us
    dot_general x4, matrix products, by_rows(): lax.dot_general(left, weight_rows, (((1,), (1,)), ((), ())), preferred_el...  11 us
    ppermute x7, starting transfers between devices, swap_pair(): return lax.ppermute(x, 'dp', [(0, 1), (1, 0)])  10.4 us
    all_to_all x1, starting transfers between devices, shards_pair(): lax.all_to_all(expert_out, 'expert', split_axis=0, concat_axis=0, tiled=T...  9.01 us
    all_to_all x1, starting transfers between devices, shards_pair(): lax.all_to_all(outgoing, 'expert', split_axis=0, concat_axis=0, tiled=True)  6.51 us
  transfers between devices with their start and end apart: 9, of which 5 were waited for; matrix products, arithmetic and copies ran while one was open for 24% of the time, Pallas kernels for 0%

profile of v8, /device:TPU:0, one launch (start us, length us, event | category | flops | bytes accessed | tf_op | source)
XLA Modules:
  0.0 114.6 jit_solution(12258865012530998147)
XLA Ops:
  0.7 3.0 %collective-permute-start.1 = (bf16[16,1024]{1,0:T(8,128)(2,1)}, bf16[16,1024]{1,0:T(8,128)(2,1)S(1)}, u32[]{:S(2)}, u32[]{:S(2)}) collective-permute-start(bf16[16,1024]{1,0:T(8,128)(2,1)} %bitcast.76), channel_id=1, source_target_pairs={{0,16},{16,0},{1,17},{17,1},{2,18},{18,2},{3,19},{19,3},{4,20},{20... | collective-permute-start | bytes 98312 | tf_op jit(solution)/shard_map/ppermute | solution.py:129
  7.4 2.1 %convolution_convert_fusion.1 = bf16[32,1024]{1,0:T(8,128)(2,1)S(1)} fusion(bf16[1024,1024]{1,0:T(8,128)(2,1)} %param.16, bf16[16,1024]{1,0:T(8,128)(2,1)S(1)} %collective-permute-done.1, bf16[16,1024]{1,0:T(8,128)(2,1)} %bitcast.77), kind=kOutput, calls=%fused_computation.22 | convolution fusion | flops 67272704 | bytes 2228224 | tf_op jit(solution)/shard_map/dot_general | solution.py:176
  9.5 2.0 %collective-permute-start.2 = (bf16[32,1024]{1,0:T(8,128)(2,1)S(1)}, bf16[32,1024]{1,0:T(8,128)(2,1)S(1)}, u32[]{:S(2)}, u32[]{:S(2)}) collective-permute-start(bf16[32,1024]{1,0:T(8,128)(2,1)S(1)} %convolution_convert_fusion.1), channel_id=1, source_target_pairs={{0,16},{16,0},{1,17},{17,1},{2,18},{18,2},{3,19},{19,3},{4,20},{20... | collective-permute-start | bytes 196616 | tf_op jit(solution)/shard_map/ppermute | solution.py:129
  11.6 2.2 %collective-permute-done.2 = bf16[32,1024]{1,0:T(8,128)(2,1)S(1)} collective-permute-done((bf16[32,1024]{1,0:T(8,128)(2,1)S(1)}, bf16[32,1024]{1,0:T(8,128)(2,1)S(1)}, u32[]{:S(2)}, u32[]{:S(2)}) %collective-permute-start.2) | collective-permute-done | bytes 65568 | tf_op jit(solution)/shard_map/ppermute | solution.py:129
  14.5 1.0 multiply_reduce_fusion
  15.6 1.8 %convolution_convert_fusion = bf16[384,2048]{1,0:T(8,128)(2,1)} fusion(pred[32,384]{1,0:T(8,128)(4,1)S(1)} %fusion.25, bf16[32,2048]{1,0:T(8,128)(2,1)S(1)} %multiply_convert_fusion), kind=kOutput, calls=%fused_computation.5 | convolution fusion | flops 51118080 | bytes 1716224 | tf_op jit(solution)/shard_map/dot_general | solution.py:212
  17.4 6.5 %all-to-all-start = ((bf16[16,24,2048]{2,1,0:T(8,128)(2,1)}), bf16[16,24,2048]{2,1,0:T(8,128)(2,1)}, u32[]{:S(2)}, u32[]{:S(2)}) async-start(bf16[16,24,2048]{2,1,0:T(8,128)(2,1)} %bitcast.65), calls=%async_computation | async-start | bytes 3145728 | tf_op jit(solution)/shard_map/all_to_all | solution.py:215
  24.4 1.5 %collective-permute-start.3 = (f32[32,8]{0,1:T(8,128)S(1)}, f32[32,8]{0,1:T(8,128)S(1)}, u32[]{:S(2)}, u32[]{:S(2)}) collective-permute-start(f32[32,8]{0,1:T(8,128)S(1)} %fusion.62), channel_id=1, source_target_pairs={{0,16},{16,0},{1,17},{17,1},{2,18},{18,2},{3,19},{19,3},{4,20},{20... | collective-permute-start | bytes 3080 | tf_op jit(solution)/shard_map/ppermute | solution.py:129
  25.9 2.7 %fusion.63 = f32[32,704]{1,0:T(8,128)S(1)} fusion(bf16[32,2048]{1,0:T(8,128)(2,1)S(1)} %multiply_convert_fusion, bf16[704,2048]{1,0:T(8,128)(2,1)} %param.24), kind=kOutput, calls=%fused_computation.88 | convolution fusion | flops 92274688 | bytes 3104768 | tf_op jit(solution)/shard_map/dot_general | solution.py:16
  28.6 27.3 %all-to-all-done = bf16[16,24,2048]{2,1,0:T(8,128)(2,1)} async-done(((bf16[16,24,2048]{2,1,0:T(8,128)(2,1)}), bf16[16,24,2048]{2,1,0:T(8,128)(2,1)}, u32[]{:S(2)}, u32[]{:S(2)}) %all-to-all-start) | async-done | bytes 1572896 | tf_op jit(solution)/shard_map/all_to_all | solution.py:215
  56.0 4.1 %fusion.2 = f32[384,704]{0,1:T(8,128)S(1)} fusion(bf16[384,2048]{1,0:T(8,128)(2,1)} %bitcast.8, bf16[1,704,2048]{2,1,0:T(8,128)(2,1)} %param.21), kind=kOutput, calls=%fused_computation.3 | convolution fusion | flops 1107296256 | bytes 5537792 | tf_op jit(solution)/shard_map/dot_general | solution.py:16
  60.1 3.3 %fusion.18 = bf16[384,704]{0,1:T(8,128)(2,1)S(1)} fusion(bf16[384,2048]{1,0:T(8,128)(2,1)} %bitcast.8, bf16[1,704,2048]{2,1,0:T(8,128)(2,1)S(1)} %copy-done.7, f32[384,704]{0,1:T(8,128)S(1)} %fusion.2), kind=kOutput, calls=%fused_computation.19 | convolution fusion | flops 1108918272 | bytes 6078464 | tf_op jit(solution)/shard_map/dot_general | solution.py:16
  63.4 1.6 %collective-permute-start.4 = (bf16[384,704]{0,1:T(8,128)(2,1)S(1)}, bf16[384,704]{0,1:T(8,128)(2,1)S(1)}, u32[]{:S(2)}, u32[]{:S(2)}) collective-permute-start(bf16[384,704]{0,1:T(8,128)(2,1)S(1)} %fusion.18), channel_id=1, source_target_pairs={{0,16},{16,0},{1,17},{17,1},{2,18},{18,2},{3,19},{19,3},{4,20},{20... | collective-permute-start | bytes 1622024 | tf_op jit(solution)/shard_map/ppermute | solution.py:129
  67.2 11.3 %collective-permute-done.4 = bf16[384,704]{0,1:T(8,128)(2,1)S(1)} collective-permute-done((bf16[384,704]{0,1:T(8,128)(2,1)S(1)}, bf16[384,704]{0,1:T(8,128)(2,1)S(1)}, u32[]{:S(2)}, u32[]{:S(2)}) %collective-permute-start.4) | collective-permute-done | bytes 540704 | tf_op jit(solution)/shard_map/ppermute | solution.py:129
  78.6 1.7 %add_convert_fusion = bf16[384,1024]{1,0:T(8,128)(2,1)} fusion(f32[384,1024]{1,0:T(8,128)S(1)} %fusion.9, bf16[384,704]{0,1:T(8,128)(2,1)S(1)} %collective-permute-done.4, bf16[2,704,1024]{2,1,0:T(8,128)(2,1)S(1)} %bitcast.64, s32[]{:T(128)S(6)} %select_n.124), kind=kOutput, calls=%fused_computation.6 | convolution fusion | flops 554434560 | bytes 4341764 | tf_op jit(solution)/shard_map/dot_general | solution.py:233
  80.3 9.0 %all-to-all-start.1 = ((bf16[16,24,1024]{2,1,0:T(8,128)(2,1)}), bf16[16,24,1024]{2,1,0:T(8,128)(2,1)}, u32[]{:S(2)}, u32[]{:S(2)}) async-start(bf16[16,24,1024]{2,1,0:T(8,128)(2,1)} %bitcast.68), calls=%async_computation.1 | async-start | bytes 1572864 | tf_op jit(solution)/shard_map/all_to_all | solution.py:240
  89.3 1.7 %fusion.6 = f32[32,1024]{1,0:T(8,128)S(1)} fusion(bf16[32,704]{1,0:T(8,128)(2,1)S(1)} %fusion.24, bf16[2,704,1024]{2,1,0:T(8,128)(2,1)} %bitcast.66, s32[]{:T(128)S(6)} %select_n.123), kind=kOutput, calls=%fused_computation.9 | convolution fusion | flops 46137344 | bytes 1617924 | tf_op jit(solution)/shard_map/dot_general | solution.py:236
  91.2 1.7 %gather_fusion = f32[192]{0:T(256)S(1)} fusion(f32[32,16]{0,1:T(8,128)S(1)} %maximum_select_fusion.2, s32[192]{0:T(256)S(1)} %reshape.226), kind=kCustom, calls=%fused_computation | custom fusion | bytes 3072 | tf_op jit(solution)/shard_map/jit(take_along_axis)/gather | solution.py:191
  93.7 1.7 %fusion.21 = f32[32,1024]{1,0:T(8,128)S(1)} fusion(f32[32,1024]{1,0:T(8,128)S(1)} %fusion.6, bf16[2,704,1024]{2,1,0:T(8,128)(2,1)} %bitcast.67, s32[]{:T(128)S(6)} %select_n.124, bf16[16,704]{1,0:T(8,128)(2,1)S(1)} %get-tuple-element.11, bf16[16,704]{1,0:T(8,128)(2,1)S(1)} %get-tuple-element.10), kind=kOutput, calls=%fused_computation.20 | convolution fusion | flops 46260224 | bytes 1748996 | tf_op jit(solution)/shard_map/dot_general | solution.py:236
  95.5 12.6 %all-to-all-done.1 = bf16[16,24,1024]{2,1,0:T(8,128)(2,1)} async-done(((bf16[16,24,1024]{2,1,0:T(8,128)(2,1)}), bf16[16,24,1024]{2,1,0:T(8,128)(2,1)}, u32[]{:S(2)}, u32[]{:S(2)}) %all-to-all-start.1) | async-done | bytes 786464 | tf_op jit(solution)/shard_map/all_to_all | solution.py:240
  108.1 1.4 %fusion.31 = f32[16,1024]{1,0:T(8,128)S(1)} fusion(f32[32,1024]{1,0:T(8,128)S(1)} %fusion.21, pred[16]{0:T(512)(128)(4,1)S(1)} %get-tuple-element.14, bf16[384,1024]{1,0:T(8,128)(2,1)} %bitcast.15, bf16[32,384]{1,0:T(8,128)(2,1)S(1)} %fusion.27), kind=kOutput, calls=%fused_computation.42 | convolution fusion | flops 12615680 | bytes 930304 | tf_op jit(solution)/shard_map/dot_general | solution.py:246
  109.4 1.5 %collective-permute-start.6 = (f32[16,1024]{1,0:T(8,128)S(1)}, f32[16,1024]{1,0:T(8,128)S(1)}, u32[]{:S(2)}, u32[]{:S(2)}) collective-permute-start(f32[16,1024]{1,0:T(8,128)S(1)} %fusion.31), channel_id=1, source_target_pairs={{0,16},{16,0},{1,17},{17,1},{2,18},{18,2},{3,19},{19,3},{4,20},{20... | collective-permute-start | bytes 196616 | tf_op jit(solution)/shard_map/ppermute | solution.py:129
  110.9 1.4 %fusion.32 = f32[16,1024]{1,0:T(8,128)S(1)} fusion(f32[32,1024]{1,0:T(8,128)S(1)} %fusion.21, pred[16]{0:T(512)(128)(4,1)S(1)} %get-tuple-element.15, bf16[384,1024]{1,0:T(8,128)(2,1)} %bitcast.15, bf16[32,384]{1,0:T(8,128)(2,1)S(1)} %fusion.27), kind=kOutput, calls=%fused_computation.44 | convolution fusion | flops 12615680 | bytes 930304 | tf_op jit(solution)/shard_map/dot_general | solution.py:249
  112.3 1.4 %collective-permute-done.6 = f32[16,1024]{1,0:T(8,128)S(1)} collective-permute-done((f32[16,1024]{1,0:T(8,128)S(1)}, f32[16,1024]{1,0:T(8,128)S(1)}, u32[]{:S(2)}, u32[]{:S(2)}) %collective-permute-start.6) | collective-permute-done | bytes 65568 | tf_op jit(solution)/shard_map/ppermute | solution.py:129
  (70 shorter events, 9.2 us)
Async XLA Ops:
  0.6 65.8 %copy-start = (bf16[1,1408,1024]{2,1,0:T(8,128)(2,1)S(1)}, bf16[1,1408,1024]{2,1,0:T(8,128)(2,1)}, u32[]{:S(2)}) copy-start(bf16[1,1408,1024]{2,1,0:T(8,128)(2,1)} %param.23) | copy-start | bytes 8650756
  0.6 13.8 %copy-start.2 = (bf16[1,1,16,2048]{3,2,1,0:T(8,128)(2,1)S(1)}, bf16[1,1,16,2048]{3,2,1,0:T(8,128)(2,1)}, u32[]{:S(2)}) copy-start(bf16[1,1,16,2048]{3,2,1,0:T(8,128)(2,1)} %param.15) | copy-start | bytes 196612
  0.7 6.7 %collective-permute-start.1 = (bf16[16,1024]{1,0:T(8,128)(2,1)}, bf16[16,1024]{1,0:T(8,128)(2,1)S(1)}, u32[]{:S(2)}, u32[]{:S(2)}) collective-permute-start(bf16[16,1024]{1,0:T(8,128)(2,1)} %bitcast.76), channel_id=1, source_target_pairs={{0,16},{16,0},{1,17},{17,1},{2,18},{18,2},{3,19},{19,3},{4,20},{20... | collective-permute-start | bytes 98312 | tf_op jit(solution)/shard_map/ppermute | solution.py:129
  3.7 10.1 %collective-permute-start = (bf16[16,2048]{1,0:T(8,128)(2,1)}, bf16[16,2048]{1,0:T(8,128)(2,1)S(1)}, u32[]{:S(2)}, u32[]{:S(2)}) collective-permute-start(bf16[16,2048]{1,0:T(8,128)(2,1)} %bitcast.74), channel_id=1, source_target_pairs={{0,16},{16,0},{1,17},{17,1},{2,18},{18,2},{3,19},{19,3},{4,20},{20... | collective-permute-start | bytes 196616 | tf_op jit(solution)/shard_map/ppermute | solution.py:129
  6.9 8.6 %copy-start.5 = (f32[2048]{0:T(1024)S(1)}, f32[2048]{0:T(1024)}, u32[]{:S(2)}) copy-start(f32[2048]{0:T(1024)} %param.17) | copy-start | bytes 24580
  9.5 4.3 %collective-permute-start.2 = (bf16[32,1024]{1,0:T(8,128)(2,1)S(1)}, bf16[32,1024]{1,0:T(8,128)(2,1)S(1)}, u32[]{:S(2)}, u32[]{:S(2)}) collective-permute-start(bf16[32,1024]{1,0:T(8,128)(2,1)S(1)} %convolution_convert_fusion.1), channel_id=1, source_target_pairs={{0,16},{16,0},{1,17},{17,1},{2,18},{18,2},{3,19},{19,3},{4,20},{20... | collective-permute-start | bytes 196616 | tf_op jit(solution)/shard_map/ppermute | solution.py:129
  13.8 0.6 copy-start.3
  17.4 6.8 %copy-start.4 = (bf16[2048,8]{0,1:T(8,128)(2,1)S(1)}, bf16[2048,8]{0,1:T(8,128)(2,1)}, u32[]{:S(2)}) copy-start(bf16[2048,8]{0,1:T(8,128)(2,1)} %param.18) | copy-start | bytes 98308
  17.4 38.6 %all-to-all-start = ((bf16[16,24,2048]{2,1,0:T(8,128)(2,1)}), bf16[16,24,2048]{2,1,0:T(8,128)(2,1)}, u32[]{:S(2)}, u32[]{:S(2)}) async-start(bf16[16,24,2048]{2,1,0:T(8,128)(2,1)} %bitcast.65), calls=%async_computation | async-start | bytes 3145728 | tf_op jit(solution)/shard_map/all_to_all | solution.py:215
  24.4 66.6 %collective-permute-start.3 = (f32[32,8]{0,1:T(8,128)S(1)}, f32[32,8]{0,1:T(8,128)S(1)}, u32[]{:S(2)}, u32[]{:S(2)}) collective-permute-start(f32[32,8]{0,1:T(8,128)S(1)} %fusion.62), channel_id=1, source_target_pairs={{0,16},{16,0},{1,17},{17,1},{2,18},{18,2},{3,19},{19,3},{4,20},{20... | collective-permute-start | bytes 3080 | tf_op jit(solution)/shard_map/ppermute | solution.py:129
  55.9 4.1 %copy-start.7 = (bf16[1,704,2048]{2,1,0:T(8,128)(2,1)S(1)}, bf16[1,704,2048]{2,1,0:T(8,128)(2,1)}, u32[]{:S(2)}) copy-start(bf16[1,704,2048]{2,1,0:T(8,128)(2,1)} %param.22) | copy-start | bytes 8650756
  60.1 4.9 %copy-start.1 = (bf16[704,2048]{1,0:T(8,128)(2,1)S(1)}, bf16[704,2048]{1,0:T(8,128)(2,1)}, u32[]{:S(2)}) copy-start(bf16[704,2048]{1,0:T(8,128)(2,1)} %param.25) | copy-start | bytes 8650756
  63.4 15.2 %collective-permute-start.4 = (bf16[384,704]{0,1:T(8,128)(2,1)S(1)}, bf16[384,704]{0,1:T(8,128)(2,1)S(1)}, u32[]{:S(2)}, u32[]{:S(2)}) collective-permute-start(bf16[384,704]{0,1:T(8,128)(2,1)S(1)} %fusion.18), channel_id=1, source_target_pairs={{0,16},{16,0},{1,17},{17,1},{2,18},{18,2},{3,19},{19,3},{4,20},{20... | collective-permute-start | bytes 1622024 | tf_op jit(solution)/shard_map/ppermute | solution.py:129
  65.9 27.9 %collective-permute-start.5 = (bf16[32,704]{1,0:T(8,128)(2,1)S(1)}, bf16[32,704]{1,0:T(8,128)(2,1)S(1)}, u32[]{:S(2)}, u32[]{:S(2)}) collective-permute-start(bf16[32,704]{1,0:T(8,128)(2,1)S(1)} %fusion.24), channel_id=1, source_target_pairs={{0,16},{16,0},{1,17},{17,1},{2,18},{18,2},{3,19},{19,3},{4,20},{20... | collective-permute-start | bytes 135176 | tf_op jit(solution)/shard_map/ppermute | solution.py:129
  80.3 27.8 %all-to-all-start.1 = ((bf16[16,24,1024]{2,1,0:T(8,128)(2,1)}), bf16[16,24,1024]{2,1,0:T(8,128)(2,1)}, u32[]{:S(2)}, u32[]{:S(2)}) async-start(bf16[16,24,1024]{2,1,0:T(8,128)(2,1)} %bitcast.68), calls=%async_computation.1 | async-start | bytes 1572864 | tf_op jit(solution)/shard_map/all_to_all | solution.py:240
  93.7 20.1 %copy-start.6 = (f32[2048]{0:T(1024)S(1)}, f32[2048]{0:T(1024)}, u32[]{:S(2)}) copy-start(f32[2048]{0:T(1024)} %param.27) | copy-start | bytes 24580
  109.4 4.3 %collective-permute-start.6 = (f32[16,1024]{1,0:T(8,128)S(1)}, f32[16,1024]{1,0:T(8,128)S(1)}, u32[]{:S(2)}, u32[]{:S(2)}) collective-permute-start(f32[16,1024]{1,0:T(8,128)S(1)} %fusion.31), channel_id=1, source_target_pairs={{0,16},{16,0},{1,17},{17,1},{2,18},{18,2},{3,19},{19,3},{4,20},{20... | collective-permute-start | bytes 196616 | tf_op jit(solution)/shard_map/ppermute | solution.py:129

commit v9 on v4

--- a/solution.py
+++ b/solution.py
@@ -203,40 +203,59 @@
     before = jnp.cumsum(onehot, axis=1) - onehot
     position = jnp.sum(before * onehot, axis=2)
     slot_total = experts * groups * capacity
-    offsets = group_of_block[:, None] * capacity
+    offsets = jnp.arange(groups, dtype=jnp.int32)[:, None] * capacity
     target = jnp.where(
         block_live, block_experts * (groups * capacity) + offsets + position, slot_total
     ).reshape(rows_all, top_count)
     slot_hit = target[:, :, None] == jnp.arange(slot_total, dtype=jnp.int32)[None, None, :]
-    fill = jnp.any(slot_hit, axis=1).astype(jnp.bfloat16)
+    own_total = experts * capacity
+    own_target = jnp.where(
+        block_live[0], block_experts[0] * capacity + position[0], own_total
+    ).reshape(row_count, top_count)
+    own_hit = own_target[:, :, None] == jnp.arange(own_total, dtype=jnp.int32)[None, None, :]
+    fill = jnp.any(own_hit, axis=1).astype(jnp.bfloat16)
     outgoing = lax.dot_general(
-        fill, column, (((0,), (0,)), ((), ())), preferred_element_type=jnp.float32
-    ).astype(jnp.bfloat16).reshape(experts, groups * capacity, column.shape[1])
-    slot_rows = lax.all_to_all(outgoing, "expert", split_axis=0, concat_axis=0, tiled=True)
-    flattened = slot_rows.reshape(-1, slot_rows.shape[-1])
-    gate_value = by_rows(flattened, gate_local)
-    up_value = by_rows(flattened, up_local)
-    hidden = (jax.nn.silu(gate_value) * up_value).astype(jnp.bfloat16)
-    hidden_peer = swap_pair(hidden)
+        fill, column[:row_count], (((0,), (0,)), ((), ())), preferred_element_type=jnp.float32
+    ).astype(jnp.bfloat16).reshape(experts, capacity, column.shape[1])
+    slot_own = lax.all_to_all(outgoing, "expert", split_axis=0, concat_axis=0, tiled=True)
+    slot_own = slot_own.reshape(-1, slot_own.shape[-1])
+    slot_other = swap_pair(slot_own)
+    hidden_own = (jax.nn.silu(by_rows(slot_own, gate_local)) * by_rows(slot_own, up_local)).astype(
+        jnp.bfloat16
+    )
+    hidden_own_peer = swap_pair(hidden_own)
+    hidden_other = (
+        jax.nn.silu(by_rows(slot_other, gate_local)) * by_rows(slot_other, up_local)
+    ).astype(jnp.bfloat16)
+    hidden_other_peer = swap_pair(hidden_other)
     shared_gate_value = by_rows(column, shared_gate)
     shared_up_value = by_rows(column, shared_up)
     shared_hidden = (jax.nn.silu(shared_gate_value) * shared_up_value).astype(jnp.bfloat16)
     shared_peer = halves_swapped(swap_pair(shared_hidden))
 
-    unit_count = hidden.shape[1]
+    unit_count = hidden_own.shape[1]
     down_blocks = down_local.reshape(groups, unit_count, column_width)
     shared_blocks = shared_down.reshape(groups, unit_count, column_width)
     down_mine = lax.dynamic_index_in_dim(down_blocks, me, 0, keepdims=False)
     down_peer = lax.dynamic_index_in_dim(down_blocks, 1 - me, 0, keepdims=False)
     shared_mine = lax.dynamic_index_in_dim(shared_blocks, me, 0, keepdims=False)
     shared_other = lax.dynamic_index_in_dim(shared_blocks, 1 - me, 0, keepdims=False)
-    routed_total = jnp.dot(hidden, down_mine, preferred_element_type=jnp.float32) + jnp.dot(
-        hidden_peer, down_peer, preferred_element_type=jnp.float32
+    out_own = jnp.dot(hidden_own, down_mine, preferred_element_type=jnp.float32) + jnp.dot(
+        hidden_other_peer, down_peer, preferred_element_type=jnp.float32
+    )
+    out_other = jnp.dot(hidden_other, down_mine, preferred_element_type=jnp.float32) + jnp.dot(
+        hidden_own_peer, down_peer, preferred_element_type=jnp.float32
     )
     shared = jnp.dot(shared_hidden, shared_mine, preferred_element_type=jnp.float32) + jnp.dot(
         shared_peer, shared_other, preferred_element_type=jnp.float32
     )
-    expert_out = routed_total.astype(jnp.bfloat16).reshape(experts, groups * capacity, column_width)
+    expert_out = jnp.concatenate(
+        [
+            out_own.astype(jnp.bfloat16).reshape(experts, capacity, column_width),
+            out_other.astype(jnp.bfloat16).reshape(experts, capacity, column_width),
+        ],
+        axis=1,
+    )
     returned = lax.all_to_all(
         expert_out, "expert", split_axis=0, concat_axis=0, tiled=True
     ).reshape(slot_total, column_width)

time: 115 us -> 123 us (1.070)
  local copies, waits for them, and re-layouts: 5.49 us -> 13 us
  waiting for transfers between devices: 56.2 us -> 50.6 us
  matrix products: 22.3 us -> 25.5 us
  other arithmetic: 3.81 us -> 5.81 us
    all_to_all x1, waiting for transfers between devices: 27.3 us -> 16.1 us  [shards_pair(): lax.all_to_all(outgoing, 'expert', split_axis=0, concat_axis=0, tiled=True)]
    reshape x0 -> x4, local copies, waits for them, and re-layouts: none -> 7.24 us  [the longest x1 2.16 us: shards_pair(): outgoing = lax.dot_general(fill, column[:row_count], (((0,), (0,)), ((),...]
    ppermute x7 -> x9, waiting for transfers between devices: 16.3 us -> 21.9 us  [swap_pair(): return lax.ppermute(x, 'dp', [(0, 1), (1, 0)])]
    dot_general x3 -> x5, matrix products: 4.28 us -> 7.91 us  [the longest x1 2.48 us: shards_pair(): jnp.dot(hidden_other_peer, down_peer, preferred_element_type=jnp.float32)]
    ppermute x7 -> x9, starting transfers between devices: 10.4 us -> 12.9 us  [swap_pair(): return lax.ppermute(x, 'dp', [(0, 1), (1, 0)])]
    all_to_all x1, starting transfers between devices: 9.01 us -> 6.6 us  [shards_pair(): lax.all_to_all(expert_out, 'expert', split_axis=0, concat_axis=0, tiled=T...]
    concatenate x0 -> x1, other arithmetic: none -> 2.16 us  [shards_pair(): jnp.concatenate([out_own.astype(jnp.bfloat16).reshape(experts, capacity,...]
    dot_general x4 -> x6, matrix products: 11 us -> 10.6 us  [by_rows(): lax.dot_general(left, weight_rows, (((1,), (1,)), ((), ())), preferred_el...]
  transfers between devices with their start and end apart: 9 -> 11, of which waited for: 5 -> 7; matrix products, arithmetic and copies ran while one was open for 23% -> 30% of each run, Pallas kernels for 0% -> 0%
where the time goes in v9:
time: 123 us; the launch traced here: 122 us
  waiting for transfers between devices  50.6 us (41%)
  starting transfers between devices  25.8 us (21%)
  matrix products  25.5 us (21%)
  local copies, waits for them, and re-layouts  13 us (11%)
  other arithmetic  5.81 us (5%)
    ppermute x9, waiting for transfers between devices, swap_pair(): return lax.ppermute(x, 'dp', [(0, 1), (1, 0)])  21.9 us
    all_to_all x1, waiting for transfers between devices, shards_pair(): lax.all_to_all(outgoing, 'expert', split_axis=0, concat_axis=0, tiled=True)  16.1 us
    ppermute x9, starting transfers between devices, swap_pair(): return lax.ppermute(x, 'dp', [(0, 1), (1, 0)])  12.9 us
    all_to_all x1, waiting for transfers between devices, shards_pair(): lax.all_to_all(expert_out, 'expert', split_axis=0, concat_axis=0, tiled=T...  12.6 us
    dot_general x6, matrix products, by_rows(): lax.dot_general(left, weight_rows, (((1,), (1,)), ((), ())), preferred_el...  10.6 us
    all_to_all x1, starting transfers between devices, shards_pair(): lax.all_to_all(expert_out, 'expert', split_axis=0, concat_axis=0, tiled=T...  6.6 us
    all_to_all x1, starting transfers between devices, shards_pair(): lax.all_to_all(outgoing, 'expert', split_axis=0, concat_axis=0, tiled=True)  6.39 us
    dot_general x1, matrix products, shards_pair(): jnp.dot(hidden_other_peer, down_peer, preferred_element_type=jnp.float32)  2.48 us
  transfers between devices with their start and end apart: 11, of which 7 were waited for; matrix products, arithmetic and copies ran while one was open for 30% of the time, Pallas kernels for 0%

profile of v9, /device:TPU:0, one launch (start us, length us, event | category | flops | bytes accessed | tf_op | source)
XLA Modules:
  0.0 121.7 jit_solution(9942559658936584102)
XLA Ops:
  0.7 3.0 %collective-permute-start.1 = (bf16[16,1024]{1,0:T(8,128)(2,1)}, bf16[16,1024]{1,0:T(8,128)(2,1)S(1)}, u32[]{:S(2)}, u32[]{:S(2)}) collective-permute-start(bf16[16,1024]{1,0:T(8,128)(2,1)} %bitcast.96), channel_id=1, source_target_pairs={{0,16},{16,0},{1,17},{17,1},{2,18},{18,2},{3,19},{19,3},{4,20},{20... | collective-permute-start | bytes 98312 | tf_op jit(solution)/shard_map/ppermute | solution.py:129
  7.1 2.1 %convolution_convert_fusion.1 = bf16[32,1024]{1,0:T(8,128)(2,1)S(1)} fusion(bf16[1024,1024]{1,0:T(8,128)(2,1)} %param.16, bf16[16,1024]{1,0:T(8,128)(2,1)S(1)} %collective-permute-done.1, bf16[16,1024]{1,0:T(8,128)(2,1)} %bitcast.97), kind=kOutput, calls=%fused_computation.38 | convolution fusion | flops 67272704 | bytes 2228224 | tf_op jit(solution)/shard_map/dot_general | solution.py:176
  9.2 2.0 %collective-permute-start.2 = (bf16[32,1024]{1,0:T(8,128)(2,1)S(1)}, bf16[32,1024]{1,0:T(8,128)(2,1)S(1)}, u32[]{:S(2)}, u32[]{:S(2)}) collective-permute-start(bf16[32,1024]{1,0:T(8,128)(2,1)S(1)} %convolution_convert_fusion.1), channel_id=1, source_target_pairs={{0,16},{16,0},{1,17},{17,1},{2,18},{18,2},{3,19},{19,3},{4,20},{20... | collective-permute-start | bytes 196616 | tf_op jit(solution)/shard_map/ppermute | solution.py:129
  11.3 2.2 %collective-permute-done.2 = bf16[32,1024]{1,0:T(8,128)(2,1)S(1)} collective-permute-done((bf16[32,1024]{1,0:T(8,128)(2,1)S(1)}, bf16[32,1024]{1,0:T(8,128)(2,1)S(1)}, u32[]{:S(2)}, u32[]{:S(2)}) %collective-permute-start.2) | collective-permute-done | bytes 65568 | tf_op jit(solution)/shard_map/ppermute | solution.py:129
  15.8 2.2 %reshape.262 = bf16[16,12,2048]{2,1,0:T(8,128)(2,1)} reshape(bf16[192,2048]{1,0:T(8,128)(2,1)} %convolution_convert_fusion) | data formatting | bytes 1572864 | tf_op jit(solution)/shard_map/reshape | solution.py:219
  18.0 6.4 %all-to-all-start = ((bf16[16,12,2048]{2,1,0:T(8,128)(2,1)}), bf16[16,12,2048]{2,1,0:T(8,128)(2,1)}, u32[]{:S(2)}, u32[]{:S(2)}) async-start(bf16[16,12,2048]{2,1,0:T(8,128)(2,1)} %reshape.262), calls=%async_computation | async-start | bytes 2097152 | tf_op jit(solution)/shard_map/all_to_all | solution.py:220
  25.3 1.5 %collective-permute-start.3 = (f32[32,8]{0,1:T(8,128)S(1)}, f32[32,8]{0,1:T(8,128)S(1)}, u32[]{:S(2)}, u32[]{:S(2)}) collective-permute-start(f32[32,8]{0,1:T(8,128)S(1)} %fusion.80), channel_id=1, source_target_pairs={{0,16},{16,0},{1,17},{17,1},{2,18},{18,2},{3,19},{19,3},{4,20},{20... | collective-permute-start | bytes 3080 | tf_op jit(solution)/shard_map/ppermute | solution.py:129
  26.9 2.7 %fusion.81 = f32[32,704]{1,0:T(8,128)S(1)} fusion(bf16[32,2048]{1,0:T(8,128)(2,1)S(1)} %multiply_convert_fusion.1, bf16[704,2048]{1,0:T(8,128)(2,1)} %param.24), kind=kOutput, calls=%fused_computation.105 | convolution fusion | flops 92274688 | bytes 3104768 | tf_op jit(solution)/shard_map/dot_general | solution.py:16
  31.3 16.1 %all-to-all-done = bf16[16,12,2048]{2,1,0:T(8,128)(2,1)} async-done(((bf16[16,12,2048]{2,1,0:T(8,128)(2,1)}), bf16[16,12,2048]{2,1,0:T(8,128)(2,1)}, u32[]{:S(2)}, u32[]{:S(2)}) %all-to-all-start) | async-done | bytes 786464 | tf_op jit(solution)/shard_map/all_to_all | solution.py:220
  47.4 2.1 %reshape.263 = bf16[192,2048]{1,0:T(8,128)(2,1)} reshape(bf16[16,12,2048]{2,1,0:T(8,128)(2,1)} %all-to-all-done) | data formatting | bytes 1572864 | tf_op jit(solution)/shard_map/reshape | solution.py:221
  51.0 3.1 %fusion.6 = f32[192,704]{1,0:T(8,128)S(1)} fusion(bf16[192,2048]{1,0:T(8,128)(2,1)} %reshape.263, bf16[1,704,2048]{2,1,0:T(8,128)(2,1)} %param.21), kind=kOutput, calls=%fused_computation.7 | convolution fusion | flops 553648128 | bytes 4210688 | tf_op jit(solution)/shard_map/dot_general | solution.py:16
  57.4 12.6 %collective-permute-done.4 = bf16[192,2048]{1,0:T(8,128)(2,1)S(1)} collective-permute-done((bf16[192,2048]{1,0:T(8,128)(2,1)}, bf16[192,2048]{1,0:T(8,128)(2,1)S(1)}, u32[]{:S(2)}, u32[]{:S(2)}) %collective-permute-start.4) | collective-permute-done | bytes 786464 | tf_op jit(solution)/shard_map/ppermute | solution.py:129
  71.1 1.8 %multiply_convert_fusion = bf16[192,704]{1,0:T(8,128)(2,1)} fusion(f32[192,704]{1,0:T(8,128)S(1)} %fusion.4, bf16[192,2048]{1,0:T(8,128)(2,1)S(1)} %collective-permute-done.4, bf16[1,704,2048]{2,1,0:T(8,128)(2,1)S(1)} %copy-done.10), kind=kOutput, calls=%fused_computation.41 | convolution fusion | flops 554459136 | bytes 4481024 | tf_op jit(solution)/shard_map/dot_general | solution.py:16
  78.7 3.8 %collective-permute-done.5 = bf16[192,704]{1,0:T(8,128)(2,1)} collective-permute-done((bf16[192,704]{1,0:T(8,128)(2,1)}, bf16[192,704]{1,0:T(8,128)(2,1)}, u32[]{:S(2)}, u32[]{:S(2)}) %collective-permute-start.5) | collective-permute-done | bytes 270368 | tf_op jit(solution)/shard_map/ppermute | solution.py:129
  82.5 2.5 %fusion.38 = bf16[192,1024]{1,0:T(8,128)(2,1)} fusion(f32[192,1024]{1,0:T(8,128)} %fusion.18, bf16[192,704]{1,0:T(8,128)(2,1)} %collective-permute-done.5, bf16[2,704,1024]{2,1,0:T(8,128)(2,1)S(1)} %bitcast.84, s32[]{:T(128)S(6)} %select_n.125), kind=kOutput, calls=%fused_computation.32 | convolution fusion | flops 277217280 | bytes 2891780 | tf_op jit(solution)/shard_map/dot_general | solution.py:243
  85.0 1.9 %reshape.264 = bf16[16,12,1024]{2,1,0:T(8,128)(2,1)} reshape(bf16[192,1024]{1,0:T(8,128)(2,1)} %fusion.38) | data formatting | bytes 786432 | tf_op jit(solution)/shard_map/reshape | solution.py:254
  86.9 2.2 %pad_maximum_fusion = bf16[16,24,1024]{2,1,0:T(8,128)(2,1)} fusion(bf16[16,12,1024]{2,1,0:T(8,128)(2,1)S(1)} %reshape.265, bf16[16,12,1024]{2,1,0:T(8,128)(2,1)} %reshape.264), kind=kLoop, calls=%fused_computation.40 | loop fusion | flops 1572864 | bytes 1572864 | tf_op jit(solution)/shard_map/concatenate | solution.py:252
  89.0 6.6 %all-to-all-start.1 = ((bf16[16,24,1024]{2,1,0:T(8,128)(2,1)}), bf16[16,24,1024]{2,1,0:T(8,128)(2,1)}, u32[]{:S(2)}, u32[]{:S(2)}) async-start(bf16[16,24,1024]{2,1,0:T(8,128)(2,1)} %pad_maximum_fusion), calls=%async_computation.1 | async-start | bytes 1572864 | tf_op jit(solution)/shard_map/all_to_all | solution.py:259
  95.6 1.7 %fusion.10 = f32[32,1024]{1,0:T(8,128)S(1)} fusion(bf16[32,704]{1,0:T(8,128)(2,1)S(1)} %fusion.48, bf16[2,704,1024]{2,1,0:T(8,128)(2,1)} %bitcast.87, s32[]{:T(128)S(6)} %select_n.124), kind=kOutput, calls=%fused_computation.12 | convolution fusion | flops 46137344 | bytes 1617924 | tf_op jit(solution)/shard_map/dot_general | solution.py:249
  97.5 1.7 %gather_fusion = f32[192]{0:T(256)S(1)} fusion(f32[32,16]{0,1:T(8,128)S(1)} %maximum_select_fusion.2, s32[192]{0:T(256)S(1)} %reshape.268), kind=kCustom, calls=%fused_computation | custom fusion | bytes 3072 | tf_op jit(solution)/shard_map/jit(take_along_axis)/gather | solution.py:191
  100.1 1.7 %fusion.45 = f32[32,1024]{1,0:T(8,128)S(1)} fusion(f32[32,1024]{1,0:T(8,128)S(1)} %fusion.10, bf16[2,704,1024]{2,1,0:T(8,128)(2,1)} %bitcast.88, s32[]{:T(128)S(6)} %select_n.125, bf16[16,704]{1,0:T(8,128)(2,1)S(1)} %get-tuple-element.13, bf16[16,704]{1,0:T(8,128)(2,1)S(1)} %get-tuple-element.12), kind=kOutput, calls=%fused_computation.36 | convolution fusion | flops 46260224 | bytes 1748996 | tf_op jit(solution)/shard_map/dot_general | solution.py:249
  101.8 12.6 %all-to-all-done.1 = bf16[16,24,1024]{2,1,0:T(8,128)(2,1)} async-done(((bf16[16,24,1024]{2,1,0:T(8,128)(2,1)}), bf16[16,24,1024]{2,1,0:T(8,128)(2,1)}, u32[]{:S(2)}, u32[]{:S(2)}) %all-to-all-start.1) | async-done | bytes 786464 | tf_op jit(solution)/shard_map/all_to_all | solution.py:259
  115.8 1.6 %collective-permute-start.8 = (f32[16,1024]{1,0:T(8,128)S(1)}, f32[16,1024]{1,0:T(8,128)S(1)}, u32[]{:S(2)}, u32[]{:S(2)}) collective-permute-start(f32[16,1024]{1,0:T(8,128)S(1)} %get-tuple-element.8), channel_id=1, source_target_pairs={{0,16},{16,0},{1,17},{17,1},{2,18},{18,2},{3,19},{19,3},{4,20},{20... | collective-permute-start | bytes 196616 | tf_op jit(solution)/shard_map/ppermute | solution.py:129
  117.4 2.7 %collective-permute-done.8 = f32[16,1024]{1,0:T(8,128)S(1)} collective-permute-done((f32[16,1024]{1,0:T(8,128)S(1)}, f32[16,1024]{1,0:T(8,128)S(1)}, u32[]{:S(2)}, u32[]{:S(2)}) %collective-permute-start.8) | collective-permute-done | bytes 65568 | tf_op jit(solution)/shard_map/ppermute | solution.py:129
  (94 shorter events, 24.0 us)
Async XLA Ops:
  0.6 55.4 %copy-start = (bf16[1,1408,1024]{2,1,0:T(8,128)(2,1)S(1)}, bf16[1,1408,1024]{2,1,0:T(8,128)(2,1)}, u32[]{:S(2)}) copy-start(bf16[1,1408,1024]{2,1,0:T(8,128)(2,1)} %param.23) | copy-start | bytes 8650756
  0.6 12.9 %copy-start.6 = (bf16[1,1,16,2048]{3,2,1,0:T(8,128)(2,1)S(1)}, bf16[1,1,16,2048]{3,2,1,0:T(8,128)(2,1)}, u32[]{:S(2)}) copy-start(bf16[1,1,16,2048]{3,2,1,0:T(8,128)(2,1)} %param.15) | copy-start | bytes 196612
  0.7 13.8 %copy-start.8 = (f32[2048]{0:T(1024)S(1)}, f32[2048]{0:T(1024)}, u32[]{:S(2)}) copy-start(f32[2048]{0:T(1024)} %param.17) | copy-start | bytes 24580
  0.7 6.4 %collective-permute-start.1 = (bf16[16,1024]{1,0:T(8,128)(2,1)}, bf16[16,1024]{1,0:T(8,128)(2,1)S(1)}, u32[]{:S(2)}, u32[]{:S(2)}) collective-permute-start(bf16[16,1024]{1,0:T(8,128)(2,1)} %bitcast.96), channel_id=1, source_target_pairs={{0,16},{16,0},{1,17},{17,1},{2,18},{18,2},{3,19},{19,3},{4,20},{20... | collective-permute-start | bytes 98312 | tf_op jit(solution)/shard_map/ppermute | solution.py:129
  3.7 9.8 %collective-permute-start = (bf16[16,2048]{1,0:T(8,128)(2,1)}, bf16[16,2048]{1,0:T(8,128)(2,1)S(1)}, u32[]{:S(2)}, u32[]{:S(2)}) collective-permute-start(bf16[16,2048]{1,0:T(8,128)(2,1)} %bitcast.94), channel_id=1, source_target_pairs={{0,16},{16,0},{1,17},{17,1},{2,18},{18,2},{3,19},{19,3},{4,20},{20... | collective-permute-start | bytes 196616 | tf_op jit(solution)/shard_map/ppermute | solution.py:129
  9.2 4.3 %collective-permute-start.2 = (bf16[32,1024]{1,0:T(8,128)(2,1)S(1)}, bf16[32,1024]{1,0:T(8,128)(2,1)S(1)}, u32[]{:S(2)}, u32[]{:S(2)}) collective-permute-start(bf16[32,1024]{1,0:T(8,128)(2,1)S(1)} %convolution_convert_fusion.1), channel_id=1, source_target_pairs={{0,16},{16,0},{1,17},{17,1},{2,18},{18,2},{3,19},{19,3},{4,20},{20... | collective-permute-start | bytes 196616 | tf_op jit(solution)/shard_map/ppermute | solution.py:129
  13.5 11.6 %copy-start.7 = (bf16[2048,8]{0,1:T(8,128)(2,1)S(1)}, bf16[2048,8]{0,1:T(8,128)(2,1)}, u32[]{:S(2)}) copy-start(bf16[2048,8]{0,1:T(8,128)(2,1)} %param.18) | copy-start | bytes 98308
  13.7 0.7 copy-start.4
  18.0 29.4 %all-to-all-start = ((bf16[16,12,2048]{2,1,0:T(8,128)(2,1)}), bf16[16,12,2048]{2,1,0:T(8,128)(2,1)}, u32[]{:S(2)}, u32[]{:S(2)}) async-start(bf16[16,12,2048]{2,1,0:T(8,128)(2,1)} %reshape.262), calls=%async_computation | async-start | bytes 2097152 | tf_op jit(solution)/shard_map/all_to_all | solution.py:220
  24.5 6.1 %copy-start.9 = (pred[32]{0:T(512)(128)(4,1)}, pred[32]{0:T(512)(128)(4,1)S(1)}, u32[]{:S(2)}) copy-start(pred[32]{0:T(512)(128)(4,1)S(1)} %lt.68) | copy-start | bytes 100
  25.2 4.4 %copy-start.3 = (bf16[704,2048]{1,0:T(8,128)(2,1)S(1)}, bf16[704,2048]{1,0:T(8,128)(2,1)}, u32[]{:S(2)}) copy-start(bf16[704,2048]{1,0:T(8,128)(2,1)} %param.25) | copy-start | bytes 8650756
  25.3 72.0 %collective-permute-start.3 = (f32[32,8]{0,1:T(8,128)S(1)}, f32[32,8]{0,1:T(8,128)S(1)}, u32[]{:S(2)}, u32[]{:S(2)}) collective-permute-start(f32[32,8]{0,1:T(8,128)S(1)} %fusion.80), channel_id=1, source_target_pairs={{0,16},{16,0},{1,17},{17,1},{2,18},{18,2},{3,19},{19,3},{4,20},{20... | collective-permute-start | bytes 3080 | tf_op jit(solution)/shard_map/ppermute | solution.py:129
  30.5 69.5 %collective-permute-start.7 = (bf16[32,704]{1,0:T(8,128)(2,1)S(1)}, bf16[32,704]{1,0:T(8,128)(2,1)S(1)}, u32[]{:S(2)}, u32[]{:S(2)}) collective-permute-start(bf16[32,704]{1,0:T(8,128)(2,1)S(1)} %fusion.48), channel_id=1, source_target_pairs={{0,16},{16,0},{1,17},{17,1},{2,18},{18,2},{3,19},{19,3},{4,20},{20... | collective-permute-start | bytes 135176 | tf_op jit(solution)/shard_map/ppermute | solution.py:129
  49.5 4.6 %copy-start.2 = (bf16[192,2048]{1,0:T(8,128)(2,1)S(1)}, bf16[192,2048]{1,0:T(8,128)(2,1)}, u32[]{:S(2)}) copy-start(bf16[192,2048]{1,0:T(8,128)(2,1)} %reshape.263) | copy-start | bytes 2359300
  49.5 4.6 %copy-start.10 = (bf16[1,704,2048]{2,1,0:T(8,128)(2,1)S(1)}, bf16[1,704,2048]{2,1,0:T(8,128)(2,1)}, u32[]{:S(2)}) copy-start(bf16[1,704,2048]{2,1,0:T(8,128)(2,1)} %param.22) | copy-start | bytes 8650756
  49.5 20.5 %collective-permute-start.4 = (bf16[192,2048]{1,0:T(8,128)(2,1)}, bf16[192,2048]{1,0:T(8,128)(2,1)S(1)}, u32[]{:S(2)}, u32[]{:S(2)}) collective-permute-start(bf16[192,2048]{1,0:T(8,128)(2,1)} %reshape.263), channel_id=1, source_target_pairs={{0,16},{16,0},{1,17},{17,1},{2,18},{18,2},{3,19},{19,3},{4,20},{20... | collective-permute-start | bytes 2359304 | tf_op jit(solution)/shard_map/ppermute | solution.py:129
  54.1 15.9 %copy-start.1 = (bf16[1,704,2048]{2,1,0:T(8,128)(2,1)S(1)}, bf16[1,704,2048]{2,1,0:T(8,128)(2,1)}, u32[]{:S(2)}) copy-start(bf16[1,704,2048]{2,1,0:T(8,128)(2,1)} %param.21) | copy-start | bytes 8650756
  55.2 21.2 %collective-permute-start.6 = (bf16[192,704]{1,0:T(8,128)(2,1)S(1)}, bf16[192,704]{1,0:T(8,128)(2,1)S(1)}, u32[]{:S(2)}, u32[]{:S(2)}) collective-permute-start(bf16[192,704]{1,0:T(8,128)(2,1)S(1)} %fusion.41), channel_id=1, source_target_pairs={{0,16},{16,0},{1,17},{17,1},{2,18},{18,2},{3,19},{19,3},{4,20},{20... | collective-permute-start | bytes 811016 | tf_op jit(solution)/shard_map/ppermute | solution.py:129
  72.8 9.7 %collective-permute-start.5 = (bf16[192,704]{1,0:T(8,128)(2,1)}, bf16[192,704]{1,0:T(8,128)(2,1)}, u32[]{:S(2)}, u32[]{:S(2)}) collective-permute-start(bf16[192,704]{1,0:T(8,128)(2,1)} %multiply_convert_fusion), channel_id=1, source_target_pairs={{0,16},{16,0},{1,17},{17,1},{2,18},{18,2},{3,19},{19,3},{4,20},{20... | collective-permute-start | bytes 811016 | tf_op jit(solution)/shard_map/ppermute | solution.py:129
  89.0 25.4 %all-to-all-start.1 = ((bf16[16,24,1024]{2,1,0:T(8,128)(2,1)}), bf16[16,24,1024]{2,1,0:T(8,128)(2,1)}, u32[]{:S(2)}, u32[]{:S(2)}) async-start(bf16[16,24,1024]{2,1,0:T(8,128)(2,1)} %pad_maximum_fusion), calls=%async_computation.1 | async-start | bytes 1572864 | tf_op jit(solution)/shard_map/all_to_all | solution.py:259
  99.2 21.0 %copy-start.5 = (f32[32,2048]{1,0:T(8,128)S(1)}, f32[32,2048]{1,0:T(8,128)}, u32[]{:S(2)}) copy-start(f32[32,2048]{1,0:T(8,128)} %copy-done.4) | copy-start | bytes 786436
  115.8 4.3 %collective-permute-start.8 = (f32[16,1024]{1,0:T(8,128)S(1)}, f32[16,1024]{1,0:T(8,128)S(1)}, u32[]{:S(2)}, u32[]{:S(2)}) collective-permute-start(f32[16,1024]{1,0:T(8,128)S(1)} %get-tuple-element.8), channel_id=1, source_target_pairs={{0,16},{16,0},{1,17},{17,1},{2,18},{18,2},{3,19},{19,3},{4,20},{20... | collective-permute-start | bytes 196616 | tf_op jit(solution)/shard_map/ppermute | solution.py:129

commit v10 on v9

--- a/solution.py
+++ b/solution.py
@@ -213,19 +213,21 @@
         block_live[0], block_experts[0] * capacity + position[0], own_total
     ).reshape(row_count, top_count)
     own_hit = own_target[:, :, None] == jnp.arange(own_total, dtype=jnp.int32)[None, None, :]
-    fill = jnp.any(own_hit, axis=1).astype(jnp.bfloat16)
+    fill = jnp.any(own_hit, axis=1).astype(jnp.bfloat16).reshape(row_count, experts, capacity)
     outgoing = lax.dot_general(
         fill, column[:row_count], (((0,), (0,)), ((), ())), preferred_element_type=jnp.float32
-    ).astype(jnp.bfloat16).reshape(experts, capacity, column.shape[1])
+    ).astype(jnp.bfloat16)
     slot_own = lax.all_to_all(outgoing, "expert", split_axis=0, concat_axis=0, tiled=True)
-    slot_own = slot_own.reshape(-1, slot_own.shape[-1])
     slot_other = swap_pair(slot_own)
-    hidden_own = (jax.nn.silu(by_rows(slot_own, gate_local)) * by_rows(slot_own, up_local)).astype(
-        jnp.bfloat16
-    )
+    by_width = (((2,), (1,)), ((), ()))
+    hidden_own = (
+        jax.nn.silu(lax.dot_general(slot_own, gate_local, by_width, preferred_element_type=jnp.float32))
+        * lax.dot_general(slot_own, up_local, by_width, preferred_element_type=jnp.float32)
+    ).astype(jnp.bfloat16)
     hidden_own_peer = swap_pair(hidden_own)
     hidden_other = (
-        jax.nn.silu(by_rows(slot_other, gate_local)) * by_rows(slot_other, up_local)
+        jax.nn.silu(lax.dot_general(slot_other, gate_local, by_width, preferred_element_type=jnp.float32))
+        * lax.dot_general(slot_other, up_local, by_width, preferred_element_type=jnp.float32)
     ).astype(jnp.bfloat16)
     hidden_other_peer = swap_pair(hidden_other)
     shared_gate_value = by_rows(column, shared_gate)
@@ -233,36 +235,32 @@
     shared_hidden = (jax.nn.silu(shared_gate_value) * shared_up_value).astype(jnp.bfloat16)
     shared_peer = halves_swapped(swap_pair(shared_hidden))
 
-    unit_count = hidden_own.shape[1]
+    unit_count = hidden_own.shape[2]
     down_blocks = down_local.reshape(groups, unit_count, column_width)
     shared_blocks = shared_down.reshape(groups, unit_count, column_width)
     down_mine = lax.dynamic_index_in_dim(down_blocks, me, 0, keepdims=False)
     down_peer = lax.dynamic_index_in_dim(down_blocks, 1 - me, 0, keepdims=False)
     shared_mine = lax.dynamic_index_in_dim(shared_blocks, me, 0, keepdims=False)
     shared_other = lax.dynamic_index_in_dim(shared_blocks, 1 - me, 0, keepdims=False)
-    out_own = jnp.dot(hidden_own, down_mine, preferred_element_type=jnp.float32) + jnp.dot(
-        hidden_other_peer, down_peer, preferred_element_type=jnp.float32
-    )
-    out_other = jnp.dot(hidden_other, down_mine, preferred_element_type=jnp.float32) + jnp.dot(
-        hidden_own_peer, down_peer, preferred_element_type=jnp.float32
-    )
+    by_units = (((2,), (0,)), ((), ()))
+    out_own = lax.dot_general(
+        hidden_own, down_mine, by_units, preferred_element_type=jnp.float32
+    ) + lax.dot_general(hidden_other_peer, down_peer, by_units, preferred_element_type=jnp.float32)
+    out_other = lax.dot_general(
+        hidden_other, down_mine, by_units, preferred_element_type=jnp.float32
+    ) + lax.dot_general(hidden_own_peer, down_peer, by_units, preferred_element_type=jnp.float32)
     shared = jnp.dot(shared_hidden, shared_mine, preferred_element_type=jnp.float32) + jnp.dot(
         shared_peer, shared_other, preferred_element_type=jnp.float32
     )
-    expert_out = jnp.concatenate(
-        [
-            out_own.astype(jnp.bfloat16).reshape(experts, capacity, column_width),
-            out_other.astype(jnp.bfloat16).reshape(experts, capacity, column_width),
-        ],
-        axis=1,
-    )
-    returned = lax.all_to_all(
-        expert_out, "expert", split_axis=0, concat_axis=0, tiled=True
-    ).reshape(slot_total, column_width)
+    expert_out = jnp.stack([out_own.astype(jnp.bfloat16), out_other.astype(jnp.bfloat16)], axis=1)
+    returned = lax.all_to_all(expert_out, "expert", split_axis=0, concat_axis=0, tiled=True)
     combine = jnp.sum(
         jnp.where(slot_hit, weights[:, :, None], jnp.zeros((), jnp.bfloat16)), axis=1
     ).astype(jnp.bfloat16)
-    routed = jnp.dot(combine, returned, preferred_element_type=jnp.float32)
+    combine = combine.reshape(rows_all, experts, groups, capacity)
+    routed = lax.dot_general(
+        combine, returned, (((1, 2, 3), (0, 1, 2)), ((), ())), preferred_element_type=jnp.float32
+    )
     combined = jnp.where(row_live[:, None], routed + shared, 0.0)
     summed = in_axis_order(first, combined[:row_count], swap_pair(combined[row_count:]), 1)
     stream_sum = stream_in + summed

time: 123 us -> 117 us (0.951)
  matrix products: 25.5 us -> 19.6 us
  waiting for transfers between devices: 50.6 us -> 53.4 us
  other arithmetic: 5.81 us -> 3.88 us
    reshape x4 -> x3, local copies, waits for them, and re-layouts: 7.24 us -> 0.36 us  [the longest x2 0.32 us: shards_pair(): jnp.any(own_hit, axis=1).astype(jnp.bfloat16)]
    dot_general x6 -> x2, matrix products: 10.6 us -> 4.26 us  [by_rows(): lax.dot_general(left, weight_rows, (((1,), (1,)), ((), ())), preferred_el...]
    ppermute x9, waiting for transfers between devices: 21.9 us -> 26.2 us  [swap_pair(): return lax.ppermute(x, 'dp', [(0, 1), (1, 0)])]
    concatenate x1 -> x0, other arithmetic: 2.16 us -> none  [shards_pair(): jnp.concatenate([out_own.astype(jnp.bfloat16).reshape(experts, capacity,...]
    all_to_all x0 -> x1, local copies, waits for them, and re-layouts: none -> 1.81 us  [shards_pair(): lax.all_to_all(outgoing, 'expert', split_axis=0, concat_axis=0, tiled=True)]
    another operation x0 -> x1, local copies, waits for them, and re-layouts: none -> 1.7 us  [shards_pair(): jnp.stack([out_own.astype(jnp.bfloat16), out_other.astype(jnp.bfloat16)],...]
    convert_element_type x0 -> x1, local copies, waits for them, and re-layouts: none -> 1.49 us  [shards_pair(): outgoing = lax.dot_general(fill, column[:row_count], (((0,), (0,)), ((),...]
    dot_general x5 -> x9, matrix products: 8 us -> 9.34 us  [the longest x1 2.84 us: shards_pair(): lax.dot_general(slot_own, gate_local, by_width, preferred_element_type=jn...]
  transfers between devices with their start and end apart: 11 -> 11, of which waited for: 7 -> 7; matrix products, arithmetic and copies ran while one was open for 30% -> 25% of each run, Pallas kernels for 0% -> 0%
where the time goes in v10:
time: 117 us; the launch traced here: 116 us
  waiting for transfers between devices  53.4 us (46%)
  starting transfers between devices  25.7 us (22%)
  matrix products  19.6 us (17%)
  local copies, waits for them, and re-layouts  12.4 us (11%)
  other arithmetic  3.88 us (3%)
    ppermute x9, waiting for transfers between devices, swap_pair(): return lax.ppermute(x, 'dp', [(0, 1), (1, 0)])  26.2 us
    all_to_all x1, waiting for transfers between devices, shards_pair(): lax.all_to_all(outgoing, 'expert', split_axis=0, concat_axis=0, tiled=True)  15.5 us
    ppermute x9, starting transfers between devices, swap_pair(): return lax.ppermute(x, 'dp', [(0, 1), (1, 0)])  12.7 us
    all_to_all x1, waiting for transfers between devices, shards_pair(): lax.all_to_all(expert_out, 'expert', split_axis=0, concat_axis=0, tiled=T...  11.6 us
    all_to_all x1, starting transfers between devices, shards_pair(): lax.all_to_all(expert_out, 'expert', split_axis=0, concat_axis=0, tiled=T...  6.6 us
    all_to_all x1, starting transfers between devices, shards_pair(): lax.all_to_all(outgoing, 'expert', split_axis=0, concat_axis=0, tiled=True)  6.39 us
    dot_general x2, matrix products, by_rows(): lax.dot_general(left, weight_rows, (((1,), (1,)), ((), ())), preferred_el...  4.26 us
    dot_general x1, matrix products, shards_pair(): lax.dot_general(slot_own, gate_local, by_width, preferred_element_type=jn...  2.84 us
  transfers between devices with their start and end apart: 11, of which 7 were waited for; matrix products, arithmetic and copies ran while one was open for 25% of the time, Pallas kernels for 0%

profile of v10, /device:TPU:0, one launch (start us, length us, event | category | flops | bytes accessed | tf_op | source)
XLA Modules:
  0.0 115.9 jit_solution(9066037283254488958)
XLA Ops:
  0.7 3.0 %collective-permute-start.1 = (bf16[16,1024]{1,0:T(8,128)(2,1)}, bf16[16,1024]{1,0:T(8,128)(2,1)S(1)}, u32[]{:S(2)}, u32[]{:S(2)}) collective-permute-start(bf16[16,1024]{1,0:T(8,128)(2,1)} %bitcast.119), channel_id=1, source_target_pairs={{0,16},{16,0},{1,17},{17,1},{2,18},{18,2},{3,19},{19,3},{4,20},{20... | collective-permute-start | bytes 98312 | tf_op jit(solution)/shard_map/ppermute | solution.py:129
  7.6 2.1 %convolution_convert_fusion.1 = bf16[32,1024]{1,0:T(8,128)(2,1)S(1)} fusion(bf16[1024,1024]{1,0:T(8,128)(2,1)} %param.16, bf16[16,1024]{1,0:T(8,128)(2,1)S(1)} %collective-permute-done.1, bf16[16,1024]{1,0:T(8,128)(2,1)} %bitcast.120), kind=kOutput, calls=%fused_computation.41 | convolution fusion | flops 67272704 | bytes 2228224 | tf_op jit(solution)/shard_map/dot_general | solution.py:176
  9.7 2.0 %collective-permute-start.2 = (bf16[32,1024]{1,0:T(8,128)(2,1)S(1)}, bf16[32,1024]{1,0:T(8,128)(2,1)S(1)}, u32[]{:S(2)}, u32[]{:S(2)}) collective-permute-start(bf16[32,1024]{1,0:T(8,128)(2,1)S(1)} %convolution_convert_fusion.1), channel_id=1, source_target_pairs={{0,16},{16,0},{1,17},{17,1},{2,18},{18,2},{3,19},{19,3},{4,20},{20... | collective-permute-start | bytes 196616 | tf_op jit(solution)/shard_map/ppermute | solution.py:129
  12.1 1.9 %collective-permute-done.2 = bf16[32,1024]{1,0:T(8,128)(2,1)S(1)} collective-permute-done((bf16[32,1024]{1,0:T(8,128)(2,1)S(1)}, bf16[32,1024]{1,0:T(8,128)(2,1)S(1)}, u32[]{:S(2)}, u32[]{:S(2)}) %collective-permute-start.2) | collective-permute-done | bytes 65568 | tf_op jit(solution)/shard_map/ppermute | solution.py:129
  17.7 6.4 %all-to-all-start = ((bf16[16,12,2048]{2,1,0:T(8,128)(2,1)}), bf16[16,12,2048]{2,1,0:T(8,128)(2,1)}, u32[]{:S(2)}, u32[]{:S(2)}) async-start(bf16[16,12,2048]{2,1,0:T(8,128)(2,1)} %copy.77), calls=%async_computation | async-start | bytes 2097152 | tf_op jit(solution)/shard_map/all_to_all | solution.py:220
  25.0 1.5 %collective-permute-start.3 = (f32[32,8]{0,1:T(8,128)S(1)}, f32[32,8]{0,1:T(8,128)S(1)}, u32[]{:S(2)}, u32[]{:S(2)}) collective-permute-start(f32[32,8]{0,1:T(8,128)S(1)} %fusion.87), channel_id=1, source_target_pairs={{0,16},{16,0},{1,17},{17,1},{2,18},{18,2},{3,19},{19,3},{4,20},{20... | collective-permute-start | bytes 3080 | tf_op jit(solution)/shard_map/ppermute | solution.py:129
  26.6 2.7 %fusion.88 = f32[32,704]{1,0:T(8,128)S(1)} fusion(bf16[32,2048]{1,0:T(8,128)(2,1)S(1)} %multiply_convert_fusion.1, bf16[704,2048]{1,0:T(8,128)(2,1)} %param.24), kind=kOutput, calls=%fused_computation.109 | convolution fusion | flops 92274688 | bytes 3104768 | tf_op jit(solution)/shard_map/dot_general | solution.py:16
  29.3 1.6 %fusion.55 = bf16[32,704]{1,0:T(8,128)(2,1)} fusion(bf16[32,2048]{1,0:T(8,128)(2,1)S(1)} %multiply_convert_fusion.1, bf16[704,2048]{1,0:T(8,128)(2,1)S(1)} %copy-done.2, f32[32,704]{1,0:T(8,128)S(1)} %fusion.88), kind=kOutput, calls=%fused_computation.42 | convolution fusion | flops 92409856 | bytes 3149824 | tf_op jit(solution)/shard_map/dot_general | solution.py:16
  31.5 15.5 %all-to-all-done = bf16[16,12,2048]{2,1,0:T(8,128)(2,1)} async-done(((bf16[16,12,2048]{2,1,0:T(8,128)(2,1)}), bf16[16,12,2048]{2,1,0:T(8,128)(2,1)}, u32[]{:S(2)}, u32[]{:S(2)}) %all-to-all-start) | async-done | bytes 786464 | tf_op jit(solution)/shard_map/all_to_all | solution.py:220
  47.1 1.8 %copy.78 = bf16[16,12,2048]{2,0,1:T(8,128)(2,1)S(1)} copy(bf16[16,12,2048]{2,1,0:T(8,128)(2,1)} %all-to-all-done) | data formatting | bytes 1572864 | tf_op jit(solution)/shard_map/all_to_all | solution.py:220
  48.9 1.6 %collective-permute-start.4 = (bf16[16,12,2048]{2,0,1:T(8,128)(2,1)S(1)}, bf16[16,12,2048]{2,0,1:T(8,128)(2,1)S(1)}, u32[]{:S(2)}, u32[]{:S(2)}) collective-permute-start(bf16[16,12,2048]{2,0,1:T(8,128)(2,1)S(1)} %copy.78), channel_id=1, source_target_pairs={{0,16},{16,0},{1,17},{17,1},{2,18},{18,2},{3,19},{19,3},{4,20},{20... | collective-permute-start | bytes 2359304 | tf_op jit(solution)/shard_map/ppermute | solution.py:129
  50.5 2.8 %fusion.6 = f32[16,12,704]{2,0,1:T(8,128)S(1)} fusion(bf16[16,12,2048]{2,0,1:T(8,128)(2,1)S(1)} %copy.78, bf16[1,704,2048]{2,1,0:T(8,128)(2,1)} %param.21), kind=kOutput, calls=%fused_computation.7 | convolution fusion | flops 553648128 | bytes 4210688 | tf_op jit(solution)/shard_map/dot_general | solution.py:224
  55.5 13.8 %collective-permute-done.4 = bf16[16,12,2048]{2,0,1:T(8,128)(2,1)S(1)} collective-permute-done((bf16[16,12,2048]{2,0,1:T(8,128)(2,1)S(1)}, bf16[16,12,2048]{2,0,1:T(8,128)(2,1)S(1)}, u32[]{:S(2)}, u32[]{:S(2)}) %collective-permute-start.4) | collective-permute-done | bytes 786464 | tf_op jit(solution)/shard_map/ppermute | solution.py:129
  71.3 1.6 %collective-permute-start.5 = (bf16[16,12,704]{2,0,1:T(8,128)(2,1)S(1)}, bf16[16,12,704]{2,0,1:T(8,128)(2,1)S(1)}, u32[]{:S(2)}, u32[]{:S(2)}) collective-permute-start(bf16[16,12,704]{2,0,1:T(8,128)(2,1)S(1)} %multiply_convert_fusion), channel_id=1, source_target_pairs={{0,16},{16,0},{1,17},{17,1},{2,18},{18,2},{3,19},{19,3},{4,20},{20... | collective-permute-start | bytes 811016 | tf_op jit(solution)/shard_map/ppermute | solution.py:129
  73.4 2.2 %collective-permute-done.6 = bf16[16,12,704]{2,0,1:T(8,128)(2,1)S(1)} collective-permute-done((bf16[16,12,704]{2,0,1:T(8,128)(2,1)S(1)}, bf16[16,12,704]{2,0,1:T(8,128)(2,1)S(1)}, u32[]{:S(2)}, u32[]{:S(2)}) %collective-permute-start.6) | collective-permute-done | bytes 270368 | tf_op jit(solution)/shard_map/ppermute | solution.py:129
  76.1 5.5 %collective-permute-done.5 = bf16[16,12,704]{2,0,1:T(8,128)(2,1)S(1)} collective-permute-done((bf16[16,12,704]{2,0,1:T(8,128)(2,1)S(1)}, bf16[16,12,704]{2,0,1:T(8,128)(2,1)S(1)}, u32[]{:S(2)}, u32[]{:S(2)}) %collective-permute-start.5) | collective-permute-done | bytes 270368 | tf_op jit(solution)/shard_map/ppermute | solution.py:129
  82.2 1.7 %copy.81 = bf16[16,2,12,1024]{3,1,2,0:T(2,128)(2,1)} copy(bf16[16,2,12,1024]{3,0,2,1:T(8,128)(2,1)S(1)} %pad_maximum_fusion) | data formatting | bytes 1572864 | tf_op jit(solution)/shard_map/stack | solution.py:255
  83.9 6.6 %all-to-all-start.1 = ((bf16[16,2,12,1024]{3,1,2,0:T(2,128)(2,1)}), bf16[16,2,12,1024]{3,1,2,0:T(2,128)(2,1)}, u32[]{:S(2)}, u32[]{:S(2)}) async-start(bf16[16,2,12,1024]{3,1,2,0:T(2,128)(2,1)} %copy.81), calls=%async_computation.1 | async-start | bytes 1572864 | tf_op jit(solution)/shard_map/all_to_all | solution.py:256
  90.5 1.7 %fusion.10 = f32[32,1024]{1,0:T(8,128)S(1)} fusion(bf16[32,704]{1,0:T(8,128)(2,1)} %fusion.55, bf16[2,704,1024]{2,1,0:T(8,128)(2,1)} %bitcast.110, s32[]{:T(128)S(6)} %select_n.124), kind=kOutput, calls=%fused_computation.12 | convolution fusion | flops 46137344 | bytes 1622020 | tf_op jit(solution)/shard_map/dot_general | solution.py:252
  92.4 1.7 %gather_fusion = f32[192]{0:T(256)S(1)} fusion(f32[32,16]{0,1:T(8,128)S(1)} %maximum_select_fusion.2, s32[192]{0:T(256)S(1)} %reshape.256), kind=kCustom, calls=%fused_computation | custom fusion | bytes 3072 | tf_op jit(solution)/shard_map/jit(take_along_axis)/gather | solution.py:191
  95.9 1.7 %fusion.52 = f32[32,1024]{1,0:T(8,128)S(1)} fusion(f32[32,1024]{1,0:T(8,128)S(1)} %fusion.10, bf16[2,704,1024]{2,1,0:T(8,128)(2,1)} %bitcast.111, s32[]{:T(128)S(6)} %select_n.125, bf16[16,704]{1,0:T(8,128)(2,1)S(1)} %get-tuple-element.13, bf16[16,704]{1,0:T(8,128)(2,1)S(1)} %get-tuple-element.12), kind=kOutput, calls=%fused_computation.39 | convolution fusion | flops 46260224 | bytes 1748996 | tf_op jit(solution)/shard_map/dot_general | solution.py:252
  97.6 11.6 %all-to-all-done.1 = bf16[16,2,12,1024]{3,1,2,0:T(2,128)(2,1)} async-done(((bf16[16,2,12,1024]{3,1,2,0:T(2,128)(2,1)}), bf16[16,2,12,1024]{3,1,2,0:T(2,128)(2,1)}, u32[]{:S(2)}, u32[]{:S(2)}) %all-to-all-start.1) | async-done | bytes 786464 | tf_op jit(solution)/shard_map/all_to_all | solution.py:256
  110.7 1.6 %collective-permute-start.8 = (f32[16,1024]{1,0:T(8,128)S(1)}, f32[16,1024]{1,0:T(8,128)S(1)}, u32[]{:S(2)}, u32[]{:S(2)}) collective-permute-start(f32[16,1024]{1,0:T(8,128)S(1)} %get-tuple-element.8), channel_id=1, source_target_pairs={{0,16},{16,0},{1,17},{17,1},{2,18},{18,2},{3,19},{19,3},{4,20},{20... | collective-permute-start | bytes 196616 | tf_op jit(solution)/shard_map/ppermute | solution.py:129
  112.3 2.7 %collective-permute-done.8 = f32[16,1024]{1,0:T(8,128)S(1)} collective-permute-done((f32[16,1024]{1,0:T(8,128)S(1)}, f32[16,1024]{1,0:T(8,128)S(1)}, u32[]{:S(2)}, u32[]{:S(2)}) %collective-permute-start.8) | collective-permute-done | bytes 65568 | tf_op jit(solution)/shard_map/ppermute | solution.py:129
  (101 shorter events, 19.5 us)
Async XLA Ops:
  0.6 54.3 %copy-start = (bf16[1,1408,1024]{2,1,0:T(8,128)(2,1)S(1)}, bf16[1,1408,1024]{2,1,0:T(8,128)(2,1)}, u32[]{:S(2)}) copy-start(bf16[1,1408,1024]{2,1,0:T(8,128)(2,1)} %param.23) | copy-start | bytes 8650756
  0.6 14.0 %copy-start.3 = (bf16[1,1,16,2048]{3,2,1,0:T(8,128)(2,1)S(1)}, bf16[1,1,16,2048]{3,2,1,0:T(8,128)(2,1)}, u32[]{:S(2)}) copy-start(bf16[1,1,16,2048]{3,2,1,0:T(8,128)(2,1)} %param.15) | copy-start | bytes 196612
  0.7 6.9 %collective-permute-start.1 = (bf16[16,1024]{1,0:T(8,128)(2,1)}, bf16[16,1024]{1,0:T(8,128)(2,1)S(1)}, u32[]{:S(2)}, u32[]{:S(2)}) collective-permute-start(bf16[16,1024]{1,0:T(8,128)(2,1)} %bitcast.119), channel_id=1, source_target_pairs={{0,16},{16,0},{1,17},{17,1},{2,18},{18,2},{3,19},{19,3},{4,20},{20... | collective-permute-start | bytes 98312 | tf_op jit(solution)/shard_map/ppermute | solution.py:129
  3.7 10.4 %collective-permute-start = (bf16[16,2048]{1,0:T(8,128)(2,1)}, bf16[16,2048]{1,0:T(8,128)(2,1)S(1)}, u32[]{:S(2)}, u32[]{:S(2)}) collective-permute-start(bf16[16,2048]{1,0:T(8,128)(2,1)} %bitcast.117), channel_id=1, source_target_pairs={{0,16},{16,0},{1,17},{17,1},{2,18},{18,2},{3,19},{19,3},{4,20},{20... | collective-permute-start | bytes 196616 | tf_op jit(solution)/shard_map/ppermute | solution.py:129
  6.1 0.5 copy-start.10
  7.6 8.1 %copy-start.6 = (f32[2048]{0:T(1024)S(1)}, f32[2048]{0:T(1024)}, u32[]{:S(2)}) copy-start(f32[2048]{0:T(1024)} %param.17) | copy-start | bytes 24580
  9.7 4.3 %collective-permute-start.2 = (bf16[32,1024]{1,0:T(8,128)(2,1)S(1)}, bf16[32,1024]{1,0:T(8,128)(2,1)S(1)}, u32[]{:S(2)}, u32[]{:S(2)}) collective-permute-start(bf16[32,1024]{1,0:T(8,128)(2,1)S(1)} %convolution_convert_fusion.1), channel_id=1, source_target_pairs={{0,16},{16,0},{1,17},{17,1},{2,18},{18,2},{3,19},{19,3},{4,20},{20... | collective-permute-start | bytes 196616 | tf_op jit(solution)/shard_map/ppermute | solution.py:129
  14.0 10.0 %copy-start.11 = (pred[2,16]{1,0:T(4,128)(4,1)S(1)}, pred[2,16]{1,0:T(4,128)(4,1)}, u32[]{:S(2)}) copy-start(pred[2,16]{1,0:T(4,128)(4,1)} %copy-done.10) | copy-start | bytes 100
  14.1 0.6 copy-start.4
  14.7 10.2 %copy-start.5 = (bf16[2048,8]{0,1:T(8,128)(2,1)S(1)}, bf16[2048,8]{0,1:T(8,128)(2,1)}, u32[]{:S(2)}) copy-start(bf16[2048,8]{0,1:T(8,128)(2,1)} %param.18) | copy-start | bytes 98308
  17.7 29.4 %all-to-all-start = ((bf16[16,12,2048]{2,1,0:T(8,128)(2,1)}), bf16[16,12,2048]{2,1,0:T(8,128)(2,1)}, u32[]{:S(2)}, u32[]{:S(2)}) async-start(bf16[16,12,2048]{2,1,0:T(8,128)(2,1)} %copy.77), calls=%async_computation | async-start | bytes 2097152 | tf_op jit(solution)/shard_map/all_to_all | solution.py:220
  24.2 6.7 %copy-start.8 = (pred[32]{0:T(512)(128)(4,1)}, pred[32]{0:T(512)(128)(4,1)S(1)}, u32[]{:S(2)}) copy-start(pred[32]{0:T(512)(128)(4,1)S(1)} %lt.68) | copy-start | bytes 100
  24.9 4.4 %copy-start.2 = (bf16[704,2048]{1,0:T(8,128)(2,1)S(1)}, bf16[704,2048]{1,0:T(8,128)(2,1)}, u32[]{:S(2)}) copy-start(bf16[704,2048]{1,0:T(8,128)(2,1)} %param.25) | copy-start | bytes 8650756
  25.0 67.2 %collective-permute-start.3 = (f32[32,8]{0,1:T(8,128)S(1)}, f32[32,8]{0,1:T(8,128)S(1)}, u32[]{:S(2)}, u32[]{:S(2)}) collective-permute-start(f32[32,8]{0,1:T(8,128)S(1)} %fusion.87), channel_id=1, source_target_pairs={{0,16},{16,0},{1,17},{17,1},{2,18},{18,2},{3,19},{19,3},{4,20},{20... | collective-permute-start | bytes 3080 | tf_op jit(solution)/shard_map/ppermute | solution.py:129
  30.8 64.3 %collective-permute-start.7 = (bf16[32,704]{1,0:T(8,128)(2,1)}, bf16[32,704]{1,0:T(8,128)(2,1)}, u32[]{:S(2)}, u32[]{:S(2)}) collective-permute-start(bf16[32,704]{1,0:T(8,128)(2,1)} %fusion.55), channel_id=1, source_target_pairs={{0,16},{16,0},{1,17},{17,1},{2,18},{18,2},{3,19},{19,3},{4,20},{20... | collective-permute-start | bytes 135176 | tf_op jit(solution)/shard_map/ppermute | solution.py:129
  47.1 6.3 %copy-start.12 = (bf16[1,704,2048]{2,1,0:T(8,128)(2,1)S(1)}, bf16[1,704,2048]{2,1,0:T(8,128)(2,1)}, u32[]{:S(2)}) copy-start(bf16[1,704,2048]{2,1,0:T(8,128)(2,1)} %param.22) | copy-start | bytes 8650756
  48.9 20.4 %collective-permute-start.4 = (bf16[16,12,2048]{2,0,1:T(8,128)(2,1)S(1)}, bf16[16,12,2048]{2,0,1:T(8,128)(2,1)S(1)}, u32[]{:S(2)}, u32[]{:S(2)}) collective-permute-start(bf16[16,12,2048]{2,0,1:T(8,128)(2,1)S(1)} %copy.78), channel_id=1, source_target_pairs={{0,16},{16,0},{1,17},{17,1},{2,18},{18,2},{3,19},{19,3},{4,20},{20... | collective-permute-start | bytes 2359304 | tf_op jit(solution)/shard_map/ppermute | solution.py:129
  53.3 15.9 %copy-start.1 = (bf16[1,704,2048]{2,1,0:T(8,128)(2,1)S(1)}, bf16[1,704,2048]{2,1,0:T(8,128)(2,1)}, u32[]{:S(2)}) copy-start(bf16[1,704,2048]{2,1,0:T(8,128)(2,1)} %param.21) | copy-start | bytes 8650756
  54.4 21.2 %collective-permute-start.6 = (bf16[16,12,704]{2,0,1:T(8,128)(2,1)S(1)}, bf16[16,12,704]{2,0,1:T(8,128)(2,1)S(1)}, u32[]{:S(2)}, u32[]{:S(2)}) collective-permute-start(bf16[16,12,704]{2,0,1:T(8,128)(2,1)S(1)} %fusion.41), channel_id=1, source_target_pairs={{0,16},{16,0},{1,17},{17,1},{2,18},{18,2},{3,19},{19,3},{4,20},{20... | collective-permute-start | bytes 811016 | tf_op jit(solution)/shard_map/ppermute | solution.py:129
  71.3 10.3 %collective-permute-start.5 = (bf16[16,12,704]{2,0,1:T(8,128)(2,1)S(1)}, bf16[16,12,704]{2,0,1:T(8,128)(2,1)S(1)}, u32[]{:S(2)}, u32[]{:S(2)}) collective-permute-start(bf16[16,12,704]{2,0,1:T(8,128)(2,1)S(1)} %multiply_convert_fusion), channel_id=1, source_target_pairs={{0,16},{16,0},{1,17},{17,1},{2,18},{18,2},{3,19},{19,3},{4,20},{20... | collective-permute-start | bytes 811016 | tf_op jit(solution)/shard_map/ppermute | solution.py:129
  83.9 25.4 %all-to-all-start.1 = ((bf16[16,2,12,1024]{3,1,2,0:T(2,128)(2,1)}), bf16[16,2,12,1024]{3,1,2,0:T(2,128)(2,1)}, u32[]{:S(2)}, u32[]{:S(2)}) async-start(bf16[16,2,12,1024]{3,1,2,0:T(2,128)(2,1)} %copy.81), calls=%async_computation.1 | async-start | bytes 1572864 | tf_op jit(solution)/shard_map/all_to_all | solution.py:256
  92.4 16.9 %copy-start.9 = (pred[32]{0:T(512)(128)(4,1)S(1)}, pred[32]{0:T(512)(128)(4,1)}, u32[]{:S(2)}) copy-start(pred[32]{0:T(512)(128)(4,1)} %copy-done.8) | copy-start | bytes 100
  94.1 21.1 %copy-start.7 = (f32[2048]{0:T(1024)S(1)}, f32[2048]{0:T(1024)}, u32[]{:S(2)}) copy-start(f32[2048]{0:T(1024)} %param.27) | copy-start | bytes 24580
  110.7 4.3 %collective-permute-start.8 = (f32[16,1024]{1,0:T(8,128)S(1)}, f32[16,1024]{1,0:T(8,128)S(1)}, u32[]{:S(2)}, u32[]{:S(2)}) collective-permute-start(f32[16,1024]{1,0:T(8,128)S(1)} %get-tuple-element.8), channel_id=1, source_target_pairs={{0,16},{16,0},{1,17},{17,1},{2,18},{18,2},{3,19},{19,3},{4,20},{20... | collective-permute-start | bytes 196616 | tf_op jit(solution)/shard_map/ppermute | solution.py:129

commit v11 on v4

--- a/solution.py
+++ b/solution.py
@@ -214,9 +214,9 @@
     ).astype(jnp.bfloat16).reshape(experts, groups * capacity, column.shape[1])
     slot_rows = lax.all_to_all(outgoing, "expert", split_axis=0, concat_axis=0, tiled=True)
     flattened = slot_rows.reshape(-1, slot_rows.shape[-1])
-    gate_value = by_rows(flattened, gate_local)
-    up_value = by_rows(flattened, up_local)
-    hidden = (jax.nn.silu(gate_value) * up_value).astype(jnp.bfloat16)
+    unit_total = gate_local.shape[0]
+    both = by_rows(flattened, jnp.concatenate([gate_local, up_local], axis=0))
+    hidden = (jax.nn.silu(both[:, :unit_total]) * both[:, unit_total:]).astype(jnp.bfloat16)
     hidden_peer = swap_pair(hidden)
     shared_gate_value = by_rows(column, shared_gate)
     shared_up_value = by_rows(column, shared_up)

time: 115 us -> 117 us (1.017)
  local copies, waits for them, and re-layouts: 5.49 us -> 7.57 us
  waiting for transfers between devices: 56.2 us -> 54.6 us
  other arithmetic: 3.81 us -> 5.08 us
    convert_element_type x0 -> x1, local copies, waits for them, and re-layouts: none -> 2.08 us  [shards_pair(): (jax.nn.silu(both[:, :unit_total]) * both[:, unit_total:]).astype(jnp.bfl...]
    ppermute x7, waiting for transfers between devices: 16.3 us -> 14.7 us  [swap_pair(): return lax.ppermute(x, 'dp', [(0, 1), (1, 0)])]
    convert_element_type x0 -> x1, other arithmetic: none -> 1.27 us  [shards_pair(): (jax.nn.silu(both[:, :unit_total]) * both[:, unit_total:]).astype(jnp.bfl...]
    dot_general x4 -> x3, matrix products: 11 us -> 11.2 us  [by_rows(): lax.dot_general(left, weight_rows, (((1,), (1,)), ((), ())), preferred_el...]
  transfers between devices with their start and end apart: 9 -> 9, of which waited for: 5 -> 5; matrix products, arithmetic and copies ran while one was open for 23% -> 25% of each run, Pallas kernels for 0% -> 0%
where the time goes in v11:
time: 117 us; the launch traced here: 116 us
  waiting for transfers between devices  54.6 us (47%)
  starting transfers between devices  25.7 us (22%)
  matrix products  22.6 us (19%)
  local copies, waits for them, and re-layouts  7.57 us (6%)
  other arithmetic  5.08 us (4%)
    all_to_all x1, waiting for transfers between devices, shards_pair(): lax.all_to_all(outgoing, 'expert', split_axis=0, concat_axis=0, tiled=True)  27.3 us
    ppermute x7, waiting for transfers between devices, swap_pair(): return lax.ppermute(x, 'dp', [(0, 1), (1, 0)])  14.7 us
    all_to_all x1, waiting for transfers between devices, shards_pair(): lax.all_to_all(expert_out, 'expert', split_axis=0, concat_axis=0, tiled=T...  12.6 us
    dot_general x3, matrix products, by_rows(): lax.dot_general(left, weight_rows, (((1,), (1,)), ((), ())), preferred_el...  11.2 us
    ppermute x7, starting transfers between devices, swap_pair(): return lax.ppermute(x, 'dp', [(0, 1), (1, 0)])  10.3 us
    all_to_all x1, starting transfers between devices, shards_pair(): lax.all_to_all(expert_out, 'expert', split_axis=0, concat_axis=0, tiled=T...  9 us
    all_to_all x1, starting transfers between devices, shards_pair(): lax.all_to_all(outgoing, 'expert', split_axis=0, concat_axis=0, tiled=True)  6.38 us
  transfers between devices with their start and end apart: 9, of which 5 were waited for; matrix products, arithmetic and copies ran while one was open for 25% of the time, Pallas kernels for 0%

profile of v11, /device:TPU:0, one launch (start us, length us, event | category | flops | bytes accessed | tf_op | source)
XLA Modules:
  0.0 116.5 jit_solution(7020241203351858283)
XLA Ops:
  0.7 3.0 %collective-permute-start.1 = (bf16[16,1024]{1,0:T(8,128)(2,1)}, bf16[16,1024]{1,0:T(8,128)(2,1)S(1)}, u32[]{:S(2)}, u32[]{:S(2)}) collective-permute-start(bf16[16,1024]{1,0:T(8,128)(2,1)} %bitcast.63), channel_id=1, source_target_pairs={{0,16},{16,0},{1,17},{17,1},{2,18},{18,2},{3,19},{19,3},{4,20},{20... | collective-permute-start | bytes 98312 | tf_op jit(solution)/shard_map/ppermute | solution.py:129
  7.4 2.1 %convolution_convert_fusion.1 = bf16[32,1024]{1,0:T(8,128)(2,1)S(1)} fusion(bf16[1024,1024]{1,0:T(8,128)(2,1)} %param.16, bf16[16,1024]{1,0:T(8,128)(2,1)S(1)} %collective-permute-done.1, bf16[16,1024]{1,0:T(8,128)(2,1)} %bitcast.64), kind=kOutput, calls=%fused_computation.24 | convolution fusion | flops 67272704 | bytes 2228224 | tf_op jit(solution)/shard_map/dot_general | solution.py:176
  9.5 2.0 %collective-permute-start.2 = (bf16[32,1024]{1,0:T(8,128)(2,1)S(1)}, bf16[32,1024]{1,0:T(8,128)(2,1)S(1)}, u32[]{:S(2)}, u32[]{:S(2)}) collective-permute-start(bf16[32,1024]{1,0:T(8,128)(2,1)S(1)} %convolution_convert_fusion.1), channel_id=1, source_target_pairs={{0,16},{16,0},{1,17},{17,1},{2,18},{18,2},{3,19},{19,3},{4,20},{20... | collective-permute-start | bytes 196616 | tf_op jit(solution)/shard_map/ppermute | solution.py:129
  11.6 2.2 %collective-permute-done.2 = bf16[32,1024]{1,0:T(8,128)(2,1)S(1)} collective-permute-done((bf16[32,1024]{1,0:T(8,128)(2,1)S(1)}, bf16[32,1024]{1,0:T(8,128)(2,1)S(1)}, u32[]{:S(2)}, u32[]{:S(2)}) %collective-permute-start.2) | collective-permute-done | bytes 65568 | tf_op jit(solution)/shard_map/ppermute | solution.py:129
  15.6 1.8 %convolution_convert_fusion = bf16[384,2048]{1,0:T(8,128)(2,1)} fusion(pred[32,384]{1,0:T(8,128)(4,1)S(1)} %fusion.21, bf16[32,2048]{1,0:T(8,128)(2,1)S(1)} %multiply_convert_fusion), kind=kOutput, calls=%fused_computation.5 | convolution fusion | flops 51118080 | bytes 1716224 | tf_op jit(solution)/shard_map/dot_general | solution.py:212
  17.4 6.4 %all-to-all-start = ((bf16[16,24,2048]{2,1,0:T(8,128)(2,1)}), bf16[16,24,2048]{2,1,0:T(8,128)(2,1)}, u32[]{:S(2)}, u32[]{:S(2)}) async-start(bf16[16,24,2048]{2,1,0:T(8,128)(2,1)} %bitcast.52), calls=%async_computation | async-start | bytes 3145728 | tf_op jit(solution)/shard_map/all_to_all | solution.py:215
  24.2 1.5 %collective-permute-start.3 = (f32[32,8]{0,1:T(8,128)S(1)}, f32[32,8]{0,1:T(8,128)S(1)}, u32[]{:S(2)}, u32[]{:S(2)}) collective-permute-start(f32[32,8]{0,1:T(8,128)S(1)} %fusion.50), channel_id=1, source_target_pairs={{0,16},{16,0},{1,17},{17,1},{2,18},{18,2},{3,19},{19,3},{4,20},{20... | collective-permute-start | bytes 3080 | tf_op jit(solution)/shard_map/ppermute | solution.py:129
  25.8 2.7 %fusion.51 = f32[32,704]{1,0:T(8,128)S(1)} fusion(bf16[32,2048]{1,0:T(8,128)(2,1)S(1)} %multiply_convert_fusion, bf16[704,2048]{1,0:T(8,128)(2,1)} %param.24), kind=kOutput, calls=%fused_computation.82 | convolution fusion | flops 92274688 | bytes 3104768 | tf_op jit(solution)/shard_map/dot_general | solution.py:16
  28.5 27.3 %all-to-all-done = bf16[16,24,2048]{2,1,0:T(8,128)(2,1)} async-done(((bf16[16,24,2048]{2,1,0:T(8,128)(2,1)}), bf16[16,24,2048]{2,1,0:T(8,128)(2,1)}, u32[]{:S(2)}, u32[]{:S(2)}) %all-to-all-start) | async-done | bytes 1572896 | tf_op jit(solution)/shard_map/all_to_all | solution.py:215
  55.8 5.8 %fusion = f32[384,1408]{1,0:T(8,128)S(1)} fusion(bf16[384,2048]{1,0:T(8,128)(2,1)} %bitcast.7, bf16[704,2048]{1,0:T(8,128)(2,1)} %bitcast.66, bf16[704,2048]{1,0:T(8,128)(2,1)} %bitcast.67), kind=kOutput, calls=%fused_computation.1 | convolution fusion | flops 2226126848 | bytes 9502720 | tf_op jit(solution)/shard_map/dot_general | solution.py:16
  61.6 1.3 %fusion.15 = bf16[384,704]{1,0:T(8,128)(2,1)} fusion(f32[384,1408]{1,0:T(8,128)S(1)} %fusion), kind=kLoop, calls=%fused_computation.19 | loop fusion | flops 1622016 | bytes 2703360 | tf_op jit(solution)/shard_map/convert_element_type | solution.py:219
  62.9 2.1 %copy.37 = bf16[384,704]{0,1:T(8,128)(2,1)} copy(bf16[384,704]{1,0:T(8,128)(2,1)} %fusion.15) | data formatting | bytes 1081344 | tf_op jit(solution)/shard_map/convert_element_type | solution.py:219
  65.0 1.5 %collective-permute-start.4 = (bf16[384,704]{0,1:T(8,128)(2,1)}, bf16[384,704]{0,1:T(8,128)(2,1)S(1)}, u32[]{:S(2)}, u32[]{:S(2)}) collective-permute-start(bf16[384,704]{0,1:T(8,128)(2,1)} %copy.37), channel_id=1, source_target_pairs={{0,16},{16,0},{1,17},{17,1},{2,18},{18,2},{3,19},{19,3},{4,20},{20... | collective-permute-start | bytes 1622024 | tf_op jit(solution)/shard_map/ppermute | solution.py:129
  66.5 2.7 %fusion.20 = bf16[32,704]{1,0:T(8,128)(2,1)S(1)} fusion(bf16[32,2048]{1,0:T(8,128)(2,1)S(1)} %multiply_convert_fusion, bf16[704,2048]{1,0:T(8,128)(2,1)} %param.25, f32[32,704]{1,0:T(8,128)S(1)} %fusion.51), kind=kOutput, calls=%fused_computation.25 | convolution fusion | flops 92409856 | bytes 3149824 | tf_op jit(solution)/shard_map/dot_general | solution.py:16
  70.6 9.7 %collective-permute-done.4 = bf16[384,704]{0,1:T(8,128)(2,1)S(1)} collective-permute-done((bf16[384,704]{0,1:T(8,128)(2,1)}, bf16[384,704]{0,1:T(8,128)(2,1)S(1)}, u32[]{:S(2)}, u32[]{:S(2)}) %collective-permute-start.4) | collective-permute-done | bytes 540704 | tf_op jit(solution)/shard_map/ppermute | solution.py:129
  80.4 1.7 %add_convert_fusion = bf16[384,1024]{1,0:T(8,128)(2,1)} fusion(f32[384,1024]{1,0:T(8,128)S(1)} %fusion.9, bf16[384,704]{0,1:T(8,128)(2,1)S(1)} %collective-permute-done.4, bf16[2,704,1024]{2,1,0:T(8,128)(2,1)S(1)} %bitcast.51, s32[]{:T(128)S(6)} %select_n.121), kind=kOutput, calls=%fused_computation.6 | convolution fusion | flops 554434560 | bytes 4341764 | tf_op jit(solution)/shard_map/dot_general | solution.py:233
  82.1 9.0 %all-to-all-start.1 = ((bf16[16,24,1024]{2,1,0:T(8,128)(2,1)}), bf16[16,24,1024]{2,1,0:T(8,128)(2,1)}, u32[]{:S(2)}, u32[]{:S(2)}) async-start(bf16[16,24,1024]{2,1,0:T(8,128)(2,1)} %bitcast.55), calls=%async_computation.1 | async-start | bytes 1572864 | tf_op jit(solution)/shard_map/all_to_all | solution.py:240
  91.1 1.7 %fusion.6 = f32[32,1024]{1,0:T(8,128)S(1)} fusion(bf16[32,704]{1,0:T(8,128)(2,1)S(1)} %fusion.20, bf16[2,704,1024]{2,1,0:T(8,128)(2,1)} %bitcast.53, s32[]{:T(128)S(6)} %select_n.120), kind=kOutput, calls=%fused_computation.9 | convolution fusion | flops 46137344 | bytes 1617924 | tf_op jit(solution)/shard_map/dot_general | solution.py:236
  93.0 1.7 %gather_fusion = f32[192]{0:T(256)S(1)} fusion(f32[32,16]{0,1:T(8,128)S(1)} %maximum_select_fusion.2, s32[192]{0:T(256)S(1)} %reshape.219), kind=kCustom, calls=%fused_computation | custom fusion | bytes 3072 | tf_op jit(solution)/shard_map/jit(take_along_axis)/gather | solution.py:191
  95.5 1.7 %fusion.17 = f32[32,1024]{1,0:T(8,128)S(1)} fusion(f32[32,1024]{1,0:T(8,128)S(1)} %fusion.6, bf16[2,704,1024]{2,1,0:T(8,128)(2,1)} %bitcast.54, s32[]{:T(128)S(6)} %select_n.121, bf16[16,704]{1,0:T(8,128)(2,1)S(1)} %get-tuple-element.13, bf16[16,704]{1,0:T(8,128)(2,1)S(1)} %get-tuple-element.12), kind=kOutput, calls=%fused_computation.22 | convolution fusion | flops 46260224 | bytes 1748996 | tf_op jit(solution)/shard_map/dot_general | solution.py:236
  97.3 12.6 %all-to-all-done.1 = bf16[16,24,1024]{2,1,0:T(8,128)(2,1)} async-done(((bf16[16,24,1024]{2,1,0:T(8,128)(2,1)}), bf16[16,24,1024]{2,1,0:T(8,128)(2,1)}, u32[]{:S(2)}, u32[]{:S(2)}) %all-to-all-start.1) | async-done | bytes 786464 | tf_op jit(solution)/shard_map/all_to_all | solution.py:240
  109.9 1.4 %fusion.16 = f32[32,1024]{1,0:T(8,128)S(1)} fusion(f32[32,1024]{1,0:T(8,128)S(1)} %fusion.17, bf16[32,384]{1,0:T(8,128)(2,1)S(1)} %fusion.23, bf16[384,1024]{1,0:T(8,128)(2,1)} %bitcast.14, pred[32]{0:T(512)(128)(4,1)S(1)} %lt.63), kind=kOutput, calls=%fused_computation.21 | convolution fusion | flops 25231360 | bytes 1073184 | tf_op jit(solution)/shard_map/dot_general | solution.py:246
  111.3 1.6 %collective-permute-start.6 = (f32[16,1024]{1,0:T(8,128)S(1)}, f32[16,1024]{1,0:T(8,128)S(1)}, u32[]{:S(2)}, u32[]{:S(2)}) collective-permute-start(f32[16,1024]{1,0:T(8,128)S(1)} %get-tuple-element.8), channel_id=1, source_target_pairs={{0,16},{16,0},{1,17},{17,1},{2,18},{18,2},{3,19},{19,3},{4,20},{20... | collective-permute-start | bytes 196616 | tf_op jit(solution)/shard_map/ppermute | solution.py:129
  112.8 2.7 %collective-permute-done.6 = f32[16,1024]{1,0:T(8,128)S(1)} collective-permute-done((f32[16,1024]{1,0:T(8,128)S(1)}, f32[16,1024]{1,0:T(8,128)S(1)}, u32[]{:S(2)}, u32[]{:S(2)}) %collective-permute-start.6) | collective-permute-done | bytes 65568 | tf_op jit(solution)/shard_map/ppermute | solution.py:129
  (68 shorter events, 9.2 us)
Async XLA Ops:
  0.6 69.2 %copy-start = (bf16[1,1408,1024]{2,1,0:T(8,128)(2,1)S(1)}, bf16[1,1408,1024]{2,1,0:T(8,128)(2,1)}, u32[]{:S(2)}) copy-start(bf16[1,1408,1024]{2,1,0:T(8,128)(2,1)} %param.23) | copy-start | bytes 8650756
  0.6 13.8 %copy-start.2 = (bf16[1,1,16,2048]{3,2,1,0:T(8,128)(2,1)S(1)}, bf16[1,1,16,2048]{3,2,1,0:T(8,128)(2,1)}, u32[]{:S(2)}) copy-start(bf16[1,1,16,2048]{3,2,1,0:T(8,128)(2,1)} %param.15) | copy-start | bytes 196612
  0.7 14.8 %copy-start.5 = (f32[2048]{0:T(1024)S(1)}, f32[2048]{0:T(1024)}, u32[]{:S(2)}) copy-start(f32[2048]{0:T(1024)} %param.17) | copy-start | bytes 24580
  0.7 6.7 %collective-permute-start.1 = (bf16[16,1024]{1,0:T(8,128)(2,1)}, bf16[16,1024]{1,0:T(8,128)(2,1)S(1)}, u32[]{:S(2)}, u32[]{:S(2)}) collective-permute-start(bf16[16,1024]{1,0:T(8,128)(2,1)} %bitcast.63), channel_id=1, source_target_pairs={{0,16},{16,0},{1,17},{17,1},{2,18},{18,2},{3,19},{19,3},{4,20},{20... | collective-permute-start | bytes 98312 | tf_op jit(solution)/shard_map/ppermute | solution.py:129
  3.7 10.1 %collective-permute-start = (bf16[16,2048]{1,0:T(8,128)(2,1)}, bf16[16,2048]{1,0:T(8,128)(2,1)S(1)}, u32[]{:S(2)}, u32[]{:S(2)}) collective-permute-start(bf16[16,2048]{1,0:T(8,128)(2,1)} %bitcast.61), channel_id=1, source_target_pairs={{0,16},{16,0},{1,17},{17,1},{2,18},{18,2},{3,19},{19,3},{4,20},{20... | collective-permute-start | bytes 196616 | tf_op jit(solution)/shard_map/ppermute | solution.py:129
  9.5 4.3 %collective-permute-start.2 = (bf16[32,1024]{1,0:T(8,128)(2,1)S(1)}, bf16[32,1024]{1,0:T(8,128)(2,1)S(1)}, u32[]{:S(2)}, u32[]{:S(2)}) collective-permute-start(bf16[32,1024]{1,0:T(8,128)(2,1)S(1)} %convolution_convert_fusion.1), channel_id=1, source_target_pairs={{0,16},{16,0},{1,17},{17,1},{2,18},{18,2},{3,19},{19,3},{4,20},{20... | collective-permute-start | bytes 196616 | tf_op jit(solution)/shard_map/ppermute | solution.py:129
  13.8 0.6 copy-start.3
  15.6 8.5 %copy-start.4 = (bf16[2048,8]{0,1:T(8,128)(2,1)S(1)}, bf16[2048,8]{0,1:T(8,128)(2,1)}, u32[]{:S(2)}) copy-start(bf16[2048,8]{0,1:T(8,128)(2,1)} %param.18) | copy-start | bytes 98308
  17.4 38.4 %all-to-all-start = ((bf16[16,24,2048]{2,1,0:T(8,128)(2,1)}), bf16[16,24,2048]{2,1,0:T(8,128)(2,1)}, u32[]{:S(2)}, u32[]{:S(2)}) async-start(bf16[16,24,2048]{2,1,0:T(8,128)(2,1)} %bitcast.52), calls=%async_computation | async-start | bytes 3145728 | tf_op jit(solution)/shard_map/all_to_all | solution.py:215
  24.2 68.6 %collective-permute-start.3 = (f32[32,8]{0,1:T(8,128)S(1)}, f32[32,8]{0,1:T(8,128)S(1)}, u32[]{:S(2)}, u32[]{:S(2)}) collective-permute-start(f32[32,8]{0,1:T(8,128)S(1)} %fusion.50), channel_id=1, source_target_pairs={{0,16},{16,0},{1,17},{17,1},{2,18},{18,2},{3,19},{19,3},{4,20},{20... | collective-permute-start | bytes 3080 | tf_op jit(solution)/shard_map/ppermute | solution.py:129
  65.0 4.8 %copy-start.1 = (bf16[384,704]{1,0:T(8,128)(2,1)S(1)}, bf16[384,704]{1,0:T(8,128)(2,1)}, u32[]{:S(2)}) copy-start(bf16[384,704]{1,0:T(8,128)(2,1)} %fusion.15) | copy-start | bytes 1622020
  65.0 15.4 %collective-permute-start.4 = (bf16[384,704]{0,1:T(8,128)(2,1)}, bf16[384,704]{0,1:T(8,128)(2,1)S(1)}, u32[]{:S(2)}, u32[]{:S(2)}) collective-permute-start(bf16[384,704]{0,1:T(8,128)(2,1)} %copy.37), channel_id=1, source_target_pairs={{0,16},{16,0},{1,17},{17,1},{2,18},{18,2},{3,19},{19,3},{4,20},{20... | collective-permute-start | bytes 1622024 | tf_op jit(solution)/shard_map/ppermute | solution.py:129
  69.3 26.3 %collective-permute-start.5 = (bf16[32,704]{1,0:T(8,128)(2,1)S(1)}, bf16[32,704]{1,0:T(8,128)(2,1)S(1)}, u32[]{:S(2)}, u32[]{:S(2)}) collective-permute-start(bf16[32,704]{1,0:T(8,128)(2,1)S(1)} %fusion.20), channel_id=1, source_target_pairs={{0,16},{16,0},{1,17},{17,1},{2,18},{18,2},{3,19},{19,3},{4,20},{20... | collective-permute-start | bytes 135176 | tf_op jit(solution)/shard_map/ppermute | solution.py:129
  82.1 27.8 %all-to-all-start.1 = ((bf16[16,24,1024]{2,1,0:T(8,128)(2,1)}), bf16[16,24,1024]{2,1,0:T(8,128)(2,1)}, u32[]{:S(2)}, u32[]{:S(2)}) async-start(bf16[16,24,1024]{2,1,0:T(8,128)(2,1)} %bitcast.55), calls=%async_computation.1 | async-start | bytes 1572864 | tf_op jit(solution)/shard_map/all_to_all | solution.py:240
  94.6 21.1 %copy-start.6 = (f32[2048]{0:T(1024)S(1)}, f32[2048]{0:T(1024)}, u32[]{:S(2)}) copy-start(f32[2048]{0:T(1024)} %param.27) | copy-start | bytes 24580
  111.3 4.3 %collective-permute-start.6 = (f32[16,1024]{1,0:T(8,128)S(1)}, f32[16,1024]{1,0:T(8,128)S(1)}, u32[]{:S(2)}, u32[]{:S(2)}) collective-permute-start(f32[16,1024]{1,0:T(8,128)S(1)} %get-tuple-element.8), channel_id=1, source_target_pairs={{0,16},{16,0},{1,17},{17,1},{2,18},{18,2},{3,19},{19,3},{4,20},{20... | collective-permute-start | bytes 196616 | tf_op jit(solution)/shard_map/ppermute | solution.py:129

commit v12 on v11

--- a/solution.py
+++ b/solution.py
@@ -215,24 +215,30 @@
     slot_rows = lax.all_to_all(outgoing, "expert", split_axis=0, concat_axis=0, tiled=True)
     flattened = slot_rows.reshape(-1, slot_rows.shape[-1])
     unit_total = gate_local.shape[0]
-    both = by_rows(flattened, jnp.concatenate([gate_local, up_local], axis=0))
-    hidden = (jax.nn.silu(both[:, :unit_total]) * both[:, unit_total:]).astype(jnp.bfloat16)
-    hidden_peer = swap_pair(hidden)
+    both = lax.dot_general(
+        jnp.concatenate([gate_local, up_local], axis=0),
+        flattened,
+        (((1,), (1,)), ((), ())),
+        preferred_element_type=jnp.float32,
+    )
+    hidden_t = (jax.nn.silu(both[:unit_total]) * both[unit_total:]).astype(jnp.bfloat16)
+    hidden_peer_t = swap_pair(hidden_t)
     shared_gate_value = by_rows(column, shared_gate)
     shared_up_value = by_rows(column, shared_up)
     shared_hidden = (jax.nn.silu(shared_gate_value) * shared_up_value).astype(jnp.bfloat16)
     shared_peer = halves_swapped(swap_pair(shared_hidden))
 
-    unit_count = hidden.shape[1]
+    unit_count = hidden_t.shape[0]
     down_blocks = down_local.reshape(groups, unit_count, column_width)
     shared_blocks = shared_down.reshape(groups, unit_count, column_width)
     down_mine = lax.dynamic_index_in_dim(down_blocks, me, 0, keepdims=False)
     down_peer = lax.dynamic_index_in_dim(down_blocks, 1 - me, 0, keepdims=False)
     shared_mine = lax.dynamic_index_in_dim(shared_blocks, me, 0, keepdims=False)
     shared_other = lax.dynamic_index_in_dim(shared_blocks, 1 - me, 0, keepdims=False)
-    routed_total = jnp.dot(hidden, down_mine, preferred_element_type=jnp.float32) + jnp.dot(
-        hidden_peer, down_peer, preferred_element_type=jnp.float32
-    )
+    by_units = (((0,), (0,)), ((), ()))
+    routed_total = lax.dot_general(
+        hidden_t, down_mine, by_units, preferred_element_type=jnp.float32
+    ) + lax.dot_general(hidden_peer_t, down_peer, by_units, preferred_element_type=jnp.float32)
     shared = jnp.dot(shared_hidden, shared_mine, preferred_element_type=jnp.float32) + jnp.dot(
         shared_peer, shared_other, preferred_element_type=jnp.float32
     )

time: 117 us -> 115 us (0.983)
  local copies, waits for them, and re-layouts: 7.57 us -> 5.49 us
  waiting for transfers between devices: 54.6 us -> 56.2 us
    dot_general x3 -> x2, matrix products: 11.2 us -> 3.63 us  [by_rows(): lax.dot_general(left, weight_rows, (((1,), (1,)), ((), ())), preferred_el...]
    dot_general x2 -> x3, matrix products: 2.51 us -> 9.04 us  [the longest x1 6.52 us: shards_pair(): lax.dot_general(jnp.concatenate([gate_local, up_local], axis=0), flattene...]
    convert_element_type x1 -> x0, local copies, waits for them, and re-layouts: 2.08 us -> none  [shards_pair(): (jax.nn.silu(both[:, :unit_total]) * both[:, unit_total:]).astype(jnp.bfl...]
    ppermute x7, waiting for transfers between devices: 14.7 us -> 16.3 us  [swap_pair(): return lax.ppermute(x, 'dp', [(0, 1), (1, 0)])]
  transfers between devices with their start and end apart: 9 -> 9, of which waited for: 5 -> 5; matrix products, arithmetic and copies ran while one was open for 25% -> 22% of each run, Pallas kernels for 0% -> 0%
where the time goes in v12:
time: 115 us; the launch traced here: 114 us
  waiting for transfers between devices  56.2 us (49%)
  starting transfers between devices  25.8 us (22%)
  matrix products  21.5 us (19%)
  local copies, waits for them, and re-layouts  5.49 us (5%)
  other arithmetic  4.13 us (4%)
    all_to_all x1, waiting for transfers between devices, shards_pair(): lax.all_to_all(outgoing, 'expert', split_axis=0, concat_axis=0, tiled=True)  27.3 us
    ppermute x7, waiting for transfers between devices, swap_pair(): return lax.ppermute(x, 'dp', [(0, 1), (1, 0)])  16.3 us
    all_to_all x1, waiting for transfers between devices, shards_pair(): lax.all_to_all(expert_out, 'expert', split_axis=0, concat_axis=0, tiled=T...  12.6 us
    ppermute x7, starting transfers between devices, swap_pair(): return lax.ppermute(x, 'dp', [(0, 1), (1, 0)])  10.4 us
    all_to_all x1, starting transfers between devices, shards_pair(): lax.all_to_all(expert_out, 'expert', split_axis=0, concat_axis=0, tiled=T...  9.01 us
    dot_general x1, matrix products, shards_pair(): lax.dot_general(jnp.concatenate([gate_local, up_local], axis=0), flattene...  6.52 us
    all_to_all x1, starting transfers between devices, shards_pair(): lax.all_to_all(outgoing, 'expert', split_axis=0, concat_axis=0, tiled=True)  6.38 us
    dot_general x2, matrix products, by_rows(): lax.dot_general(left, weight_rows, (((1,), (1,)), ((), ())), preferred_el...  3.63 us
  transfers between devices with their start and end apart: 9, of which 5 were waited for; matrix products, arithmetic and copies ran while one was open for 22% of the time, Pallas kernels for 0%

profile of v12, /device:TPU:0, one launch (start us, length us, event | category | flops | bytes accessed | tf_op | source)
XLA Modules:
  0.0 114.0 jit_solution(952906144510660215)
XLA Ops:
  0.7 3.0 %collective-permute-start.1 = (bf16[16,1024]{1,0:T(8,128)(2,1)}, bf16[16,1024]{1,0:T(8,128)(2,1)S(1)}, u32[]{:S(2)}, u32[]{:S(2)}) collective-permute-start(bf16[16,1024]{1,0:T(8,128)(2,1)} %bitcast.63), channel_id=1, source_target_pairs={{0,16},{16,0},{1,17},{17,1},{2,18},{18,2},{3,19},{19,3},{4,20},{20... | collective-permute-start | bytes 98312 | tf_op jit(solution)/shard_map/ppermute | solution.py:129
  7.4 2.1 %convolution_convert_fusion.1 = bf16[32,1024]{1,0:T(8,128)(2,1)S(1)} fusion(bf16[1024,1024]{1,0:T(8,128)(2,1)} %param.16, bf16[16,1024]{1,0:T(8,128)(2,1)S(1)} %collective-permute-done.1, bf16[16,1024]{1,0:T(8,128)(2,1)} %bitcast.64), kind=kOutput, calls=%fused_computation.22 | convolution fusion | flops 67272704 | bytes 2228224 | tf_op jit(solution)/shard_map/dot_general | solution.py:176
  9.5 2.0 %collective-permute-start.2 = (bf16[32,1024]{1,0:T(8,128)(2,1)S(1)}, bf16[32,1024]{1,0:T(8,128)(2,1)S(1)}, u32[]{:S(2)}, u32[]{:S(2)}) collective-permute-start(bf16[32,1024]{1,0:T(8,128)(2,1)S(1)} %convolution_convert_fusion.1), channel_id=1, source_target_pairs={{0,16},{16,0},{1,17},{17,1},{2,18},{18,2},{3,19},{19,3},{4,20},{20... | collective-permute-start | bytes 196616 | tf_op jit(solution)/shard_map/ppermute | solution.py:129
  11.6 2.2 %collective-permute-done.2 = bf16[32,1024]{1,0:T(8,128)(2,1)S(1)} collective-permute-done((bf16[32,1024]{1,0:T(8,128)(2,1)S(1)}, bf16[32,1024]{1,0:T(8,128)(2,1)S(1)}, u32[]{:S(2)}, u32[]{:S(2)}) %collective-permute-start.2) | collective-permute-done | bytes 65568 | tf_op jit(solution)/shard_map/ppermute | solution.py:129
  14.5 1.0 multiply_reduce_fusion
  15.6 1.8 %convolution_convert_fusion = bf16[384,2048]{1,0:T(8,128)(2,1)} fusion(pred[32,384]{1,0:T(8,128)(4,1)S(1)} %fusion.21, bf16[32,2048]{1,0:T(8,128)(2,1)S(1)} %multiply_convert_fusion), kind=kOutput, calls=%fused_computation.5 | convolution fusion | flops 51118080 | bytes 1716224 | tf_op jit(solution)/shard_map/dot_general | solution.py:212
  17.4 6.4 %all-to-all-start = ((bf16[16,24,2048]{2,1,0:T(8,128)(2,1)}), bf16[16,24,2048]{2,1,0:T(8,128)(2,1)}, u32[]{:S(2)}, u32[]{:S(2)}) async-start(bf16[16,24,2048]{2,1,0:T(8,128)(2,1)} %bitcast.52), calls=%async_computation | async-start | bytes 3145728 | tf_op jit(solution)/shard_map/all_to_all | solution.py:215
  24.2 1.5 %collective-permute-start.3 = (f32[32,8]{0,1:T(8,128)S(1)}, f32[32,8]{0,1:T(8,128)S(1)}, u32[]{:S(2)}, u32[]{:S(2)}) collective-permute-start(f32[32,8]{0,1:T(8,128)S(1)} %fusion.50), channel_id=1, source_target_pairs={{0,16},{16,0},{1,17},{17,1},{2,18},{18,2},{3,19},{19,3},{4,20},{20... | collective-permute-start | bytes 3080 | tf_op jit(solution)/shard_map/ppermute | solution.py:129
  25.8 2.7 %fusion.51 = f32[32,704]{1,0:T(8,128)S(1)} fusion(bf16[32,2048]{1,0:T(8,128)(2,1)S(1)} %multiply_convert_fusion, bf16[704,2048]{1,0:T(8,128)(2,1)} %param.24), kind=kOutput, calls=%fused_computation.82 | convolution fusion | flops 92274688 | bytes 3104768 | tf_op jit(solution)/shard_map/dot_general | solution.py:16
  28.5 27.3 %all-to-all-done = bf16[16,24,2048]{2,1,0:T(8,128)(2,1)} async-done(((bf16[16,24,2048]{2,1,0:T(8,128)(2,1)}), bf16[16,24,2048]{2,1,0:T(8,128)(2,1)}, u32[]{:S(2)}, u32[]{:S(2)}) %all-to-all-start) | async-done | bytes 1572896 | tf_op jit(solution)/shard_map/all_to_all | solution.py:215
  55.8 6.5 %fusion = f32[1408,384]{1,0:T(8,128)S(1)} fusion(bf16[384,2048]{1,0:T(8,128)(2,1)} %bitcast.9, bf16[704,2048]{1,0:T(8,128)(2,1)} %bitcast.66, bf16[704,2048]{1,0:T(8,128)(2,1)} %bitcast.67), kind=kOutput, calls=%fused_computation.1 | convolution fusion | flops 2226126848 | bytes 9502720 | tf_op jit(solution)/shard_map/dot_general | solution.py:218
  62.7 1.6 %collective-permute-start.4 = (bf16[704,384]{1,0:T(8,128)(2,1)S(1)}, bf16[704,384]{1,0:T(8,128)(2,1)S(1)}, u32[]{:S(2)}, u32[]{:S(2)}) collective-permute-start(bf16[704,384]{1,0:T(8,128)(2,1)S(1)} %fusion.20), channel_id=1, source_target_pairs={{0,16},{16,0},{1,17},{17,1},{2,18},{18,2},{3,19},{19,3},{4,20},{20... | collective-permute-start | bytes 1622024 | tf_op jit(solution)/shard_map/ppermute | solution.py:129
  64.3 0.9 fusion.19
  65.8 0.8 fusion.9
  66.6 11.3 %collective-permute-done.4 = bf16[704,384]{1,0:T(8,128)(2,1)S(1)} collective-permute-done((bf16[704,384]{1,0:T(8,128)(2,1)S(1)}, bf16[704,384]{1,0:T(8,128)(2,1)S(1)}, u32[]{:S(2)}, u32[]{:S(2)}) %collective-permute-start.4) | collective-permute-done | bytes 540704 | tf_op jit(solution)/shard_map/ppermute | solution.py:129
  77.9 1.7 %add_convert_fusion = bf16[384,1024]{1,0:T(8,128)(2,1)} fusion(f32[384,1024]{1,0:T(8,128)S(1)} %fusion.9, bf16[704,384]{1,0:T(8,128)(2,1)S(1)} %collective-permute-done.4, bf16[2,704,1024]{2,1,0:T(8,128)(2,1)S(1)} %bitcast.51, s32[]{:T(128)S(6)} %select_n.121), kind=kOutput, calls=%fused_computation.6 | convolution fusion | flops 554434560 | bytes 4341764 | tf_op jit(solution)/shard_map/dot_general | solution.py:241
  79.6 9.0 %all-to-all-start.1 = ((bf16[16,24,1024]{2,1,0:T(8,128)(2,1)}), bf16[16,24,1024]{2,1,0:T(8,128)(2,1)}, u32[]{:S(2)}, u32[]{:S(2)}) async-start(bf16[16,24,1024]{2,1,0:T(8,128)(2,1)} %bitcast.55), calls=%async_computation.1 | async-start | bytes 1572864 | tf_op jit(solution)/shard_map/all_to_all | solution.py:246
  88.6 1.7 %fusion.6 = f32[32,1024]{1,0:T(8,128)S(1)} fusion(bf16[32,704]{1,0:T(8,128)(2,1)S(1)} %fusion.19, bf16[2,704,1024]{2,1,0:T(8,128)(2,1)} %bitcast.53, s32[]{:T(128)S(6)} %select_n.120), kind=kOutput, calls=%fused_computation.9 | convolution fusion | flops 46137344 | bytes 1617924 | tf_op jit(solution)/shard_map/dot_general | solution.py:242
  90.5 1.7 %gather_fusion = f32[192]{0:T(256)S(1)} fusion(f32[32,16]{0,1:T(8,128)S(1)} %maximum_select_fusion.2, s32[192]{0:T(256)S(1)} %reshape.219), kind=kCustom, calls=%fused_computation | custom fusion | bytes 3072 | tf_op jit(solution)/shard_map/jit(take_along_axis)/gather | solution.py:191
  93.1 1.7 %fusion.16 = f32[32,1024]{1,0:T(8,128)S(1)} fusion(f32[32,1024]{1,0:T(8,128)S(1)} %fusion.6, bf16[2,704,1024]{2,1,0:T(8,128)(2,1)} %bitcast.54, s32[]{:T(128)S(6)} %select_n.121, bf16[16,704]{1,0:T(8,128)(2,1)S(1)} %get-tuple-element.13, bf16[16,704]{1,0:T(8,128)(2,1)S(1)} %get-tuple-element.12), kind=kOutput, calls=%fused_computation.20 | convolution fusion | flops 46260224 | bytes 1748996 | tf_op jit(solution)/shard_map/dot_general | solution.py:242
  94.8 12.6 %all-to-all-done.1 = bf16[16,24,1024]{2,1,0:T(8,128)(2,1)} async-done(((bf16[16,24,1024]{2,1,0:T(8,128)(2,1)}), bf16[16,24,1024]{2,1,0:T(8,128)(2,1)}, u32[]{:S(2)}, u32[]{:S(2)}) %all-to-all-start.1) | async-done | bytes 786464 | tf_op jit(solution)/shard_map/all_to_all | solution.py:246
  107.4 1.4 %fusion.15 = f32[32,1024]{1,0:T(8,128)S(1)} fusion(f32[32,1024]{1,0:T(8,128)S(1)} %fusion.16, bf16[32,384]{1,0:T(8,128)(2,1)S(1)} %fusion.23, bf16[384,1024]{1,0:T(8,128)(2,1)} %bitcast.14, pred[32]{0:T(512)(128)(4,1)S(1)} %lt.63), kind=kOutput, calls=%fused_computation.19 | convolution fusion | flops 25231360 | bytes 1073184 | tf_op jit(solution)/shard_map/dot_general | solution.py:252
  108.8 1.6 %collective-permute-start.6 = (f32[16,1024]{1,0:T(8,128)S(1)}, f32[16,1024]{1,0:T(8,128)S(1)}, u32[]{:S(2)}, u32[]{:S(2)}) collective-permute-start(f32[16,1024]{1,0:T(8,128)S(1)} %get-tuple-element.8), channel_id=1, source_target_pairs={{0,16},{16,0},{1,17},{17,1},{2,18},{18,2},{3,19},{19,3},{4,20},{20... | collective-permute-start | bytes 196616 | tf_op jit(solution)/shard_map/ppermute | solution.py:129
  110.4 2.7 %collective-permute-done.6 = f32[16,1024]{1,0:T(8,128)S(1)} collective-permute-done((f32[16,1024]{1,0:T(8,128)S(1)}, f32[16,1024]{1,0:T(8,128)S(1)}, u32[]{:S(2)}, u32[]{:S(2)}) %collective-permute-start.6) | collective-permute-done | bytes 65568 | tf_op jit(solution)/shard_map/ppermute | solution.py:129
  (67 shorter events, 7.8 us)
Async XLA Ops:
  0.6 65.1 %copy-start = (bf16[1,1408,1024]{2,1,0:T(8,128)(2,1)S(1)}, bf16[1,1408,1024]{2,1,0:T(8,128)(2,1)}, u32[]{:S(2)}) copy-start(bf16[1,1408,1024]{2,1,0:T(8,128)(2,1)} %param.23) | copy-start | bytes 8650756
  0.6 13.8 %copy-start.2 = (bf16[1,1,16,2048]{3,2,1,0:T(8,128)(2,1)S(1)}, bf16[1,1,16,2048]{3,2,1,0:T(8,128)(2,1)}, u32[]{:S(2)}) copy-start(bf16[1,1,16,2048]{3,2,1,0:T(8,128)(2,1)} %param.15) | copy-start | bytes 196612
  0.7 14.8 %copy-start.5 = (f32[2048]{0:T(1024)S(1)}, f32[2048]{0:T(1024)}, u32[]{:S(2)}) copy-start(f32[2048]{0:T(1024)} %param.17) | copy-start | bytes 24580
  0.7 6.7 %collective-permute-start.1 = (bf16[16,1024]{1,0:T(8,128)(2,1)}, bf16[16,1024]{1,0:T(8,128)(2,1)S(1)}, u32[]{:S(2)}, u32[]{:S(2)}) collective-permute-start(bf16[16,1024]{1,0:T(8,128)(2,1)} %bitcast.63), channel_id=1, source_target_pairs={{0,16},{16,0},{1,17},{17,1},{2,18},{18,2},{3,19},{19,3},{4,20},{20... | collective-permute-start | bytes 98312 | tf_op jit(solution)/shard_map/ppermute | solution.py:129
  3.7 10.1 %collective-permute-start = (bf16[16,2048]{1,0:T(8,128)(2,1)}, bf16[16,2048]{1,0:T(8,128)(2,1)S(1)}, u32[]{:S(2)}, u32[]{:S(2)}) collective-permute-start(bf16[16,2048]{1,0:T(8,128)(2,1)} %bitcast.61), channel_id=1, source_target_pairs={{0,16},{16,0},{1,17},{17,1},{2,18},{18,2},{3,19},{19,3},{4,20},{20... | collective-permute-start | bytes 196616 | tf_op jit(solution)/shard_map/ppermute | solution.py:129
  9.5 4.3 %collective-permute-start.2 = (bf16[32,1024]{1,0:T(8,128)(2,1)S(1)}, bf16[32,1024]{1,0:T(8,128)(2,1)S(1)}, u32[]{:S(2)}, u32[]{:S(2)}) collective-permute-start(bf16[32,1024]{1,0:T(8,128)(2,1)S(1)} %convolution_convert_fusion.1), channel_id=1, source_target_pairs={{0,16},{16,0},{1,17},{17,1},{2,18},{18,2},{3,19},{19,3},{4,20},{20... | collective-permute-start | bytes 196616 | tf_op jit(solution)/shard_map/ppermute | solution.py:129
  13.8 0.6 copy-start.3
  15.6 8.5 %copy-start.4 = (bf16[2048,8]{0,1:T(8,128)(2,1)S(1)}, bf16[2048,8]{0,1:T(8,128)(2,1)}, u32[]{:S(2)}) copy-start(bf16[2048,8]{0,1:T(8,128)(2,1)} %param.18) | copy-start | bytes 98308
  17.4 38.4 %all-to-all-start = ((bf16[16,24,2048]{2,1,0:T(8,128)(2,1)}), bf16[16,24,2048]{2,1,0:T(8,128)(2,1)}, u32[]{:S(2)}, u32[]{:S(2)}) async-start(bf16[16,24,2048]{2,1,0:T(8,128)(2,1)} %bitcast.52), calls=%async_computation | async-start | bytes 3145728 | tf_op jit(solution)/shard_map/all_to_all | solution.py:215
  24.2 66.1 %collective-permute-start.3 = (f32[32,8]{0,1:T(8,128)S(1)}, f32[32,8]{0,1:T(8,128)S(1)}, u32[]{:S(2)}, u32[]{:S(2)}) collective-permute-start(f32[32,8]{0,1:T(8,128)S(1)} %fusion.50), channel_id=1, source_target_pairs={{0,16},{16,0},{1,17},{17,1},{2,18},{18,2},{3,19},{19,3},{4,20},{20... | collective-permute-start | bytes 3080 | tf_op jit(solution)/shard_map/ppermute | solution.py:129
  55.8 8.4 %copy-start.1 = (bf16[704,2048]{1,0:T(8,128)(2,1)S(1)}, bf16[704,2048]{1,0:T(8,128)(2,1)}, u32[]{:S(2)}) copy-start(bf16[704,2048]{1,0:T(8,128)(2,1)} %param.25) | copy-start | bytes 8650756
  62.7 15.2 %collective-permute-start.4 = (bf16[704,384]{1,0:T(8,128)(2,1)S(1)}, bf16[704,384]{1,0:T(8,128)(2,1)S(1)}, u32[]{:S(2)}, u32[]{:S(2)}) collective-permute-start(bf16[704,384]{1,0:T(8,128)(2,1)S(1)} %fusion.20), channel_id=1, source_target_pairs={{0,16},{16,0},{1,17},{17,1},{2,18},{18,2},{3,19},{19,3},{4,20},{20... | collective-permute-start | bytes 1622024 | tf_op jit(solution)/shard_map/ppermute | solution.py:129
  65.2 27.9 %collective-permute-start.5 = (bf16[32,704]{1,0:T(8,128)(2,1)S(1)}, bf16[32,704]{1,0:T(8,128)(2,1)S(1)}, u32[]{:S(2)}, u32[]{:S(2)}) collective-permute-start(bf16[32,704]{1,0:T(8,128)(2,1)S(1)} %fusion.19), channel_id=1, source_target_pairs={{0,16},{16,0},{1,17},{17,1},{2,18},{18,2},{3,19},{19,3},{4,20},{20... | collective-permute-start | bytes 135176 | tf_op jit(solution)/shard_map/ppermute | solution.py:129
  79.6 27.8 %all-to-all-start.1 = ((bf16[16,24,1024]{2,1,0:T(8,128)(2,1)}), bf16[16,24,1024]{2,1,0:T(8,128)(2,1)}, u32[]{:S(2)}, u32[]{:S(2)}) async-start(bf16[16,24,1024]{2,1,0:T(8,128)(2,1)} %bitcast.55), calls=%async_computation.1 | async-start | bytes 1572864 | tf_op jit(solution)/shard_map/all_to_all | solution.py:246
  92.2 21.1 %copy-start.6 = (f32[2048]{0:T(1024)S(1)}, f32[2048]{0:T(1024)}, u32[]{:S(2)}) copy-start(f32[2048]{0:T(1024)} %param.27) | copy-start | bytes 24580
  108.8 4.3 %collective-permute-start.6 = (f32[16,1024]{1,0:T(8,128)S(1)}, f32[16,1024]{1,0:T(8,128)S(1)}, u32[]{:S(2)}, u32[]{:S(2)}) collective-permute-start(f32[16,1024]{1,0:T(8,128)S(1)} %get-tuple-element.8), channel_id=1, source_target_pairs={{0,16},{16,0},{1,17},{17,1},{2,18},{18,2},{3,19},{19,3},{4,20},{20... | collective-permute-start | bytes 196616 | tf_op jit(solution)/shard_map/ppermute | solution.py:129

commit v13 on v12

--- a/solution.py
+++ b/solution.py
@@ -249,9 +249,12 @@
     combine = jnp.sum(
         jnp.where(slot_hit, weights[:, :, None], jnp.zeros((), jnp.bfloat16)), axis=1
     ).astype(jnp.bfloat16)
-    routed = jnp.dot(combine, returned, preferred_element_type=jnp.float32)
-    combined = jnp.where(row_live[:, None], routed + shared, 0.0)
-    summed = in_axis_order(first, combined[:row_count], swap_pair(combined[row_count:]), 1)
+    routed_peer = jnp.dot(combine[row_count:], returned, preferred_element_type=jnp.float32)
+    combined_peer = jnp.where(row_live[row_count:, None], routed_peer + shared[row_count:], 0.0)
+    from_peer = swap_pair(combined_peer)
+    routed_mine = jnp.dot(combine[:row_count], returned, preferred_element_type=jnp.float32)
+    combined_mine = jnp.where(row_live[:row_count, None], routed_mine + shared[:row_count], 0.0)
+    summed = in_axis_order(first, combined_mine, from_peer, 1)
     stream_sum = stream_in + summed
     stream = stream_sum.astype(jnp.bfloat16)[None, None]
     normed = rms_scale(stream_sum, gain_out).astype(jnp.bfloat16)[None, None]

time: 115 us -> 115 us (level)
  waiting for transfers between devices: 56.2 us -> 54.9 us
  matrix products: 21.5 us -> 22.8 us
    ppermute x7, waiting for transfers between devices: 16.3 us -> 15 us  [swap_pair(): return lax.ppermute(x, 'dp', [(0, 1), (1, 0)])]
    dot_general x1 -> x2, matrix products: 1.37 us -> 2.7 us  [the longest x1 1.35 us: shards_pair(): jnp.dot(combine[row_count:], returned, preferred_element_type=jnp.float32)]
  transfers between devices with their start and end apart: 9 -> 9, of which waited for: 5 -> 5; matrix products, arithmetic and copies ran while one was open for 22% -> 23% of each run, Pallas kernels for 0% -> 0%
where the time goes in v13:
time: 115 us; the launch traced here: 114 us
  waiting for transfers between devices  54.9 us (48%)
  starting transfers between devices  25.7 us (22%)
  matrix products  22.8 us (20%)
  local copies, waits for them, and re-layouts  5.49 us (5%)
  other arithmetic  4.13 us (4%)
    all_to_all x1, waiting for transfers between devices, shards_pair(): lax.all_to_all(outgoing, 'expert', split_axis=0, concat_axis=0, tiled=True)  27.3 us
    ppermute x7, waiting for transfers between devices, swap_pair(): return lax.ppermute(x, 'dp', [(0, 1), (1, 0)])  15 us
    all_to_all x1, waiting for transfers between devices, shards_pair(): lax.all_to_all(expert_out, 'expert', split_axis=0, concat_axis=0, tiled=T...  12.6 us
    ppermute x7, starting transfers between devices, swap_pair(): return lax.ppermute(x, 'dp', [(0, 1), (1, 0)])  10.4 us
    all_to_all x1, starting transfers between devices, shards_pair(): lax.all_to_all(expert_out, 'expert', split_axis=0, concat_axis=0, tiled=T...  9 us
    dot_general x1, matrix products, shards_pair(): lax.dot_general(jnp.concatenate([gate_local, up_local], axis=0), flattene...  6.53 us
    all_to_all x1, starting transfers between devices, shards_pair(): lax.all_to_all(outgoing, 'expert', split_axis=0, concat_axis=0, tiled=True)  6.38 us
    dot_general x2, matrix products, by_rows(): lax.dot_general(left, weight_rows, (((1,), (1,)), ((), ())), preferred_el...  3.63 us
  transfers between devices with their start and end apart: 9, of which 5 were waited for; matrix products, arithmetic and copies ran while one was open for 23% of the time, Pallas kernels for 0%

profile of v13, /device:TPU:0, one launch (start us, length us, event | category | flops | bytes accessed | tf_op | source)
XLA Modules:
  0.0 113.9 jit_solution(14922759978771115128)
XLA Ops:
  0.7 3.0 %collective-permute-start.1 = (bf16[16,1024]{1,0:T(8,128)(2,1)}, bf16[16,1024]{1,0:T(8,128)(2,1)S(1)}, u32[]{:S(2)}, u32[]{:S(2)}) collective-permute-start(bf16[16,1024]{1,0:T(8,128)(2,1)} %bitcast.67), channel_id=1, source_target_pairs={{0,16},{16,0},{1,17},{17,1},{2,18},{18,2},{3,19},{19,3},{4,20},{20... | collective-permute-start | bytes 98312 | tf_op jit(solution)/shard_map/ppermute | solution.py:129
  7.4 2.1 %convolution_convert_fusion.1 = bf16[32,1024]{1,0:T(8,128)(2,1)S(1)} fusion(bf16[1024,1024]{1,0:T(8,128)(2,1)} %param.16, bf16[16,1024]{1,0:T(8,128)(2,1)S(1)} %collective-permute-done.1, bf16[16,1024]{1,0:T(8,128)(2,1)} %bitcast.68), kind=kOutput, calls=%fused_computation.20 | convolution fusion | flops 67272704 | bytes 2228224 | tf_op jit(solution)/shard_map/dot_general | solution.py:176
  9.5 2.0 %collective-permute-start.2 = (bf16[32,1024]{1,0:T(8,128)(2,1)S(1)}, bf16[32,1024]{1,0:T(8,128)(2,1)S(1)}, u32[]{:S(2)}, u32[]{:S(2)}) collective-permute-start(bf16[32,1024]{1,0:T(8,128)(2,1)S(1)} %convolution_convert_fusion.1), channel_id=1, source_target_pairs={{0,16},{16,0},{1,17},{17,1},{2,18},{18,2},{3,19},{19,3},{4,20},{20... | collective-permute-start | bytes 196616 | tf_op jit(solution)/shard_map/ppermute | solution.py:129
  11.6 2.2 %collective-permute-done.2 = bf16[32,1024]{1,0:T(8,128)(2,1)S(1)} collective-permute-done((bf16[32,1024]{1,0:T(8,128)(2,1)S(1)}, bf16[32,1024]{1,0:T(8,128)(2,1)S(1)}, u32[]{:S(2)}, u32[]{:S(2)}) %collective-permute-start.2) | collective-permute-done | bytes 65568 | tf_op jit(solution)/shard_map/ppermute | solution.py:129
  14.5 1.0 multiply_reduce_fusion
  15.6 1.8 %convolution_convert_fusion = bf16[384,2048]{1,0:T(8,128)(2,1)} fusion(pred[32,384]{1,0:T(8,128)(4,1)S(1)} %fusion.20, bf16[32,2048]{1,0:T(8,128)(2,1)S(1)} %multiply_convert_fusion), kind=kOutput, calls=%fused_computation.5 | convolution fusion | flops 51118080 | bytes 1716224 | tf_op jit(solution)/shard_map/dot_general | solution.py:212
  17.4 6.4 %all-to-all-start = ((bf16[16,24,2048]{2,1,0:T(8,128)(2,1)}), bf16[16,24,2048]{2,1,0:T(8,128)(2,1)}, u32[]{:S(2)}, u32[]{:S(2)}) async-start(bf16[16,24,2048]{2,1,0:T(8,128)(2,1)} %bitcast.56), calls=%async_computation | async-start | bytes 3145728 | tf_op jit(solution)/shard_map/all_to_all | solution.py:215
  24.3 1.5 %collective-permute-start.3 = (f32[32,8]{0,1:T(8,128)S(1)}, f32[32,8]{0,1:T(8,128)S(1)}, u32[]{:S(2)}, u32[]{:S(2)}) collective-permute-start(f32[32,8]{0,1:T(8,128)S(1)} %fusion.58), channel_id=1, source_target_pairs={{0,16},{16,0},{1,17},{17,1},{2,18},{18,2},{3,19},{19,3},{4,20},{20... | collective-permute-start | bytes 3080 | tf_op jit(solution)/shard_map/ppermute | solution.py:129
  25.8 2.7 %fusion.59 = f32[32,704]{1,0:T(8,128)S(1)} fusion(bf16[32,2048]{1,0:T(8,128)(2,1)S(1)} %multiply_convert_fusion, bf16[704,2048]{1,0:T(8,128)(2,1)} %param.24), kind=kOutput, calls=%fused_computation.89 | convolution fusion | flops 92274688 | bytes 3104768 | tf_op jit(solution)/shard_map/dot_general | solution.py:16
  28.5 27.3 %all-to-all-done = bf16[16,24,2048]{2,1,0:T(8,128)(2,1)} async-done(((bf16[16,24,2048]{2,1,0:T(8,128)(2,1)}), bf16[16,24,2048]{2,1,0:T(8,128)(2,1)}, u32[]{:S(2)}, u32[]{:S(2)}) %all-to-all-start) | async-done | bytes 1572896 | tf_op jit(solution)/shard_map/all_to_all | solution.py:215
  55.8 6.5 %fusion = f32[1408,384]{1,0:T(8,128)S(1)} fusion(bf16[384,2048]{1,0:T(8,128)(2,1)} %bitcast.10, bf16[704,2048]{1,0:T(8,128)(2,1)} %bitcast.70, bf16[704,2048]{1,0:T(8,128)(2,1)} %bitcast.71), kind=kOutput, calls=%fused_computation.1 | convolution fusion | flops 2226126848 | bytes 9502720 | tf_op jit(solution)/shard_map/dot_general | solution.py:218
  62.7 1.6 %collective-permute-start.4 = (bf16[704,384]{1,0:T(8,128)(2,1)S(1)}, bf16[704,384]{1,0:T(8,128)(2,1)S(1)}, u32[]{:S(2)}, u32[]{:S(2)}) collective-permute-start(bf16[704,384]{1,0:T(8,128)(2,1)S(1)} %fusion.19), channel_id=1, source_target_pairs={{0,16},{16,0},{1,17},{17,1},{2,18},{18,2},{3,19},{19,3},{4,20},{20... | collective-permute-start | bytes 1622024 | tf_op jit(solution)/shard_map/ppermute | solution.py:129
  64.3 0.9 fusion.18
  66.6 11.3 %collective-permute-done.4 = bf16[704,384]{1,0:T(8,128)(2,1)S(1)} collective-permute-done((bf16[704,384]{1,0:T(8,128)(2,1)S(1)}, bf16[704,384]{1,0:T(8,128)(2,1)S(1)}, u32[]{:S(2)}, u32[]{:S(2)}) %collective-permute-start.4) | collective-permute-done | bytes 540704 | tf_op jit(solution)/shard_map/ppermute | solution.py:129
  77.9 1.7 %add_convert_fusion = bf16[384,1024]{1,0:T(8,128)(2,1)} fusion(f32[384,1024]{1,0:T(8,128)S(1)} %fusion.9, bf16[704,384]{1,0:T(8,128)(2,1)S(1)} %collective-permute-done.4, bf16[2,704,1024]{2,1,0:T(8,128)(2,1)S(1)} %bitcast.55, s32[]{:T(128)S(6)} %select_n.124), kind=kOutput, calls=%fused_computation.6 | convolution fusion | flops 554434560 | bytes 4341764 | tf_op jit(solution)/shard_map/dot_general | solution.py:241
  79.6 9.0 %all-to-all-start.1 = ((bf16[16,24,1024]{2,1,0:T(8,128)(2,1)}), bf16[16,24,1024]{2,1,0:T(8,128)(2,1)}, u32[]{:S(2)}, u32[]{:S(2)}) async-start(bf16[16,24,1024]{2,1,0:T(8,128)(2,1)} %bitcast.59), calls=%async_computation.1 | async-start | bytes 1572864 | tf_op jit(solution)/shard_map/all_to_all | solution.py:246
  88.6 1.7 %fusion.6 = f32[32,1024]{1,0:T(8,128)S(1)} fusion(bf16[32,704]{1,0:T(8,128)(2,1)S(1)} %fusion.18, bf16[2,704,1024]{2,1,0:T(8,128)(2,1)} %bitcast.57, s32[]{:T(128)S(6)} %select_n.123), kind=kOutput, calls=%fused_computation.9 | convolution fusion | flops 46137344 | bytes 1617924 | tf_op jit(solution)/shard_map/dot_general | solution.py:242
  90.5 1.7 %gather_fusion = f32[192]{0:T(256)S(1)} fusion(f32[32,16]{0,1:T(8,128)S(1)} %maximum_select_fusion.2, s32[192]{0:T(256)S(1)} %reshape.226), kind=kCustom, calls=%fused_computation | custom fusion | bytes 3072 | tf_op jit(solution)/shard_map/jit(take_along_axis)/gather | solution.py:191
  93.1 1.7 %fusion.15 = f32[32,1024]{1,0:T(8,128)S(1)} fusion(f32[32,1024]{1,0:T(8,128)S(1)} %fusion.6, bf16[2,704,1024]{2,1,0:T(8,128)(2,1)} %bitcast.58, s32[]{:T(128)S(6)} %select_n.124, bf16[16,704]{1,0:T(8,128)(2,1)S(1)} %get-tuple-element.11, bf16[16,704]{1,0:T(8,128)(2,1)S(1)} %get-tuple-element.10), kind=kOutput, calls=%fused_computation.18 | convolution fusion | flops 46260224 | bytes 1748996 | tf_op jit(solution)/shard_map/dot_general | solution.py:242
  94.8 12.6 %all-to-all-done.1 = bf16[16,24,1024]{2,1,0:T(8,128)(2,1)} async-done(((bf16[16,24,1024]{2,1,0:T(8,128)(2,1)}), bf16[16,24,1024]{2,1,0:T(8,128)(2,1)}, u32[]{:S(2)}, u32[]{:S(2)}) %all-to-all-start.1) | async-done | bytes 786464 | tf_op jit(solution)/shard_map/all_to_all | solution.py:246
  107.4 1.4 %fusion.26 = f32[16,1024]{1,0:T(8,128)S(1)} fusion(f32[32,1024]{1,0:T(8,128)S(1)} %fusion.15, pred[16]{0:T(512)(128)(4,1)S(1)} %get-tuple-element.14, bf16[384,1024]{1,0:T(8,128)(2,1)} %bitcast.15, bf16[32,384]{1,0:T(8,128)(2,1)S(1)} %fusion.22), kind=kOutput, calls=%fused_computation.42 | convolution fusion | flops 12615680 | bytes 930304 | tf_op jit(solution)/shard_map/dot_general | solution.py:252
  108.8 1.5 %collective-permute-start.6 = (f32[16,1024]{1,0:T(8,128)S(1)}, f32[16,1024]{1,0:T(8,128)S(1)}, u32[]{:S(2)}, u32[]{:S(2)}) collective-permute-start(f32[16,1024]{1,0:T(8,128)S(1)} %fusion.26), channel_id=1, source_target_pairs={{0,16},{16,0},{1,17},{17,1},{2,18},{18,2},{3,19},{19,3},{4,20},{20... | collective-permute-start | bytes 196616 | tf_op jit(solution)/shard_map/ppermute | solution.py:129
  110.3 1.4 %fusion.27 = f32[16,1024]{1,0:T(8,128)S(1)} fusion(f32[32,1024]{1,0:T(8,128)S(1)} %fusion.15, pred[16]{0:T(512)(128)(4,1)S(1)} %get-tuple-element.15, bf16[384,1024]{1,0:T(8,128)(2,1)} %bitcast.15, bf16[32,384]{1,0:T(8,128)(2,1)S(1)} %fusion.22), kind=kOutput, calls=%fused_computation.44 | convolution fusion | flops 12615680 | bytes 930304 | tf_op jit(solution)/shard_map/dot_general | solution.py:255
  111.6 1.4 %collective-permute-done.6 = f32[16,1024]{1,0:T(8,128)S(1)} collective-permute-done((f32[16,1024]{1,0:T(8,128)S(1)}, f32[16,1024]{1,0:T(8,128)S(1)}, u32[]{:S(2)}, u32[]{:S(2)}) %collective-permute-start.6) | collective-permute-done | bytes 65568 | tf_op jit(solution)/shard_map/ppermute | solution.py:129
  (68 shorter events, 8.6 us)
Async XLA Ops:
  0.6 65.1 %copy-start = (bf16[1,1408,1024]{2,1,0:T(8,128)(2,1)S(1)}, bf16[1,1408,1024]{2,1,0:T(8,128)(2,1)}, u32[]{:S(2)}) copy-start(bf16[1,1408,1024]{2,1,0:T(8,128)(2,1)} %param.23) | copy-start | bytes 8650756
  0.6 13.8 %copy-start.2 = (bf16[1,1,16,2048]{3,2,1,0:T(8,128)(2,1)S(1)}, bf16[1,1,16,2048]{3,2,1,0:T(8,128)(2,1)}, u32[]{:S(2)}) copy-start(bf16[1,1,16,2048]{3,2,1,0:T(8,128)(2,1)} %param.15) | copy-start | bytes 196612
  0.7 14.8 %copy-start.5 = (f32[2048]{0:T(1024)S(1)}, f32[2048]{0:T(1024)}, u32[]{:S(2)}) copy-start(f32[2048]{0:T(1024)} %param.17) | copy-start | bytes 24580
  0.7 6.7 %collective-permute-start.1 = (bf16[16,1024]{1,0:T(8,128)(2,1)}, bf16[16,1024]{1,0:T(8,128)(2,1)S(1)}, u32[]{:S(2)}, u32[]{:S(2)}) collective-permute-start(bf16[16,1024]{1,0:T(8,128)(2,1)} %bitcast.67), channel_id=1, source_target_pairs={{0,16},{16,0},{1,17},{17,1},{2,18},{18,2},{3,19},{19,3},{4,20},{20... | collective-permute-start | bytes 98312 | tf_op jit(solution)/shard_map/ppermute | solution.py:129
  3.7 10.1 %collective-permute-start = (bf16[16,2048]{1,0:T(8,128)(2,1)}, bf16[16,2048]{1,0:T(8,128)(2,1)S(1)}, u32[]{:S(2)}, u32[]{:S(2)}) collective-permute-start(bf16[16,2048]{1,0:T(8,128)(2,1)} %bitcast.65), channel_id=1, source_target_pairs={{0,16},{16,0},{1,17},{17,1},{2,18},{18,2},{3,19},{19,3},{4,20},{20... | collective-permute-start | bytes 196616 | tf_op jit(solution)/shard_map/ppermute | solution.py:129
  9.5 4.3 %collective-permute-start.2 = (bf16[32,1024]{1,0:T(8,128)(2,1)S(1)}, bf16[32,1024]{1,0:T(8,128)(2,1)S(1)}, u32[]{:S(2)}, u32[]{:S(2)}) collective-permute-start(bf16[32,1024]{1,0:T(8,128)(2,1)S(1)} %convolution_convert_fusion.1), channel_id=1, source_target_pairs={{0,16},{16,0},{1,17},{17,1},{2,18},{18,2},{3,19},{19,3},{4,20},{20... | collective-permute-start | bytes 196616 | tf_op jit(solution)/shard_map/ppermute | solution.py:129
  13.8 0.6 copy-start.3
  15.6 8.5 %copy-start.4 = (bf16[2048,8]{0,1:T(8,128)(2,1)S(1)}, bf16[2048,8]{0,1:T(8,128)(2,1)}, u32[]{:S(2)}) copy-start(bf16[2048,8]{0,1:T(8,128)(2,1)} %param.18) | copy-start | bytes 98308
  17.4 38.4 %all-to-all-start = ((bf16[16,24,2048]{2,1,0:T(8,128)(2,1)}), bf16[16,24,2048]{2,1,0:T(8,128)(2,1)}, u32[]{:S(2)}, u32[]{:S(2)}) async-start(bf16[16,24,2048]{2,1,0:T(8,128)(2,1)} %bitcast.56), calls=%async_computation | async-start | bytes 3145728 | tf_op jit(solution)/shard_map/all_to_all | solution.py:215
  24.3 66.1 %collective-permute-start.3 = (f32[32,8]{0,1:T(8,128)S(1)}, f32[32,8]{0,1:T(8,128)S(1)}, u32[]{:S(2)}, u32[]{:S(2)}) collective-permute-start(f32[32,8]{0,1:T(8,128)S(1)} %fusion.58), channel_id=1, source_target_pairs={{0,16},{16,0},{1,17},{17,1},{2,18},{18,2},{3,19},{19,3},{4,20},{20... | collective-permute-start | bytes 3080 | tf_op jit(solution)/shard_map/ppermute | solution.py:129
  55.8 8.4 %copy-start.1 = (bf16[704,2048]{1,0:T(8,128)(2,1)S(1)}, bf16[704,2048]{1,0:T(8,128)(2,1)}, u32[]{:S(2)}) copy-start(bf16[704,2048]{1,0:T(8,128)(2,1)} %param.25) | copy-start | bytes 8650756
  62.7 15.2 %collective-permute-start.4 = (bf16[704,384]{1,0:T(8,128)(2,1)S(1)}, bf16[704,384]{1,0:T(8,128)(2,1)S(1)}, u32[]{:S(2)}, u32[]{:S(2)}) collective-permute-start(bf16[704,384]{1,0:T(8,128)(2,1)S(1)} %fusion.19), channel_id=1, source_target_pairs={{0,16},{16,0},{1,17},{17,1},{2,18},{18,2},{3,19},{19,3},{4,20},{20... | collective-permute-start | bytes 1622024 | tf_op jit(solution)/shard_map/ppermute | solution.py:129
  65.2 27.9 %collective-permute-start.5 = (bf16[32,704]{1,0:T(8,128)(2,1)S(1)}, bf16[32,704]{1,0:T(8,128)(2,1)S(1)}, u32[]{:S(2)}, u32[]{:S(2)}) collective-permute-start(bf16[32,704]{1,0:T(8,128)(2,1)S(1)} %fusion.18), channel_id=1, source_target_pairs={{0,16},{16,0},{1,17},{17,1},{2,18},{18,2},{3,19},{19,3},{4,20},{20... | collective-permute-start | bytes 135176 | tf_op jit(solution)/shard_map/ppermute | solution.py:129
  79.6 27.8 %all-to-all-start.1 = ((bf16[16,24,1024]{2,1,0:T(8,128)(2,1)}), bf16[16,24,1024]{2,1,0:T(8,128)(2,1)}, u32[]{:S(2)}, u32[]{:S(2)}) async-start(bf16[16,24,1024]{2,1,0:T(8,128)(2,1)} %bitcast.59), calls=%async_computation.1 | async-start | bytes 1572864 | tf_op jit(solution)/shard_map/all_to_all | solution.py:246
  92.2 21.0 %copy-start.6 = (f32[2048]{0:T(1024)S(1)}, f32[2048]{0:T(1024)}, u32[]{:S(2)}) copy-start(f32[2048]{0:T(1024)} %param.27) | copy-start | bytes 24580
  108.8 4.3 %collective-permute-start.6 = (f32[16,1024]{1,0:T(8,128)S(1)}, f32[16,1024]{1,0:T(8,128)S(1)}, u32[]{:S(2)}, u32[]{:S(2)}) collective-permute-start(f32[16,1024]{1,0:T(8,128)S(1)} %fusion.26), channel_id=1, source_target_pairs={{0,16},{16,0},{1,17},{17,1},{2,18},{18,2},{3,19},{19,3},{4,20},{20... | collective-permute-start | bytes 196616 | tf_op jit(solution)/shard_map/ppermute | solution.py:129
